TPU v7x, 32 devices: a whole 2x2x4 slice. The times are simulated.
32 devices in a mesh: slab: 8 (over z, y), coil: 4 (over x, core).
Axes of the slice: x: 2, y: 2, z: 4, core: 2. Of those that a mesh axis runs over, the one named last changes fastest.
Arguments:
- image: bfloat16 [2, 320, 256, 128], P(None, None, 'slab'), may hold values from -6 to 6
- coil_maps: bfloat16 [16, 320, 256, 128], P('coil', None, 'slab'), may hold values from -5 to 5
- y_data: bfloat16 [2, 16, 320, 128, 128], P(None, 'coil', 'slab'), may hold values from -6 to 6
- kz_lines: int32 [2, 320, 128], P(None, 'slab'), may hold values from -1 to 255, as said below
Outputs:
- gradient: bfloat16 [2, 320, 256, 128], P(None, 'coil', 'slab')
Inputs may be any that keep to these rules, and one draw needn't show every extreme that they name: kz_lines[m, ky, :] lists distinct sampled kz of that ky row first and -1 in the unused slots after them; every row has at least one sampled kz; row 160 uses all 128 slots.
All inputs are finite; a program needn't handle non-finite values.
Results may differ from a plain program's by a relative error of at most 0.0061.
Values may be sent and summed in bfloat16 or wider, within the bound.
No kernel may reach another device: no remote copies, remote signals or barrier semaphores. Data moves between devices by JAX's collectives and lax.ppermute only.
A program may use at most 256 MiB of HBM per device.

v0:
```python
import math

import jax
import jax.numpy as jnp
from jax import lax
from jax.sharding import PartitionSpec as P


def cos_sin(length):
    positions = jnp.arange(length, dtype=jnp.int32)
    phase = (positions[:, None] * positions[None, :] % length).astype(jnp.float32) * (
        2.0 * math.pi / length
    )
    factor = 1.0 / math.sqrt(length)
    return (
        (jnp.cos(phase) * factor).astype(jnp.bfloat16),
        (jnp.sin(phase) * factor).astype(jnp.bfloat16),
    )


def lane_tables(lane_count):
    half_lanes = lane_count // 2
    rows = jnp.arange(lane_count, dtype=jnp.int32)[:, None]
    cols = jnp.arange(lane_count, dtype=jnp.int32)[None, :]
    rotate = jnp.where((rows == cols + half_lanes) & (cols < half_lanes), -1.0, 0.0)
    rotate = rotate + jnp.where((cols == rows + half_lanes) & (rows < half_lanes), 1.0, 0.0)
    same_slot = rows % half_lanes == cols % half_lanes
    dup_real = jnp.where(same_slot & (rows < half_lanes), 1.0, 0.0)
    dup_imag = jnp.where(same_slot & (rows >= half_lanes), 1.0, 0.0)
    return (
        rotate.astype(jnp.bfloat16),
        dup_real.astype(jnp.bfloat16),
        dup_imag.astype(jnp.bfloat16),
    )


def lane_map(values, table):
    if values.dtype == jnp.bfloat16:
        return jnp.einsum("...l,lm->...m", values, table, preferred_element_type=jnp.float32)
    return jnp.einsum(
        "...l,lm->...m", values, table.astype(jnp.float32), precision=lax.Precision.HIGHEST
    )


def transform(image, coil_maps, y_data, kz_lines, forward, backward):
    state_count, y_count, z_local, lane_count = image.shape
    rotate, dup_real, dup_imag = lane_tables(lane_count)
    y_cos, y_sin = cos_sin(y_count)
    sens_real = lane_map(coil_maps, dup_real)[None]
    sens_imag = lane_map(coil_maps, dup_imag)[None]
    pixels = image.astype(jnp.float32)[:, None]
    turned_pixels = lane_map(image, rotate)[:, None]
    coil_image = (sens_real * pixels + sens_imag * turned_pixels).astype(jnp.bfloat16)
    turned_image = lane_map(coil_image, rotate).astype(jnp.bfloat16)
    spectrum = (
        jnp.einsum("ky,scyzl->sckzl", y_cos, coil_image, preferred_element_type=jnp.float32)
        - jnp.einsum("ky,scyzl->sckzl", y_sin, turned_image, preferred_element_type=jnp.float32)
    ).astype(jnp.bfloat16)
    gathered = forward(spectrum)
    z_count = gathered.shape[3]
    z_cos, z_sin = cos_sin(z_count)
    turned_gathered = lane_map(gathered, rotate).astype(jnp.bfloat16)
    sampled = kz_lines >= 0
    kz_index = jnp.maximum(kz_lines, 0)
    onehot = (
        (kz_index[..., None] == jnp.arange(z_count, dtype=jnp.int32)) & sampled[..., None]
    ).astype(jnp.bfloat16)
    measured = y_data.astype(jnp.float32)
    sampled_wide = sampled[:, None, :, :, None]
    kspace = jnp.einsum(
        "jq,sckql->sckjl", z_cos, gathered, preferred_element_type=jnp.float32
    ) - jnp.einsum("jq,sckql->sckjl", z_sin, turned_gathered, preferred_element_type=jnp.float32)
    picked = jnp.einsum(
        "skjq,sckql->sckjl", onehot.astype(jnp.float32), kspace, precision=lax.Precision.HIGHEST
    )
    residual = jnp.where(sampled_wide, picked - measured, jnp.float32(0.0)).astype(jnp.bfloat16)
    kz_grid = jnp.einsum(
        "skjq,sckjl->sckql", onehot, residual, preferred_element_type=jnp.float32
    ).astype(jnp.bfloat16)
    turned_grid = lane_map(kz_grid, rotate).astype(jnp.bfloat16)
    adjoint_z = (
        jnp.einsum("qz,sckql->sckzl", z_cos, kz_grid, preferred_element_type=jnp.float32)
        + jnp.einsum("qz,sckql->sckzl", z_sin, turned_grid, preferred_element_type=jnp.float32)
    ).astype(jnp.bfloat16)
    returned = backward(adjoint_z)
    turned_returned = lane_map(returned, rotate).astype(jnp.bfloat16)
    coil_back = jnp.einsum(
        "ky,sckzl->scyzl", y_cos, returned, preferred_element_type=jnp.float32
    ) + jnp.einsum("ky,sckzl->scyzl", y_sin, turned_returned, preferred_element_type=jnp.float32)
    turned_back = lane_map(coil_back, rotate)
    return jnp.sum(sens_real * coil_back - sens_imag * turned_back, axis=1)


def shards(image, coil_maps, y_data, kz_lines):
    partial_image = transform(
        image,
        coil_maps,
        y_data,
        kz_lines,
        lambda payload: lax.all_to_all(payload, "slab", split_axis=2, concat_axis=3, tiled=True),
        lambda payload: lax.all_to_all(payload, "slab", split_axis=3, concat_axis=2, tiled=True),
    )
    summed = lax.psum(partial_image, "coil")
    portion = summed.shape[1] // lax.axis_size("coil")
    summed = lax.dynamic_slice_in_dim(summed, lax.axis_index("coil") * portion, portion, 1)
    return summed.astype(jnp.bfloat16)


def solution(mesh):
    in_specs = (
        P(None, None, "slab", None),
        P("coil", None, "slab", None),
        P(None, "coil", "slab", None, None),
        P(None, "slab", None),
    )
    out_specs = P(None, "coil", "slab", None)
    return jax.shard_map(shards, mesh=mesh, in_specs=in_specs, out_specs=out_specs, check_vma=False)
```

profile of v0, /device:TPU:0, one launch (start us, length us, event | category | flops | bytes accessed | tf_op | source)
XLA Modules:
  0.0 1599.1 jit_solution(7993726364527364379)
XLA Ops:
  0.0 2.0 fusion.257
  2.0 0.0 slice-start.1
  2.0 8.3 copy.50
  10.3 8.6 fusion.72
  19.0 9.1 fusion.56
  28.1 9.1 fusion.59
  37.2 44.6 %fusion.8 = f32[2,4,32,128,320]{3,4,2,1,0:T(8,128)} fusion(f32[2,320,32,128]{3,1,2,0:T(8,128)} %fusion.72, f32[4,320,32,128]{3,1,2,0:T(8,128)} %fusion.59, f32[2,320,32,128]{3,1,2,0:T(8,128)} %copy.50, f32[4,320,32,128]{3,1,2,0:T(8,128)} %fusion.56), kind=kOutput, calls=%fused_computation.12 | convolution fusion | flops 6753955840 | bytes 104857600 | tf_op jit(solution)/shard_map/ky,scyzl->sckzl/dot_general | solution.py:56
  81.8 43.1 %fusion.9 = bf16[2,4,320,32,128]{4,2,3,1,0:T(8,128)(2,1)} fusion(f32[2,4,32,128,320]{3,4,2,1,0:T(8,128)} %fusion.8, f32[2,320,32,128]{3,1,2,0:T(8,128)} %fusion.72, f32[4,320,32,128]{3,1,2,0:T(8,128)} %fusion.59, f32[2,320,32,128]{3,1,2,0:T(8,128)} %copy.50, f32[4,320,32,128]{3,1,2,0:T(8,128)} %fusion.56, s32[128]{0:T(128)S(1)} %iota_add_fusion, ...), kind=kOutput, calls=%fused_computation.13 | convolution fusion | flops 9468772352 | bytes 126034560 | tf_op jit(solution)/shard_map/ky,scyzl->sckzl/dot_general | solution.py:57
  124.9 21.4 %copy.55 = bf16[2,4,320,32,128]{4,3,1,0,2:T(8,128)(2,1)} copy(bf16[2,4,320,32,128]{4,2,3,1,0:T(8,128)(2,1)} %fusion.9) | data formatting | bytes 41943040 | tf_op jit(solution)/shard_map/convert_element_type | solution.py:58
  146.3 7.7 all-to-all-start
  154.1 13.7 copy.60
  167.8 1.0 fusion.263
  168.8 1.0 fusion.261
  169.9 437.8 %all-to-all-done = bf16[2,4,320,32,128]{4,3,1,0,2:T(8,128)(2,1)} async-done(((bf16[2,4,320,32,128]{4,3,1,0,2:T(8,128)(2,1)}), bf16[2,4,320,32,128]{4,3,1,0,2:T(8,128)(2,1)}, u32[]{:S(2)}, u32[]{:S(2)}) %all-to-all-start) | async-done | bytes 20971552 | tf_op jit(solution)/shard_map/all_to_all | solution.py:100
  607.6 19.2 %copy.57 = bf16[2,4,40,8,32,128]{5,4,3,2,1,0:T(8,128)(2,1)} copy(bf16[2,4,40,8,32,128]{5,4,1,0,2,3:T(8,128)(2,1)} %bitcast.16) | data formatting | bytes 41943040 | tf_op jit(solution)/shard_map/all_to_all | solution.py:100
  626.8 21.7 %fusion.98 = f32[2,4,40,128,256]{4,3,2,1,0:T(8,128)} fusion(bf16[2,4,40,256,128]{4,3,2,1,0:T(8,128)(2,1)} %bitcast.172), kind=kOutput, calls=%fused_computation.86 | convolution fusion | flops 5369757696 | bytes 62914560 | tf_op jit(solution)/shard_map/jq,sckql->sckjl/dot_general | solution.py:70
  648.6 24.3 %fusion.21 = f32[2,4,40,128,256]{4,3,2,1,0:T(8,128)} fusion(bf16[2,4,40,256,128]{4,3,2,1,0:T(8,128)(2,1)} %bitcast.173, s32[128]{0:T(128)S(1)} %iota_add_fusion, pred[128]{0:T(512)(128)(4,1)S(1)} %iota_compare_fusion.4, bf16[256,256,1,1,1]{1,0,4,3,2:T(8,128)(2,1)S(1)} %fusion.263), kind=kOutput, calls=%fused_computation.25 | convolution fusion | flops 8063680512 | bytes 63046272 | tf_op jit(solution)/shard_map/jq,sckql->sckjl/dot_general | solution.py:72
  672.9 38.0 %fusion.12 = bf16[2,4,40,128,128]{3,4,2,1,0:T(8,128)(2,1)} fusion(bf16[2,4,40,128,128]{3,4,2,1,0:T(8,128)(2,1)} %copy.60, pred[2,40,128]{2,1,0:T(8,128)(4,1)S(1)} %broadcast_compare_fusion, f32[2,4,40,128,256]{4,3,2,1,0:T(8,128)} %fusion.98, f32[2,4,40,128,256]{4,3,2,1,0:T(8,128)} %fusion.21, s32[2,40,128]{2,1,0:T(8,128)S(1)} %broadcast_maximum_fusion), kind=kOutput, calls=%fused_computation.17 | convolution fusion | flops 16142827520 | bytes 104908800 | tf_op jit(solution)/shard_map/skjq,sckql->sckjl/dot_general | solution.py:73
  710.9 13.7 convert_bitcast_fusion
  724.5 28.2 %fusion.17 = f32[2,4,40,128,256]{4,3,2,1,0:T(8,128)} fusion(bf16[2,4,40,256,128]{3,4,1,2,0:T(8,128)(2,1)} %convert_bitcast_fusion, s32[128]{0:T(128)S(1)} %iota_add_fusion, pred[128]{0:T(512)(128)(4,1)S(1)} %iota_compare_fusion.4, bf16[256,256,1,1,1]{1,0,4,3,2:T(8,128)(2,1)S(1)} %fusion.261), kind=kOutput, calls=%fused_computation.21 | convolution fusion | flops 8063680512 | bytes 63046272 | tf_op jit(solution)/shard_map/qz,sckql->sckzl/dot_general | solution.py:83
  752.8 29.8 %fusion.10 = bf16[2,4,40,256,128]{3,4,2,1,0:T(8,128)(2,1)} fusion(f32[2,4,40,128,256]{4,3,2,1,0:T(8,128)} %fusion.17, bf16[2,4,40,256,128]{3,4,1,2,0:T(8,128)(2,1)} %convert_bitcast_fusion), kind=kOutput, calls=%fused_computation.14 | convolution fusion | flops 5390729216 | bytes 83886080 | tf_op jit(solution)/shard_map/qz,sckql->sckzl/dot_general | solution.py:82
  782.6 30.6 %copy.65 = bf16[2,4,40,256,128]{4,2,1,0,3:T(8,128)(2,1)} copy(bf16[2,4,40,256,128]{3,4,2,1,0:T(8,128)(2,1)} %fusion.10) | data formatting | bytes 41943040 | tf_op jit(solution)/shard_map/convert_element_type | solution.py:84
  813.3 6.1 all-to-all-start.1
  819.4 2.0 fusion.259
  821.3 450.3 %all-to-all-done.1 = bf16[2,4,40,256,128]{4,2,1,0,3:T(8,128)(2,1)} async-done(((bf16[2,4,40,256,128]{4,2,1,0,3:T(8,128)(2,1)}), bf16[2,4,40,256,128]{4,2,1,0,3:T(8,128)(2,1)}, u32[]{:S(2)}, u32[]{:S(2)}) %all-to-all-start.1) | async-done | bytes 20971552 | tf_op jit(solution)/shard_map/all_to_all | solution.py:101
  1271.7 19.4 %copy.67 = bf16[2,4,8,40,32,128]{5,3,2,4,1,0:T(8,128)(2,1)} copy(bf16[2,4,8,40,32,128]{5,3,1,0,4,2:T(8,128)(2,1)} %bitcast.33) | data formatting | bytes 41943040 | tf_op jit(solution)/shard_map/all_to_all | solution.py:101
  1291.1 26.3 %fusion.90 = f32[2,4,32,128,320]{3,4,2,1,0:T(8,128)} fusion(bf16[2,4,320,32,128]{4,2,3,1,0:T(8,128)(2,1)} %bitcast.170), kind=kOutput, calls=%fused_computation.83 | convolution fusion | flops 6712012800 | bytes 62914560 | tf_op jit(solution)/shard_map/ky,sckzl->scyzl/dot_general | solution.py:87
  1317.4 27.4 %fusion.13 = f32[2,4,32,128,320]{3,4,2,1,0:T(8,128)} fusion(bf16[2,4,320,32,128]{4,2,3,1,0:T(8,128)(2,1)} %bitcast.171, s32[128]{0:T(128)S(1)} %iota_add_fusion, pred[128]{0:T(512)(128)(4,1)S(1)} %iota_compare_fusion.4, bf16[320,320,1,1,1]{0,1,4,3,2:T(8,128)(2,1)S(1)} %fusion.259), kind=kOutput, calls=%fused_computation.18 | convolution fusion | flops 9405857792 | bytes 63120000 | tf_op jit(solution)/shard_map/ky,sckzl->scyzl/dot_general | solution.py:89
  1344.8 69.9 %fusion.3 = f32[2,320,32,128]{3,1,2,0:T(8,128)} fusion(f32[4,320,32,128]{3,1,2,0:T(8,128)} %fusion.59, f32[4,320,32,128]{3,1,2,0:T(8,128)} %fusion.56, f32[2,4,32,128,320]{3,4,2,1,0:T(8,128)} %fusion.90, f32[2,4,32,128,320]{3,4,2,1,0:T(8,128)} %fusion.13, s32[128]{0:T(128)S(1)} %iota_add_fusion, pred[128]{0:T(512)(128)(4,1)S(1)} %iota_compare_fusion.4), kind=kOutput, calls=%fused_computation.4 | convolution fusion | flops 16166551552 | bytes 136315520 | tf_op jit(solution)/shard_map/...l,lm->...m/dot_general | solution.py:40
  1414.7 181.1 %all-reduce.1 = bf16[2,320,32,128]{3,1,2,0:T(8,128)(2,1)} all-reduce(f32[2,320,32,128]{3,1,2,0:T(8,128)} %fusion.3), channel_id=1, replica_groups=mesh['slab'=8,'coil'=4] {'coil'}, use_global_device_ids=true, to_apply=%region_1.2 | all-reduce | flops 2621440 | bytes 15728640 | tf_op jit(solution)/shard_map/psum | solution.py:103
  1595.8 1.4 dynamic-slice_convert_fusion
  1597.2 1.4 copy.70
  (14 shorter events, 0.1 us)
Async XLA Ops:
  0.0 18.9 %slice-start = ((s8[10485760]{0:T(1024)(128)(4,1)}), s8[4194304]{0:T(1024)(128)(4,1)S(1)}, s32[]{:S(2)}) async-start(s8[10485760]{0:T(1024)(128)(4,1)} %bitcast.174), calls=%async_computation.2 | async-start | bytes 8388608
  2.0 16.9 %slice-start.1 = ((s8[10485760]{0:T(1024)(128)(4,1)}), s8[4194304]{0:T(1024)(128)(4,1)S(1)}, s32[]{:S(2)}) async-start(s8[10485760]{0:T(1024)(128)(4,1)} %bitcast.174), calls=%async_computation.3 | async-start | bytes 8388608
  10.3 8.6 slice-start.2
  146.3 461.3 %all-to-all-start = ((bf16[2,4,320,32,128]{4,3,1,0,2:T(8,128)(2,1)}), bf16[2,4,320,32,128]{4,3,1,0,2:T(8,128)(2,1)}, u32[]{:S(2)}, u32[]{:S(2)}) async-start(bf16[2,4,320,32,128]{4,3,1,0,2:T(8,128)(2,1)} %copy.55), calls=%async_computation | async-start | bytes 41943040 | tf_op jit(solution)/shard_map/all_to_all | solution.py:100
  154.1 15.7 copy-start
  813.3 458.4 %all-to-all-start.1 = ((bf16[2,4,40,256,128]{4,2,1,0,3:T(8,128)(2,1)}), bf16[2,4,40,256,128]{4,2,1,0,3:T(8,128)(2,1)}, u32[]{:S(2)}, u32[]{:S(2)}) async-start(bf16[2,4,40,256,128]{4,2,1,0,3:T(8,128)(2,1)} %copy.65), calls=%async_computation.1 | async-start | bytes 41943040 | tf_op jit(solution)/shard_map/all_to_all | solution.py:101
where the time goes:
time: 1610 us; the launch traced here: 1600 us
  waiting for transfers between devices  888 us (55%)
  matrix products  394 us (24%)
  blocking collectives  181 us (11%)
  local copies, waits for them, and re-layouts  116 us (7%)
    all_to_all x1, waiting for transfers between devices, shards(): lax.all_to_all(payload, 'slab', split_axis=3, concat_axis=2, tiled=True)  450 us
    all_to_all x1, waiting for transfers between devices, shards(): lax.all_to_all(payload, 'slab', split_axis=2, concat_axis=3, tiled=True)  438 us
    psum x1, blocking collectives, shards(): summed = lax.psum(partial_image, 'coil')  181 us
    dot_general x1, matrix products, lane_map(): jnp.einsum('...l,lm->...m', values, table.astype(jnp.float32), precision=...  69.9 us
    dot_general x1, matrix products, transform(): jnp.einsum('ky,scyzl->sckzl', y_cos, coil_image, preferred_element_type=j...  44.6 us
    dot_general x1, matrix products, transform(): jnp.einsum('ky,scyzl->sckzl', y_sin, turned_image, preferred_element_type...  43.1 us
    dot_general x1, matrix products, transform(): jnp.einsum('skjq,sckql->sckjl', onehot.astype(jnp.float32), kspace, preci...  38 us
  transfers between devices with their start and end apart: 2, of which 2 were waited for; matrix products, arithmetic and copies ran while one was open for 1% of the time, Pallas kernels for 0%

commit v1 on v0

v1 whole, which is shorter than its diff:
```python
import math

import jax
import jax.numpy as jnp
from jax import lax
from jax.sharding import PartitionSpec as P

F32 = jnp.float32
BF16 = jnp.bfloat16


def cos_sin(length):
    positions = jnp.arange(length, dtype=jnp.int32)
    phase = (positions[:, None] * positions[None, :] % length).astype(F32) * (
        2.0 * math.pi / length
    )
    factor = 1.0 / math.sqrt(length)
    return (
        (jnp.cos(phase) * factor).astype(BF16),
        (jnp.sin(phase) * factor).astype(BF16),
    )


def turned(values):
    half = values.shape[-1] // 2
    return jnp.concatenate([-values[..., half:], values[..., :half]], axis=-1)


def dup_halves(values):
    half = values.shape[-1] // 2
    real = values[..., :half]
    imag = values[..., half:]
    return (
        jnp.concatenate([real, real], axis=-1),
        jnp.concatenate([imag, imag], axis=-1),
    )


def state_gradient(pixels, sens_real, sens_imag, measured, kz_lines, y_tab):
    y_count = pixels.shape[0]
    coil_image = (sens_real * pixels + sens_imag * turned(pixels)).astype(BF16)
    prod = jnp.einsum("ky,cyzl->ckzl", y_tab, coil_image, preferred_element_type=F32)
    spectrum = (prod[:, :y_count] - turned(prod[:, y_count:])).astype(BF16)
    gathered = lax.all_to_all(spectrum, "slab", split_axis=1, concat_axis=2, tiled=True)
    z_count = gathered.shape[2]
    z_cos, z_sin = cos_sin(z_count)
    z_tab = jnp.concatenate([z_cos, z_sin], axis=1)
    sampled = kz_lines >= 0
    kz_index = jnp.maximum(kz_lines, 0)
    onehot = (
        (kz_index[..., None] == jnp.arange(z_count, dtype=jnp.int32)) & sampled[..., None]
    ).astype(BF16)
    rows = jnp.einsum("kjq,qz->kjz", onehot, z_tab, preferred_element_type=F32).astype(BF16)
    rows_cos = rows[..., :z_count]
    rows_sin = rows[..., z_count:]
    k_cos = jnp.einsum("kjz,ckzl->ckjl", rows_cos, gathered, preferred_element_type=F32)
    k_sin = jnp.einsum("kjz,ckzl->ckjl", rows_sin, gathered, preferred_element_type=F32)
    kspace = k_cos - turned(k_sin)
    residual = jnp.where(
        sampled[None, :, :, None], kspace - measured.astype(F32), F32(0.0)
    ).astype(BF16)
    a_cos = jnp.einsum("kjz,ckjl->ckzl", rows_cos, residual, preferred_element_type=F32)
    a_sin = jnp.einsum("kjz,ckjl->ckzl", rows_sin, residual, preferred_element_type=F32)
    adjoint_z = (a_cos + turned(a_sin)).astype(BF16)
    returned = lax.all_to_all(adjoint_z, "slab", split_axis=2, concat_axis=1, tiled=True)
    prod_back = jnp.einsum("yk,ckzl->cyzl", y_tab, returned, preferred_element_type=F32)
    coil_back = prod_back[:, :y_count] + turned(prod_back[:, y_count:])
    term = sens_real * coil_back - sens_imag * turned(coil_back)
    partial = jnp.sum(term, axis=0)
    summed = lax.psum_scatter(partial, "coil", scatter_dimension=0, tiled=True)
    return summed.astype(BF16)


def shards(image, coil_maps, y_data, kz_lines):
    state_count, y_count = image.shape[0], image.shape[1]
    y_cos, y_sin = cos_sin(y_count)
    y_tab = jnp.concatenate([y_cos, y_sin], axis=0)
    sens_real, sens_imag = dup_halves(coil_maps.astype(F32))
    outputs = []
    for state in range(state_count):
        outputs.append(
            state_gradient(
                image[state].astype(F32),
                sens_real,
                sens_imag,
                y_data[state],
                kz_lines[state],
                y_tab,
            )
        )
    return jnp.stack(outputs)


def solution(mesh):
    in_specs = (
        P(None, None, "slab", None),
        P("coil", None, "slab", None),
        P(None, "coil", "slab", None, None),
        P(None, "slab", None),
    )
    out_specs = P(None, "coil", "slab", None)
    return jax.shard_map(shards, mesh=mesh, in_specs=in_specs, out_specs=out_specs, check_vma=False)
```

time: 1610 us -> 1470 us (0.913)
  other arithmetic: 5.94 us -> 331 us
  waiting for transfers between devices: 888 us -> 613 us
  blocking collectives: 181 us -> 0 us
  matrix products: 394 us -> 239 us
  local copies, waits for them, and re-layouts: 116 us -> 240 us
    all_to_all x2 -> x4, waiting for transfers between devices: 888 us -> 516 us  [the longest x2 306 us: state_gradient(): lax.all_to_all(adjoint_z, 'slab', split_axis=2, concat_axis=1, tiled=True)]
    psum x1 -> x0, blocking collectives: 181 us -> none  [shards(): summed = lax.psum(partial_image, 'coil')]
    neg x0 -> x11, other arithmetic: none -> 171 us  [turned(): return jnp.concatenate([-values[..., half:], values[..., :half]], axis=-1)]
    dot_general x14, matrix products: 394 us -> 239 us  [the longest x2 76.4 us: state_gradient(): jnp.einsum('ky,cyzl->ckzl', y_tab, coil_image, preferred_element_type=F32)]
    reduce_scatter x0 -> x2, waiting for transfers between devices: none -> 97.1 us  [state_gradient(): summed = lax.psum_scatter(partial, 'coil', scatter_dimension=0, tiled=True)]
    reduce_sum x0 -> x1, other arithmetic: none -> 53.5 us  [state_gradient(): partial = jnp.sum(term, axis=0)]
    add x1 -> x2, other arithmetic: 0.01 us -> 43.6 us  [state_gradient(): coil_back = prod_back[:, :y_count] + turned(prod_back[:, y_count:])]
    convert_element_type x0 -> x4, other arithmetic: none -> 39.2 us  [the longest x2 35.9 us: state_gradient(): spectrum = (prod[:, :y_count] - turned(prod[:, y_count:])).astype(BF16)]
  transfers between devices with their start and end apart: 2 -> 6, of which waited for: 2 -> 6; matrix products, arithmetic and copies ran while one was open for 1% -> 27% of each run, Pallas kernels for 0% -> 0%
where the time goes in v1:
time: 1470 us; the launch traced here: 1460 us
  waiting for transfers between devices  613 us (42%)
  other arithmetic  331 us (23%)
  local copies, waits for them, and re-layouts  240 us (16%)
  matrix products  239 us (16%)
  starting transfers between devices  23.6 us (2%)
    all_to_all x2, waiting for transfers between devices, state_gradient(): lax.all_to_all(adjoint_z, 'slab', split_axis=2, concat_axis=1, tiled=True)  306 us
    all_to_all x2, waiting for transfers between devices, state_gradient(): lax.all_to_all(spectrum, 'slab', split_axis=1, concat_axis=2, tiled=True)  210 us
    neg x11, other arithmetic, turned(): return jnp.concatenate([-values[..., half:], values[..., :half]], axis=-1)  171 us
    reduce_scatter x2, waiting for transfers between devices, state_gradient(): summed = lax.psum_scatter(partial, 'coil', scatter_dimension=0, tiled=True)  97.1 us
    dot_general x2, matrix products, state_gradient(): jnp.einsum('ky,cyzl->ckzl', y_tab, coil_image, preferred_element_type=F32)  76.4 us
    reduce_sum x1, other arithmetic, state_gradient(): partial = jnp.sum(term, axis=0)  53.5 us
    all_to_all x4, local copies, waits for them, and re-layouts, state_gradient(): lax.all_to_all(adjoint_z, 'slab', split_axis=2, concat_axis=1, tiled=True)  53.4 us
    dot_general x2, matrix products, state_gradient(): jnp.einsum('yk,ckzl->cyzl', y_tab, returned, preferred_element_type=F32)  45.2 us
  transfers between devices with their start and end apart: 6, of which 6 were waited for; matrix products, arithmetic and copies ran while one was open for 27% of the time, Pallas kernels for 0%

profile of v1, /device:TPU:0, one launch (start us, length us, event | category | flops | bytes accessed | tf_op | source)
XLA Modules:
  0.0 1460.2 jit_solution(11463581786942432484)
XLA Ops:
  46.6 15.9 %copy.65 = bf16[4,320,32,128]{1,3,2,0:T(8,128)(2,1)} copy(bf16[4,320,32,128]{3,2,1,0:T(8,128)(2,1)} %param.5) | data formatting | bytes 20971520 | tf_op args[1]
  75.5 38.2 %convolution_bitcast_fusion.1 = f32[4,640,32,128]{1,3,2,0:T(8,128)} fusion(f32[4,320,32,64]{1,3,2,0:T(8,128)} %get-tuple-element.24, f32[4,320,32,64]{1,3,2,0:T(8,128)} %get-tuple-element.23, f32[320,32,128]{0,2,1:T(8,128)} %copy.80, f32[320,32,128]{0,2,1:T(8,128)} %copy.79, bf16[320,320]{0,1:T(8,128)(2,1)S(1)} %get-tuple-element.43, ...), kind=kOutput, calls=%fused_computation.29 | convolution fusion | flops 6743162880 | bytes 73809920 | tf_op jit(solution)/shard_map/ky,cyzl->ckzl/dot_general | solution.py:42
  113.8 16.6 %slice_negate_fusion.2 = (f32[4,320,32,64]{1,3,2,0:T(8,128)S(1)}, f32[4,320,32,64]{1,3,2,0:T(8,128)}) fusion(f32[4,640,32,128]{1,3,2,0:T(8,128)} %convolution_bitcast_fusion.1), kind=kLoop, calls=%fused_computation.34 | loop fusion | flops 2621440 | bytes 41943040 | tf_op jit(solution)/shard_map/neg | solution.py:26
  130.3 18.0 %fusion = bf16[4,320,32,128]{1,3,2,0:T(8,128)(2,1)} fusion(f32[4,640,32,128]{1,3,2,0:T(8,128)} %convolution_bitcast_fusion.1, f32[4,320,32,64]{1,3,2,0:T(8,128)} %get-tuple-element.10, f32[4,320,32,64]{1,3,2,0:T(8,128)S(1)} %get-tuple-element.9), kind=kLoop, calls=%fused_computation.2 | loop fusion | flops 15728640 | bytes 52428800 | tf_op jit(solution)/shard_map/convert_element_type | solution.py:43
  148.4 16.0 %copy.82 = bf16[4,320,32,128]{3,2,0,1:T(8,128)(2,1)} copy(bf16[4,320,32,128]{1,3,2,0:T(8,128)(2,1)} %fusion) | data formatting | bytes 20971520 | tf_op jit(solution)/shard_map/convert_element_type | solution.py:43
  192.1 38.2 %convolution_bitcast_fusion.3 = f32[4,640,32,128]{1,3,2,0:T(8,128)} fusion(f32[4,320,32,64]{1,3,2,0:T(8,128)} %get-tuple-element.24, f32[4,320,32,64]{1,3,2,0:T(8,128)} %get-tuple-element.23, f32[320,32,128]{0,2,1:T(8,128)} %copy.67, f32[320,32,128]{0,2,1:T(8,128)} %copy.66, bf16[320,320]{0,1:T(8,128)(2,1)S(1)} %get-tuple-element.43, ...), kind=kOutput, calls=%fused_computation.31 | convolution fusion | flops 6743162880 | bytes 73809920 | tf_op jit(solution)/shard_map/ky,cyzl->ckzl/dot_general | solution.py:42
  230.4 16.6 %slice_negate_fusion.5 = (f32[4,320,32,64]{1,3,2,0:T(8,128)S(1)}, f32[4,320,32,64]{1,3,2,0:T(8,128)}) fusion(f32[4,640,32,128]{1,3,2,0:T(8,128)} %convolution_bitcast_fusion.3), kind=kLoop, calls=%fused_computation.37 | loop fusion | flops 2621440 | bytes 41943040 | tf_op jit(solution)/shard_map/neg | solution.py:26
  246.9 17.9 %fusion.1 = bf16[4,320,32,128]{1,3,2,0:T(8,128)(2,1)} fusion(f32[4,640,32,128]{1,3,2,0:T(8,128)} %convolution_bitcast_fusion.3, f32[4,320,32,64]{1,3,2,0:T(8,128)} %get-tuple-element.14, f32[4,320,32,64]{1,3,2,0:T(8,128)S(1)} %get-tuple-element.13), kind=kLoop, calls=%fused_computation.5 | loop fusion | flops 15728640 | bytes 52428800 | tf_op jit(solution)/shard_map/convert_element_type | solution.py:43
  264.8 16.0 %copy.69 = bf16[4,320,32,128]{3,2,0,1:T(8,128)(2,1)} copy(bf16[4,320,32,128]{1,3,2,0:T(8,128)(2,1)} %fusion.1) | data formatting | bytes 20971520 | tf_op jit(solution)/shard_map/convert_element_type | solution.py:43
  280.8 119.0 %all-to-all-done.2 = bf16[4,320,32,128]{3,2,0,1:T(8,128)(2,1)} async-done(((bf16[4,320,32,128]{3,2,0,1:T(8,128)(2,1)}), bf16[4,320,32,128]{3,2,0,1:T(8,128)(2,1)}, u32[]{:S(2)}, u32[]{:S(2)}) %all-to-all-start.2) | async-done | bytes 10485792 | tf_op jit(solution)/shard_map/all_to_all | solution.py:44
  492.4 15.5 %slice_negate_fusion.6 = (f32[4,40,256,64]{2,3,0,1:T(8,128)}, f32[4,40,256,64]{2,3,0,1:T(8,128)}) fusion(f32[4,40,256,128]{2,3,0,1:T(8,128)} %convolution_bitcast_fusion.4), kind=kLoop, calls=%fused_computation.42 | loop fusion | flops 2621440 | bytes 41943040 | tf_op jit(solution)/shard_map/neg | solution.py:26
  507.9 15.1 %fusion.19 = bf16[4,40,256,128]{2,3,0,1:T(8,128)(2,1)} fusion(f32[4,40,256,64]{2,3,0,1:T(8,128)} %get-tuple-element.20, f32[4,40,256,64]{2,3,0,1:T(8,128)} %get-tuple-element.19, bf16[4,40,128,128]{2,3,0,1:T(8,128)(2,1)} %fusion.31, bf16[40,128,512]{2,1,0:T(8,128)(2,1)} %fusion.52), kind=kOutput, calls=%fused_computation.27 | convolution fusion | flops 1357905920 | bytes 39321600 | tf_op jit(solution)/shard_map/kjz,ckjl->ckzl/dot_general | solution.py:62
  523.0 18.0 %copy.88 = bf16[4,40,256,128]{3,0,1,2:T(4,128)(2,1)} copy(bf16[4,40,256,128]{2,3,0,1:T(8,128)(2,1)} %fusion.19) | data formatting | bytes 20971520 | tf_op jit(solution)/shard_map/convert_element_type | solution.py:64
  541.0 91.3 %all-to-all-done = bf16[4,320,32,128]{3,2,0,1:T(8,128)(2,1)} async-done(((bf16[4,320,32,128]{3,2,0,1:T(8,128)(2,1)}), bf16[4,320,32,128]{3,2,0,1:T(8,128)(2,1)}, u32[]{:S(2)}, u32[]{:S(2)}) %all-to-all-start) | async-done | bytes 10485792 | tf_op jit(solution)/shard_map/all_to_all | solution.py:44
  710.4 15.5 %slice_negate_fusion.7 = (f32[4,40,256,64]{2,3,0,1:T(8,128)}, f32[4,40,256,64]{2,3,0,1:T(8,128)}) fusion(f32[4,40,256,128]{2,3,0,1:T(8,128)} %convolution_bitcast_fusion.5), kind=kLoop, calls=%fused_computation.43 | loop fusion | flops 2621440 | bytes 41943040 | tf_op jit(solution)/shard_map/neg | solution.py:26
  725.9 15.1 %fusion.18 = bf16[4,40,256,128]{2,3,0,1:T(8,128)(2,1)} fusion(f32[4,40,256,64]{2,3,0,1:T(8,128)} %get-tuple-element.22, f32[4,40,256,64]{2,3,0,1:T(8,128)} %get-tuple-element.21, bf16[4,40,128,128]{2,3,0,1:T(8,128)(2,1)} %fusion.28, bf16[40,128,512]{2,1,0:T(8,128)(2,1)} %fusion.55), kind=kOutput, calls=%fused_computation.25 | convolution fusion | flops 1357905920 | bytes 39321600 | tf_op jit(solution)/shard_map/kjz,ckjl->ckzl/dot_general | solution.py:62
  741.0 18.0 %copy.75 = bf16[4,40,256,128]{3,0,1,2:T(4,128)(2,1)} copy(bf16[4,40,256,128]{2,3,0,1:T(8,128)(2,1)} %fusion.18) | data formatting | bytes 20971520 | tf_op jit(solution)/shard_map/convert_element_type | solution.py:64
  759.0 105.4 %all-to-all-done.3 = bf16[4,40,256,128]{3,0,1,2:T(4,128)(2,1)} async-done(((bf16[4,40,256,128]{3,0,1,2:T(4,128)(2,1)}), bf16[4,40,256,128]{3,0,1,2:T(4,128)(2,1)}, u32[]{:S(2)}, u32[]{:S(2)}) %all-to-all-start.3) | async-done | bytes 10485792 | tf_op jit(solution)/shard_map/all_to_all | solution.py:65
  882.0 14.7 %copy.90 = bf16[4,8,40,32,128]{4,2,1,3,0:T(8,128)(2,1)} copy(bf16[4,8,40,32,128]{4,3,1,2,0:T(8,128)(2,1)} %bitcast.110) | data formatting | bytes 20971520 | tf_op jit(solution)/shard_map/all_to_all | solution.py:65
  896.6 200.1 %all-to-all-done.1 = bf16[4,40,256,128]{3,0,1,2:T(4,128)(2,1)} async-done(((bf16[4,40,256,128]{3,0,1,2:T(4,128)(2,1)}), bf16[4,40,256,128]{3,0,1,2:T(4,128)(2,1)}, u32[]{:S(2)}, u32[]{:S(2)}) %all-to-all-start.1) | async-done | bytes 10485792 | tf_op jit(solution)/shard_map/all_to_all | solution.py:65
  1108.8 14.8 %copy.77 = bf16[4,8,40,32,128]{4,2,1,3,0:T(8,128)(2,1)} copy(bf16[4,8,40,32,128]{4,3,1,2,0:T(8,128)(2,1)} %bitcast.111) | data formatting | bytes 20971520 | tf_op jit(solution)/shard_map/all_to_all | solution.py:65
  1123.5 22.5 %convolution_bitcast_fusion.2 = f32[4,640,32,128]{1,3,2,0:T(8,128)} fusion(bf16[4,320,32,128]{3,1,2,0:T(8,128)(2,1)} %bitcast.113, bf16[320,320]{0,1:T(8,128)(2,1)S(1)} %copy-done.1, bf16[320,320]{0,1:T(8,128)(2,1)S(1)} %copy-done.3), kind=kOutput, calls=%fused_computation.30 | convolution fusion | flops 6711705600 | bytes 52838400 | tf_op jit(solution)/shard_map/yk,ckzl->cyzl/dot_general | solution.py:66
  1146.0 16.5 %slice_negate_fusion.4 = (f32[4,320,32,64]{1,3,2,0:T(8,128)S(1)}, f32[4,320,32,64]{1,3,2,0:T(8,128)}) fusion(f32[4,640,32,128]{1,3,2,0:T(8,128)} %convolution_bitcast_fusion.2), kind=kLoop, calls=%fused_computation.36 | loop fusion | flops 2621440 | bytes 41943040 | tf_op jit(solution)/shard_map/neg | solution.py:26
  1162.6 21.8 %slice_add_fusion.1 = f32[4,320,32,128]{1,3,2,0:T(8,128)} fusion(f32[4,640,32,128]{1,3,2,0:T(8,128)} %convolution_bitcast_fusion.2, f32[4,320,32,64]{1,3,2,0:T(8,128)} %get-tuple-element.12, f32[4,320,32,64]{1,3,2,0:T(8,128)S(1)} %get-tuple-element.11), kind=kLoop, calls=%fused_computation.3 | loop fusion | flops 10485760 | bytes 62914560 | tf_op jit(solution)/shard_map/add | solution.py:67
  1184.4 20.1 %slice_negate_fusion.3 = (f32[4,320,32,64]{1,3,2,0:T(8,128)}, f32[4,320,32,64]{1,3,2,0:T(8,128)}) fusion(f32[4,320,32,128]{1,3,2,0:T(8,128)} %slice_add_fusion.1), kind=kLoop, calls=%fused_computation.35 | loop fusion | flops 2621440 | bytes 41943040 | tf_op jit(solution)/shard_map/neg | solution.py:26
  1204.4 22.7 %convolution_bitcast_fusion = f32[4,640,32,128]{1,3,2,0:T(8,128)} fusion(bf16[4,320,32,128]{3,1,2,0:T(8,128)(2,1)} %bitcast.112, bf16[320,320]{0,1:T(8,128)(2,1)S(1)} %copy-done.1, bf16[320,320]{0,1:T(8,128)(2,1)S(1)} %copy-done.3), kind=kOutput, calls=%fused_computation.28 | convolution fusion | flops 6711705600 | bytes 52838400 | tf_op jit(solution)/shard_map/yk,ckzl->cyzl/dot_general | solution.py:66
  1227.1 16.7 %slice_negate_fusion.1 = (f32[4,320,32,64]{1,3,2,0:T(8,128)S(1)}, f32[4,320,32,64]{1,3,2,0:T(8,128)}) fusion(f32[4,640,32,128]{1,3,2,0:T(8,128)} %convolution_bitcast_fusion), kind=kLoop, calls=%fused_computation.33 | loop fusion | flops 2621440 | bytes 41943040 | tf_op jit(solution)/shard_map/neg | solution.py:26
  1243.8 21.8 %slice_add_fusion = f32[4,320,32,128]{1,3,2,0:T(8,128)} fusion(f32[4,640,32,128]{1,3,2,0:T(8,128)} %convolution_bitcast_fusion, f32[4,320,32,64]{1,3,2,0:T(8,128)} %get-tuple-element.8, f32[4,320,32,64]{1,3,2,0:T(8,128)S(1)} %get-tuple-element.7), kind=kLoop, calls=%fused_computation | loop fusion | flops 10485760 | bytes 62914560 | tf_op jit(solution)/shard_map/add | solution.py:67
  1265.6 20.0 %slice_negate_fusion = (f32[4,320,32,64]{1,3,2,0:T(8,128)}, f32[4,320,32,64]{1,3,2,0:T(8,128)}) fusion(f32[4,320,32,128]{1,3,2,0:T(8,128)} %slice_add_fusion), kind=kLoop, calls=%fused_computation.32 | loop fusion | flops 2621440 | bytes 41943040 | tf_op jit(solution)/shard_map/neg | solution.py:26
  1285.6 53.5 %fusion.9 = (f32[320,32,128]{0,2,1:T(8,128)}, f32[320,32,128]{0,2,1:T(8,128)}) fusion(f32[4,320,32,128]{1,3,2,0:T(8,128)} %slice_add_fusion.1, f32[4,320,32,64]{1,3,2,0:T(8,128)} %get-tuple-element.24, f32[4,320,32,64]{1,3,2,0:T(8,128)} %get-tuple-element.23, f32[4,320,32,64]{1,3,2,0:T(8,128)} %get-tuple-element.18, ...), kind=kLoop, calls=%fused_computation.14 | loop fusion | flops 60293120 | bytes 115343360 | tf_op jit(solution)/shard_map/reduce_sum | solution.py:69
  1352.0 44.5 %reduce-scatter.3.cloned.1.call-done = f32[80,32,128]{2,1,0:T(8,128)} async-done(((f32[320,32,128]{2,1,0:T(8,128)}), f32[80,32,128]{2,1,0:T(8,128)}) %reduce-scatter.3.cloned.1.call-update) | async-done | bytes 1310736 | tf_op jit(solution)/shard_map/reduce_scatter | solution.py:70
  1397.9 52.7 %reduce-scatter.5.cloned.1.call-done = f32[80,32,128]{2,1,0:T(8,128)} async-done(((f32[320,32,128]{2,1,0:T(8,128)}), f32[80,32,128]{2,1,0:T(8,128)}) %reduce-scatter.5.cloned.1.call-update) | async-done | bytes 1310736 | tf_op jit(solution)/shard_map/reduce_scatter | solution.py:70
  (53 shorter events, 298.0 us)
Async XLA Ops:
  8.7 183.4 %copy-start = (bf16[320,320]{0,1:T(8,128)(2,1)}, bf16[320,320]{0,1:T(8,128)(2,1)S(1)}, u32[]{:S(2)}) copy-start(bf16[320,320]{0,1:T(8,128)(2,1)S(1)} %get-tuple-element.43) | copy-start | bytes 614404
  8.7 183.4 %copy-start.2 = (bf16[320,320]{0,1:T(8,128)(2,1)}, bf16[320,320]{0,1:T(8,128)(2,1)S(1)}, u32[]{:S(2)}) copy-start(bf16[320,320]{0,1:T(8,128)(2,1)S(1)} %get-tuple-element.44) | copy-start | bytes 614404
  164.4 235.4 %all-to-all-start.2 = ((bf16[4,320,32,128]{3,2,0,1:T(8,128)(2,1)}), bf16[4,320,32,128]{3,2,0,1:T(8,128)(2,1)}, u32[]{:S(2)}, u32[]{:S(2)}) async-start(bf16[4,320,32,128]{3,2,0,1:T(8,128)(2,1)} %copy.82), calls=%async_computation.3 | async-start | bytes 20971520 | tf_op jit(solution)/shard_map/all_to_all | solution.py:44
  399.8 232.5 %all-to-all-start = ((bf16[4,320,32,128]{3,2,0,1:T(8,128)(2,1)}), bf16[4,320,32,128]{3,2,0,1:T(8,128)(2,1)}, u32[]{:S(2)}, u32[]{:S(2)}) async-start(bf16[4,320,32,128]{3,2,0,1:T(8,128)(2,1)} %copy.69), calls=%async_computation | async-start | bytes 20971520 | tf_op jit(solution)/shard_map/all_to_all | solution.py:44
  418.0 9.1 copy-start.4
  632.3 232.1 %all-to-all-start.3 = ((bf16[4,40,256,128]{3,0,1,2:T(4,128)(2,1)}), bf16[4,40,256,128]{3,0,1,2:T(4,128)(2,1)}, u32[]{:S(2)}, u32[]{:S(2)}) async-start(bf16[4,40,256,128]{3,0,1,2:T(4,128)(2,1)} %copy.88), calls=%async_computation.4 | async-start | bytes 20971520 | tf_op jit(solution)/shard_map/all_to_all | solution.py:65
  864.4 232.3 %all-to-all-start.1 = ((bf16[4,40,256,128]{3,0,1,2:T(4,128)(2,1)}), bf16[4,40,256,128]{3,0,1,2:T(4,128)(2,1)}, u32[]{:S(2)}, u32[]{:S(2)}) async-start(bf16[4,40,256,128]{3,0,1,2:T(4,128)(2,1)} %copy.75), calls=%async_computation.1 | async-start | bytes 20971520 | tf_op jit(solution)/shard_map/all_to_all | solution.py:65
  869.6 526.9 %reduce-scatter.3.cloned.1.call-start = ((), (), s32[]{:S(2)}) async-start(), calls=%async_computation.6 | async-start | bytes 6553600 | tf_op jit(solution)/shard_map/reduce_scatter | solution.py:70
  1108.8 14.8 %copy-start.1 = (bf16[320,320]{0,1:T(8,128)(2,1)S(1)}, bf16[320,320]{0,1:T(8,128)(2,1)}, u32[]{:S(2)}) copy-start(bf16[320,320]{0,1:T(8,128)(2,1)} %copy-done) | copy-start | bytes 614404
  1108.8 14.8 %copy-start.3 = (bf16[320,320]{0,1:T(8,128)(2,1)S(1)}, bf16[320,320]{0,1:T(8,128)(2,1)}, u32[]{:S(2)}) copy-start(bf16[320,320]{0,1:T(8,128)(2,1)} %copy-done.2) | copy-start | bytes 614404
  1345.5 105.1 %reduce-scatter.5.cloned.1.call-start = ((), (), s32[]{:S(2)}) async-start(), calls=%async_computation.7 | async-start | bytes 6553600 | tf_op jit(solution)/shard_map/reduce_scatter | solution.py:70
Sparse Core Ops, SparseCore 0:
  1345.6 50.8 reduce-scatter.2
  1399.2 51.3 reduce-scatter.4

commit v2 on v1

v2 whole, which is shorter than its diff:
```python
import math

import jax
import jax.numpy as jnp
from jax import lax
from jax.sharding import PartitionSpec as P

F32 = jnp.float32
BF16 = jnp.bfloat16


def cos_sin(length):
    positions = jnp.arange(length, dtype=jnp.int32)
    phase = (positions[:, None] * positions[None, :] % length).astype(F32) * (
        2.0 * math.pi / length
    )
    factor = 1.0 / math.sqrt(length)
    return (
        (jnp.cos(phase) * factor).astype(BF16),
        (jnp.sin(phase) * factor).astype(BF16),
    )


def turned(values):
    half = values.shape[-1] // 2
    return jnp.concatenate([-values[..., half:], values[..., :half]], axis=-1)


def dup_halves(values):
    half = values.shape[-1] // 2
    real = values[..., :half]
    imag = values[..., half:]
    return (
        jnp.concatenate([real, real], axis=-1),
        jnp.concatenate([imag, imag], axis=-1),
    )


def with_turned(values, axis):
    return jnp.concatenate([values, turned(values)], axis=axis)


def chunk_gradient(pixels, sens_real, sens_imag, measured, kz_lines, y_fwd, y_back):
    y_count = pixels.shape[0]
    coil_image = (sens_real * pixels + sens_imag * turned(pixels)).astype(BF16)
    spectrum = jnp.einsum(
        "ky,cyzl->ckzl", y_fwd, with_turned(coil_image, 1), preferred_element_type=F32
    ).astype(BF16)
    gathered = lax.all_to_all(spectrum, "slab", split_axis=1, concat_axis=2, tiled=True)
    z_count = gathered.shape[2]
    z_cos, z_sin = cos_sin(z_count)
    sampled = kz_lines >= 0
    kz_index = jnp.maximum(kz_lines, 0)
    onehot = (
        (kz_index[..., None] == jnp.arange(z_count, dtype=jnp.int32)) & sampled[..., None]
    ).astype(BF16)
    z_fwd = jnp.concatenate([z_cos, -z_sin], axis=1)
    rows_fwd = jnp.einsum("kjq,qz->kjz", onehot, z_fwd, preferred_element_type=F32).astype(BF16)
    kspace = jnp.einsum(
        "kjz,ckzl->ckjl", rows_fwd, with_turned(gathered, 2), preferred_element_type=F32
    )
    residual = jnp.where(
        sampled[None, :, :, None], kspace - measured.astype(F32), F32(0.0)
    ).astype(BF16)
    rows_back = jnp.concatenate(
        [rows_fwd[..., :z_count], -rows_fwd[..., z_count:]], axis=1
    )
    adjoint_z = jnp.einsum(
        "kjz,ckjl->ckzl", rows_back, with_turned(residual, 2), preferred_element_type=F32
    ).astype(BF16)
    returned = lax.all_to_all(adjoint_z, "slab", split_axis=2, concat_axis=1, tiled=True)
    both = jnp.einsum(
        "yk,ckzl->cyzl", y_back, with_turned(returned, 1), preferred_element_type=F32
    )
    coil_back = both[:, :y_count]
    turned_back = both[:, y_count:]
    return jnp.sum(sens_real * coil_back - sens_imag * turned_back, axis=0)


def shards(image, coil_maps, y_data, kz_lines):
    state_count, y_count = image.shape[0], image.shape[1]
    coil_count = coil_maps.shape[0]
    group = 2 if coil_count % 2 == 0 else 1
    y_cos, y_sin = cos_sin(y_count)
    y_fwd = jnp.concatenate([y_cos, -y_sin], axis=1)
    y_back = jnp.concatenate(
        [jnp.concatenate([y_cos, y_sin], axis=1), jnp.concatenate([-y_sin, y_cos], axis=1)],
        axis=0,
    )
    sens_real, sens_imag = dup_halves(coil_maps.astype(F32))
    outputs = []
    for state in range(state_count):
        pixels = image[state].astype(F32)
        total = None
        for first in range(0, coil_count, group):
            part = chunk_gradient(
                pixels,
                sens_real[first : first + group],
                sens_imag[first : first + group],
                y_data[state, first : first + group],
                kz_lines[state],
                y_fwd,
                y_back,
            )
            total = part if total is None else total + part
        summed = lax.psum_scatter(total, "coil", scatter_dimension=0, tiled=True)
        outputs.append(summed.astype(BF16))
    return jnp.stack(outputs)


def solution(mesh):
    in_specs = (
        P(None, None, "slab", None),
        P("coil", None, "slab", None),
        P(None, "coil", "slab", None, None),
        P(None, "slab", None),
    )
    out_specs = P(None, "coil", "slab", None)
    return jax.shard_map(shards, mesh=mesh, in_specs=in_specs, out_specs=out_specs, check_vma=False)
```

time: 1470 us -> 1400 us (0.952)
  matrix products: 239 us -> 160 us
  other arithmetic: 331 us -> 276 us
  local copies, waits for them, and re-layouts: 240 us -> 281 us
  starting transfers between devices: 23.6 us -> 41.9 us
    dot_general x14 -> x18, matrix products: 239 us -> 160 us  [the longest x4 70.3 us: chunk_gradient(): jnp.einsum('yk,ckzl->cyzl', y_back, with_turned(returned, 1), preferred_e...]
    neg x11 -> x17, other arithmetic: 171 us -> 96.8 us  [turned(): return jnp.concatenate([-values[..., half:], values[..., :half]], axis=-1)]
    convert_element_type x2 -> x4, other arithmetic: 35.9 us -> 87.1 us  [the longest x2 71.6 us: chunk_gradient(): coil_image = (sens_real * pixels + sens_imag * turned(pixels)).astype(BF16)]
    all_to_all x6 -> x20, local copies, waits for them, and re-layouts: 75.9 us -> 123 us  [the longest x12 64.7 us: chunk_gradient(): lax.all_to_all(adjoint_z, 'slab', split_axis=2, concat_axis=1, tiled=True)]
    add x2, other arithmetic: 43.6 us -> 12.7 us  [shards(): total = part if total is None else total + part]
    all_to_all x4 -> x8, starting transfers between devices: 23.1 us -> 41.8 us  [the longest x4 22.4 us: chunk_gradient(): lax.all_to_all(spectrum, 'slab', split_axis=1, concat_axis=2, tiled=True)]
    slice x1, local copies, waits for them, and re-layouts: 13.1 us -> 30.7 us  [dup_halves(): imag = values[..., half:]]
    unnamed x13 -> x66, local copies, waits for them, and re-layouts: 31.8 us -> 17.4 us
  transfers between devices with their start and end apart: 6 -> 10, of which waited for: 6 -> 10; matrix products, arithmetic and copies ran while one was open for 27% -> 29% of each run, Pallas kernels for 0% -> 0%
where the time goes in v2:
time: 1400 us; the launch traced here: 1390 us
  waiting for transfers between devices  614 us (44%)
  local copies, waits for them, and re-layouts  281 us (20%)
  other arithmetic  276 us (20%)
  matrix products  160 us (11%)
  starting transfers between devices  41.9 us (3%)
  between operations  14.2 us (1%)
    all_to_all x4, waiting for transfers between devices, chunk_gradient(): lax.all_to_all(spectrum, 'slab', split_axis=1, concat_axis=2, tiled=True)  281 us
    all_to_all x4, waiting for transfers between devices, chunk_gradient(): lax.all_to_all(adjoint_z, 'slab', split_axis=2, concat_axis=1, tiled=True)  237 us
    neg x17, other arithmetic, turned(): return jnp.concatenate([-values[..., half:], values[..., :half]], axis=-1)  96.8 us
    reduce_scatter x2, waiting for transfers between devices, shards(): summed = lax.psum_scatter(total, 'coil', scatter_dimension=0, tiled=True)  96 us
    convert_element_type x2, other arithmetic, chunk_gradient(): coil_image = (sens_real * pixels + sens_imag * turned(pixels)).astype(BF16)  71.6 us
    dot_general x4, matrix products, chunk_gradient(): jnp.einsum('yk,ckzl->cyzl', y_back, with_turned(returned, 1), preferred_e...  70.3 us
    all_to_all x12, local copies, waits for them, and re-layouts, chunk_gradient(): lax.all_to_all(adjoint_z, 'slab', split_axis=2, concat_axis=1, tiled=True)  64.7 us
    all_to_all x8, local copies, waits for them, and re-layouts, chunk_gradient(): lax.all_to_all(spectrum, 'slab', split_axis=1, concat_axis=2, tiled=True)  57.9 us
  transfers between devices with their start and end apart: 10, of which 10 were waited for; matrix products, arithmetic and copies ran while one was open for 29% of the time, Pallas kernels for 0%

profile of v2, /device:TPU:0, one launch (start us, length us, event | category | flops | bytes accessed | tf_op | source)
XLA Modules:
  0.0 1387.0 jit_solution(7721470221482170204)
XLA Ops:
  20.9 9.0 slice_negate_fusion.2
  40.8 14.6 %copy_convert_fusion = f32[4,320,32,128]{3,1,2,0:T(8,128)} fusion(bf16[4,320,32,128]{3,2,1,0:T(8,128)(2,1)} %param.5), kind=kLoop, calls=%fused_computation.96 | loop fusion | flops 5242880 | bytes 31457280 | tf_op jit(solution)/shard_map/convert_element_type | solution.py:90
  55.4 30.7 %fusion.211 = (f32[4,320,32,64]{3,1,2,0:T(8,128)}, f32[4,320,32,64]{3,1,2,0:T(8,128)}) fusion(f32[4,320,32,128]{3,1,2,0:T(8,128)} %copy_convert_fusion), kind=kLoop, calls=%fused_computation.241 | loop fusion | bytes 41943040 | tf_op jit(solution)/shard_map/slice | solution.py:32
  86.1 50.6 %add_convert_fusion = (bf16[2,320,32,128]{3,1,2,0:T(8,128)(2,1)}, f32[2,320,32,128]{3,1,2,0:T(8,128)}, f32[2,320,32,128]{3,1,2,0:T(8,128)}, bf16[2,320,32,128]{3...) fusion(f32[320,32,128]{2,0,1:T(8,128)} %copy.161, f32[320,32,128]{2,0,1:T(8,128)} %copy.160, ...), kind=kLoop, calls=%fused_computation.97 | loop fusion | flops 31457280 | bytes 83886080 | tf_op jit(solution)/shard_map/convert_element_type | solution.py:45
  136.7 9.9 slice_negate_fusion
  185.9 21.0 %add_convert_fusion.2 = (bf16[2,320,32,128]{3,1,2,0:T(8,128)(2,1)}, bf16[2,320,32,128]{3,1,2,0:T(8,128)(2,1)}) fusion(f32[2,320,32,128]{3,1,2,0:T(8,128)} %get-tuple-element.11, f32[2,320,32,128]{3,1,2,0:T(8,128)} %get-tuple-element.10, f32[320,32,128]{2,0,1:T(8,128)} %copy.131, f32[320,32,128]{2,0,1:T(8,128)S(1)} %copy-done.5, ...), kind=kLoop, calls=%fused_computation.99 | loop fusion | flops 20971520 | bytes 62914560 | tf_op jit(solution)/shard_map/convert_element_type | solution.py:45
  206.9 9.9 slice_negate_fusion.3
  231.2 53.0 %all-to-all-done.6 = bf16[2,320,32,128]{3,2,0,1:T(8,128)(2,1)} async-done(((bf16[2,320,32,128]{3,2,0,1:T(8,128)(2,1)}), bf16[2,320,32,128]{3,2,0,1:T(8,128)(2,1)}, u32[]{:S(2)}, u32[]{:S(2)}) %all-to-all-start.6) | async-done | bytes 5242912 | tf_op jit(solution)/shard_map/all_to_all | solution.py:49
  289.3 9.9 slice_negate_fusion.1
  313.6 90.6 %all-to-all-done.2 = bf16[2,320,32,128]{3,2,0,1:T(8,128)(2,1)} async-done(((bf16[2,320,32,128]{3,2,0,1:T(8,128)(2,1)}), bf16[2,320,32,128]{3,2,0,1:T(8,128)(2,1)}, u32[]{:S(2)}, u32[]{:S(2)}) %all-to-all-start.2) | async-done | bytes 5242912 | tf_op jit(solution)/shard_map/all_to_all | solution.py:49
  409.1 10.1 slice_negate_fusion.4
  433.5 90.4 %all-to-all-done.4 = bf16[2,320,32,128]{3,2,0,1:T(8,128)(2,1)} async-done(((bf16[2,320,32,128]{3,2,0,1:T(8,128)(2,1)}), bf16[2,320,32,128]{3,2,0,1:T(8,128)(2,1)}, u32[]{:S(2)}, u32[]{:S(2)}) %all-to-all-start.4) | async-done | bytes 5242912 | tf_op jit(solution)/shard_map/all_to_all | solution.py:49
  582.8 13.8 copy.183
  596.6 47.2 %all-to-all-done = bf16[2,320,32,128]{3,2,0,1:T(8,128)(2,1)} async-done(((bf16[2,320,32,128]{3,2,0,1:T(8,128)(2,1)}), bf16[2,320,32,128]{3,2,0,1:T(8,128)(2,1)}, u32[]{:S(2)}, u32[]{:S(2)}) %all-to-all-start) | async-done | bytes 5242912 | tf_op jit(solution)/shard_map/all_to_all | solution.py:49
  693.4 13.7 copy.153
  707.1 56.5 %all-to-all-done.7 = bf16[2,40,256,128]{3,0,1,2:T(2,128)(2,1)} async-done(((bf16[2,40,256,128]{3,0,1,2:T(2,128)(2,1)}), bf16[2,40,256,128]{3,0,1,2:T(2,128)(2,1)}, u32[]{:S(2)}, u32[]{:S(2)}) %all-to-all-start.7) | async-done | bytes 5242912 | tf_op jit(solution)/shard_map/all_to_all | solution.py:71
  806.5 13.8 copy.169
  820.2 62.9 %all-to-all-done.3 = bf16[2,40,256,128]{3,0,1,2:T(2,128)(2,1)} async-done(((bf16[2,40,256,128]{3,0,1,2:T(2,128)(2,1)}), bf16[2,40,256,128]{3,0,1,2:T(2,128)(2,1)}, u32[]{:S(2)}, u32[]{:S(2)}) %all-to-all-start.3) | async-done | bytes 5242912 | tf_op jit(solution)/shard_map/all_to_all | solution.py:71
  926.6 13.7 copy.139
  940.3 62.9 %all-to-all-done.5 = bf16[2,40,256,128]{3,0,1,2:T(2,128)(2,1)} async-done(((bf16[2,40,256,128]{3,0,1,2:T(2,128)(2,1)}), bf16[2,40,256,128]{3,0,1,2:T(2,128)(2,1)}, u32[]{:S(2)}, u32[]{:S(2)}) %all-to-all-start.5) | async-done | bytes 5242912 | tf_op jit(solution)/shard_map/all_to_all | solution.py:71
  1015.4 8.8 copy.188
  1047.8 8.7 copy.174
  1068.5 54.3 %all-to-all-done.1 = bf16[2,40,256,128]{3,0,1,2:T(2,128)(2,1)} async-done(((bf16[2,40,256,128]{3,0,1,2:T(2,128)(2,1)}), bf16[2,40,256,128]{3,0,1,2:T(2,128)(2,1)}, u32[]{:S(2)}, u32[]{:S(2)}) %all-to-all-start.1) | async-done | bytes 5242912 | tf_op jit(solution)/shard_map/all_to_all | solution.py:71
  1130.2 8.7 copy.144
  1144.9 17.8 %fusion.82 = f32[2,640,32,128]{3,1,2,0:T(8,128)} fusion(bf16[2,320,32,64]{1,3,2,0:T(8,128)(2,1)} %get-tuple-element.27, bf16[2,320,32,64]{1,3,2,0:T(8,128)(2,1)} %get-tuple-element.26, bf16[2,320,32,128]{1,3,2,0:T(8,128)(2,1)} %copy.188, bf16[320,320]{1,0:T(8,128)(2,1)} %copy-done.20, bf16[320,320]{1,0:T(8,128)(2,1)} %copy-done.21, ...), kind=kOutput, calls=%fused_computation.101 | convolution fusion | flops 6745620480 | bytes 32071680 | tf_op jit(solution)/shard_map/yk,ckzl->cyzl/dot_general | solution.py:72
  1162.7 17.7 %fusion.88 = f32[2,640,32,128]{3,1,2,0:T(8,128)} fusion(bf16[2,320,32,64]{1,3,2,0:T(8,128)(2,1)} %get-tuple-element.29, bf16[2,320,32,64]{1,3,2,0:T(8,128)(2,1)} %get-tuple-element.28, bf16[2,320,32,128]{1,3,2,0:T(8,128)(2,1)} %copy.158, bf16[320,320]{1,0:T(8,128)(2,1)} %copy-done.20, bf16[320,320]{1,0:T(8,128)(2,1)} %copy-done.21, ...), kind=kOutput, calls=%fused_computation.103 | convolution fusion | flops 6745620480 | bytes 32071680 | tf_op jit(solution)/shard_map/yk,ckzl->cyzl/dot_general | solution.py:72
  1180.4 25.5 %fusion.7 = (f32[320,32,128]{2,0,1:T(8,128)}, f32[320,32,128]{2,0,1:T(8,128)}) fusion(f32[2,320,32,128]{3,1,2,0:T(8,128)} %get-tuple-element.11, f32[2,640,32,128]{3,1,2,0:T(8,128)} %fusion.88, f32[2,320,32,128]{3,1,2,0:T(8,128)} %get-tuple-element.10, f32[2,640,32,128]{3,1,2,0:T(8,128)} %fusion.82), kind=kLoop, calls=%fused_computation.16 | loop fusion | flops 18350080 | bytes 73400320 | tf_op jit(solution)/shard_map/reduce_sum | solution.py:77
  1205.9 17.1 %fusion.85 = f32[2,640,32,128]{3,1,2,0:T(8,128)} fusion(bf16[2,320,32,64]{1,3,2,0:T(8,128)(2,1)} %get-tuple-element.31, bf16[2,320,32,64]{1,3,2,0:T(8,128)(2,1)S(1)} %get-tuple-element.30, bf16[2,320,32,128]{1,3,2,0:T(8,128)(2,1)} %copy.174, bf16[320,320]{1,0:T(8,128)(2,1)} %copy-done.20, bf16[320,320]{1,0:T(8,128)(2,1)} %copy-done.21, ...), kind=kOutput, calls=%fused_computation.102 | convolution fusion | flops 6745620480 | bytes 32071680 | tf_op jit(solution)/shard_map/yk,ckzl->cyzl/dot_general | solution.py:72
  1223.0 17.8 %fusion.91 = f32[2,640,32,128]{3,1,2,0:T(8,128)} fusion(bf16[2,320,32,64]{1,3,2,0:T(8,128)(2,1)} %get-tuple-element.33, bf16[2,320,32,64]{1,3,2,0:T(8,128)(2,1)} %get-tuple-element.32, bf16[2,320,32,128]{1,3,2,0:T(8,128)(2,1)} %copy.144, bf16[320,320]{1,0:T(8,128)(2,1)} %copy-done.20, bf16[320,320]{1,0:T(8,128)(2,1)} %copy-done.21, ...), kind=kOutput, calls=%fused_computation.104 | convolution fusion | flops 6745620480 | bytes 32071680 | tf_op jit(solution)/shard_map/yk,ckzl->cyzl/dot_general | solution.py:72
  1240.7 25.9 %fusion.9 = (f32[320,32,128]{2,0,1:T(8,128)}, f32[320,32,128]{2,0,1:T(8,128)}) fusion(f32[2,320,32,128]{3,1,2,0:T(8,128)} %get-tuple-element.16, f32[2,640,32,128]{3,1,2,0:T(8,128)} %fusion.91, f32[2,320,32,128]{3,1,2,0:T(8,128)} %get-tuple-element.17, f32[2,640,32,128]{3,1,2,0:T(8,128)} %fusion.85), kind=kLoop, calls=%fused_computation.22 | loop fusion | flops 18350080 | bytes 73400320 | tf_op jit(solution)/shard_map/reduce_sum | solution.py:77
  1279.4 43.3 %reduce-scatter.3.cloned.1.call-done = f32[80,32,128]{2,0,1:T(8,128)} async-done(((f32[320,32,128]{2,0,1:T(8,128)}), f32[80,32,128]{2,0,1:T(8,128)}) %reduce-scatter.3.cloned.1.call-update) | async-done | bytes 1310736 | tf_op jit(solution)/shard_map/reduce_scatter | solution.py:106
  1324.1 52.7 %reduce-scatter.5.cloned.1.call-done = f32[80,32,128]{2,0,1:T(8,128)} async-done(((f32[320,32,128]{2,0,1:T(8,128)}), f32[80,32,128]{2,0,1:T(8,128)}) %reduce-scatter.5.cloned.1.call-update) | async-done | bytes 1310736 | tf_op jit(solution)/shard_map/reduce_scatter | solution.py:106
  (151 shorter events, 390.4 us)
Async XLA Ops:
  9.4 409.7 %copy-start.20 = (bf16[320,320]{1,0:T(8,128)(2,1)}, bf16[320,320]{1,0:T(8,128)(2,1)S(1)}, u32[]{:S(2)}) copy-start(bf16[320,320]{1,0:T(8,128)(2,1)S(1)} %get-tuple-element.75) | copy-start | bytes 614404
  11.4 407.8 %copy-start.21 = (bf16[320,320]{1,0:T(8,128)(2,1)}, bf16[320,320]{1,0:T(8,128)(2,1)S(1)}, u32[]{:S(2)}) copy-start(bf16[320,320]{1,0:T(8,128)(2,1)S(1)} %fusion.190) | copy-start | bytes 614404
  15.5 5.4 copy-start
  160.9 15.7 %slice-start.6 = ((s8[5242880]{0:T(1024)(128)(4,1)}), s8[1048576]{0:T(1024)(128)(4,1)S(1)}, s32[]{:S(2)}) async-start(s8[5242880]{0:T(1024)(128)(4,1)} %bitcast.162), calls=%async_computation.18 | async-start | bytes 2097152
  160.9 123.3 %all-to-all-start.6 = ((bf16[2,320,32,128]{3,2,0,1:T(8,128)(2,1)}), bf16[2,320,32,128]{3,2,0,1:T(8,128)(2,1)}, u32[]{:S(2)}, u32[]{:S(2)}) async-start(bf16[2,320,32,128]{3,2,0,1:T(8,128)(2,1)} %copy.176), calls=%async_computation.7 | async-start | bytes 10485760 | tf_op jit(solution)/shard_map/all_to_all | solution.py:49
  168.5 8.0 slice-start.7
  180.5 5.4 copy-start.5
  284.2 120.0 %all-to-all-start.2 = ((bf16[2,320,32,128]{3,2,0,1:T(8,128)(2,1)}), bf16[2,320,32,128]{3,2,0,1:T(8,128)(2,1)}, u32[]{:S(2)}, u32[]{:S(2)}) async-start(bf16[2,320,32,128]{3,2,0,1:T(8,128)(2,1)} %copy.146), calls=%async_computation.2 | async-start | bytes 10485760 | tf_op jit(solution)/shard_map/all_to_all | solution.py:49
  404.2 119.7 %all-to-all-start.4 = ((bf16[2,320,32,128]{3,2,0,1:T(8,128)(2,1)}), bf16[2,320,32,128]{3,2,0,1:T(8,128)(2,1)}, u32[]{:S(2)}, u32[]{:S(2)}) async-start(bf16[2,320,32,128]{3,2,0,1:T(8,128)(2,1)} %copy.162), calls=%async_computation.5 | async-start | bytes 10485760 | tf_op jit(solution)/shard_map/all_to_all | solution.py:49
  524.0 119.8 %all-to-all-start = ((bf16[2,320,32,128]{3,2,0,1:T(8,128)(2,1)}), bf16[2,320,32,128]{3,2,0,1:T(8,128)(2,1)}, u32[]{:S(2)}, u32[]{:S(2)}) async-start(bf16[2,320,32,128]{3,2,0,1:T(8,128)(2,1)} %copy.132), calls=%async_computation | async-start | bytes 10485760 | tf_op jit(solution)/shard_map/all_to_all | solution.py:49
  536.0 4.6 copy-start.22
  543.1 4.1 copy-start.9
  561.6 5.3 copy-start.3
  596.6 52.1 %copy-start.8 = (bf16[1,2,40,128,128]{4,3,2,1,0:T(8,128)(2,1)S(1)}, bf16[1,2,40,128,128]{4,3,2,1,0:T(8,128)(2,1)}, u32[]{:S(2)}) copy-start(bf16[1,2,40,128,128]{4,3,2,1,0:T(8,128)(2,1)} %get-tuple-element.22) | copy-start | bytes 7864324
  643.7 119.8 %all-to-all-start.7 = ((bf16[2,40,256,128]{3,0,1,2:T(2,128)(2,1)}), bf16[2,40,256,128]{3,0,1,2:T(2,128)(2,1)}, u32[]{:S(2)}, u32[]{:S(2)}) async-start(bf16[2,40,256,128]{3,0,1,2:T(2,128)(2,1)} %copy.183), calls=%async_computation.8 | async-start | bytes 10485760 | tf_op jit(solution)/shard_map/all_to_all | solution.py:71
  653.8 3.9 copy-start.10
  672.2 5.4 copy-start.4
  707.1 61.1 %copy-start.7 = (bf16[1,2,40,128,128]{4,3,2,1,0:T(8,128)(2,1)S(1)}, bf16[1,2,40,128,128]{4,3,2,1,0:T(8,128)(2,1)}, u32[]{:S(2)}) copy-start(bf16[1,2,40,128,128]{4,3,2,1,0:T(8,128)(2,1)} %get-tuple-element.21) | copy-start | bytes 7864324
  763.6 119.6 %all-to-all-start.3 = ((bf16[2,40,256,128]{3,0,1,2:T(2,128)(2,1)}), bf16[2,40,256,128]{3,0,1,2:T(2,128)(2,1)}, u32[]{:S(2)}, u32[]{:S(2)}) async-start(bf16[2,40,256,128]{3,0,1,2:T(2,128)(2,1)} %copy.153), calls=%async_computation.3 | async-start | bytes 10485760 | tf_op jit(solution)/shard_map/all_to_all | solution.py:71
  785.4 5.3 copy-start.1
  820.2 68.0 %copy-start.6 = (bf16[1,2,40,128,128]{4,3,2,1,0:T(8,128)(2,1)S(1)}, bf16[1,2,40,128,128]{4,3,2,1,0:T(8,128)(2,1)}, u32[]{:S(2)}) copy-start(bf16[1,2,40,128,128]{4,3,2,1,0:T(8,128)(2,1)} %get-tuple-element.23) | copy-start | bytes 7864324
  883.1 120.0 %all-to-all-start.5 = ((bf16[2,40,256,128]{3,0,1,2:T(2,128)(2,1)}), bf16[2,40,256,128]{3,0,1,2:T(2,128)(2,1)}, u32[]{:S(2)}, u32[]{:S(2)}) async-start(bf16[2,40,256,128]{3,0,1,2:T(2,128)(2,1)} %copy.169), calls=%async_computation.6 | async-start | bytes 10485760 | tf_op jit(solution)/shard_map/all_to_all | solution.py:71
  905.3 5.4 copy-start.2
  1003.2 119.6 %all-to-all-start.1 = ((bf16[2,40,256,128]{3,0,1,2:T(2,128)(2,1)}), bf16[2,40,256,128]{3,0,1,2:T(2,128)(2,1)}, u32[]{:S(2)}, u32[]{:S(2)}) async-start(bf16[2,40,256,128]{3,0,1,2:T(2,128)(2,1)} %copy.139), calls=%async_computation.1 | async-start | bytes 10485760 | tf_op jit(solution)/shard_map/all_to_all | solution.py:71
  1007.8 314.9 %reduce-scatter.3.cloned.1.call-start = ((), (), s32[]{:S(2)}) async-start(), calls=%async_computation.10 | async-start | bytes 6553600 | tf_op jit(solution)/shard_map/reduce_scatter | solution.py:106
  1047.8 15.3 %slice-start.2 = ((s8[6291456]{0:T(1024)(128)(4,1)}), s8[2097152]{0:T(1024)(128)(4,1)S(1)}, s32[]{:S(2)}) async-start(s8[6291456]{0:T(1024)(128)(4,1)} %bitcast.158), calls=%async_computation.14 | async-start | bytes 4194304
  1056.5 6.6 slice-start.3
  1056.5 9.7 slice-start
  1138.9 6.1 copy-start.19
  1223.0 43.6 %slice-start.4 = ((s8[5242880]{0:T(1024)(128)(4,1)}), s8[1048576]{0:T(1024)(128)(4,1)S(1)}, s32[]{:S(2)}) async-start(s8[5242880]{0:T(1024)(128)(4,1)} %bitcast.160), calls=%async_computation.16 | async-start | bytes 2097152
  1240.7 25.9 %slice-start.5 = ((s8[5242880]{0:T(1024)(128)(4,1)}), s8[4194304]{0:T(1024)(128)(4,1)S(1)}, s32[]{:S(2)}) async-start(s8[5242880]{0:T(1024)(128)(4,1)} %bitcast.160), calls=%async_computation.17 | async-start | bytes 8388608
  1272.1 104.7 %reduce-scatter.5.cloned.1.call-start = ((), (), s32[]{:S(2)}) async-start(), calls=%async_computation.11 | async-start | bytes 6553600 | tf_op jit(solution)/shard_map/reduce_scatter | solution.py:106
  (9 other events, 26.6 us)
Sparse Core Ops, SparseCore 0:
  1272.3 50.4 reduce-scatter.2
  1325.4 51.3 reduce-scatter.4

commit v3 on v2

--- a/solution.py
+++ b/solution.py
@@ -40,13 +40,14 @@
     return jnp.concatenate([values, turned(values)], axis=axis)
 
 
-def chunk_gradient(pixels, sens_real, sens_imag, measured, kz_lines, y_fwd, y_back):
-    y_count = pixels.shape[0]
+def forward_y(pixels, sens_real, sens_imag, y_fwd):
     coil_image = (sens_real * pixels + sens_imag * turned(pixels)).astype(BF16)
-    spectrum = jnp.einsum(
+    return jnp.einsum(
         "ky,cyzl->ckzl", y_fwd, with_turned(coil_image, 1), preferred_element_type=F32
     ).astype(BF16)
-    gathered = lax.all_to_all(spectrum, "slab", split_axis=1, concat_axis=2, tiled=True)
+
+
+def middle_z(gathered, measured, kz_lines):
     z_count = gathered.shape[2]
     z_cos, z_sin = cos_sin(z_count)
     sampled = kz_lines >= 0
@@ -62,19 +63,34 @@
     residual = jnp.where(
         sampled[None, :, :, None], kspace - measured.astype(F32), F32(0.0)
     ).astype(BF16)
-    rows_back = jnp.concatenate(
-        [rows_fwd[..., :z_count], -rows_fwd[..., z_count:]], axis=1
-    )
-    adjoint_z = jnp.einsum(
+    rows_back = jnp.concatenate([rows_fwd[..., :z_count], -rows_fwd[..., z_count:]], axis=1)
+    return jnp.einsum(
         "kjz,ckjl->ckzl", rows_back, with_turned(residual, 2), preferred_element_type=F32
     ).astype(BF16)
-    returned = lax.all_to_all(adjoint_z, "slab", split_axis=2, concat_axis=1, tiled=True)
+
+
+def backward_y(returned, sens_real, sens_imag, y_back):
+    y_count = returned.shape[1]
     both = jnp.einsum(
         "yk,ckzl->cyzl", y_back, with_turned(returned, 1), preferred_element_type=F32
     )
     coil_back = both[:, :y_count]
     turned_back = both[:, y_count:]
     return jnp.sum(sens_real * coil_back - sens_imag * turned_back, axis=0)
+
+
+def to_ky_blocks(values):
+    return lax.all_to_all(values, "slab", split_axis=1, concat_axis=2, tiled=True)
+
+
+def to_z_slabs(values):
+    return lax.all_to_all(values, "slab", split_axis=2, concat_axis=1, tiled=True)
+
+
+def after(value, *others):
+    if not others:
+        return value
+    return lax.optimization_barrier((value,) + tuple(others))[0]
 
 
 def shards(image, coil_maps, y_data, kz_lines):
@@ -88,21 +104,51 @@
         axis=0,
     )
     sens_real, sens_imag = dup_halves(coil_maps.astype(F32))
+    chunks = [(state, first) for state in range(state_count) for first in range(0, coil_count, group)]
+    count = len(chunks)
+
+    def sens_of(index):
+        first = chunks[index][1]
+        return sens_real[first : first + group], sens_imag[first : first + group]
+
+    def forward(index):
+        state = chunks[index][0]
+        return forward_y(image[state].astype(F32), *sens_of(index), y_fwd)
+
+    def middle(index, gathered):
+        state, first = chunks[index]
+        return middle_z(gathered, y_data[state, first : first + group], kz_lines[state])
+
+    def backward(index, returned):
+        return backward_y(returned, *sens_of(index), y_back)
+
+    gathered = {0: to_ky_blocks(forward(0))}
+    returned = {}
+    partials = {}
+    for step in range(1, count + 1):
+        if step >= 2:
+            partials[step - 2] = backward(step - 2, returned[step - 2])
+        if step < count:
+            spectrum = forward(step)
+            if step >= 2:
+                spectrum = after(spectrum, returned[step - 2])
+            gathered[step] = to_ky_blocks(spectrum)
+        adjoint_z = middle(step - 1, gathered[step - 1])
+        holds = []
+        if step < count:
+            holds.append(gathered[step])
+            if step >= 2:
+                holds.append(partials[step - 2])
+        elif step >= 2:
+            holds.append(returned[step - 2])
+        returned[step - 1] = to_z_slabs(after(adjoint_z, *holds))
+    partials[count - 1] = backward(count - 1, returned[count - 1])
     outputs = []
     for state in range(state_count):
-        pixels = image[state].astype(F32)
         total = None
-        for first in range(0, coil_count, group):
-            part = chunk_gradient(
-                pixels,
-                sens_real[first : first + group],
-                sens_imag[first : first + group],
-                y_data[state, first : first + group],
-                kz_lines[state],
-                y_fwd,
-                y_back,
-            )
-            total = part if total is None else total + part
+        for index in range(count):
+            if chunks[index][0] == state:
+                total = partials[index] if total is None else total + partials[index]
         summed = lax.psum_scatter(total, "coil", scatter_dimension=0, tiled=True)
         outputs.append(summed.astype(BF16))
     return jnp.stack(outputs)

time: 1400 us -> 1490 us (1.064)
  blocking collectives: 0 us -> 120 us
  waiting for transfers between devices: 614 us -> 576 us
  other arithmetic: 276 us -> 293 us
    all_to_all x0 -> x1, blocking collectives: none -> 120 us  [to_z_slabs(): lax.all_to_all(values, 'slab', split_axis=2, concat_axis=1, tiled=True)]
    optimization_barrier x0 -> x6, local copies, waits for them, and re-layouts: none -> 66.5 us  [after(): return lax.optimization_barrier((value,) + tuple(others))[0]]
    convert_element_type x8 -> x2, local copies, waits for them, and re-layouts: 77.7 us -> 11.4 us  [forward_y(): return jnp.einsum('ky,cyzl->ckzl', y_fwd, with_turned(coil_image, 1), pre...]
    reduce_scatter x2, waiting for transfers between devices: 96 us -> 49.2 us  [shards(): summed = lax.psum_scatter(total, 'coil', scatter_dimension=0, tiled=True)]
    reduce_sum x2 -> x4, other arithmetic: 51.4 us -> 73.4 us  [backward_y(): return jnp.sum(sens_real * coil_back - sens_imag * turned_back, axis=0)]
    all_to_all x8 -> x7, waiting for transfers between devices: 518 us -> 527 us  [the longest x4 291 us: to_ky_blocks(): lax.all_to_all(values, 'slab', split_axis=1, concat_axis=2, tiled=True)]
    all_to_all x8 -> x7, starting transfers between devices: 41.8 us -> 37.1 us  [the longest x4 22.4 us: to_ky_blocks(): lax.all_to_all(values, 'slab', split_axis=1, concat_axis=2, tiled=True)]
  transfers between devices with their start and end apart: 10 -> 9, of which waited for: 10 -> 8; matrix products, arithmetic and copies ran while one was open for 29% -> 22% of each run, Pallas kernels for 0% -> 0%
where the time goes in v3:
time: 1490 us; the launch traced here: 1480 us
  waiting for transfers between devices  576 us (39%)
  other arithmetic  293 us (20%)
  local copies, waits for them, and re-layouts  277 us (19%)
  matrix products  159 us (11%)
  blocking collectives  120 us (8%)
  starting transfers between devices  37.2 us (2%)
    all_to_all x4, waiting for transfers between devices, to_ky_blocks(): lax.all_to_all(values, 'slab', split_axis=1, concat_axis=2, tiled=True)  291 us
    all_to_all x3, waiting for transfers between devices, to_z_slabs(): lax.all_to_all(values, 'slab', split_axis=2, concat_axis=1, tiled=True)  236 us
    all_to_all x1, blocking collectives, to_z_slabs(): lax.all_to_all(values, 'slab', split_axis=2, concat_axis=1, tiled=True)  120 us
    neg x17, other arithmetic, turned(): return jnp.concatenate([-values[..., half:], values[..., :half]], axis=-1)  100 us
    reduce_sum x4, other arithmetic, backward_y(): return jnp.sum(sens_real * coil_back - sens_imag * turned_back, axis=0)  73.4 us
    dot_general x4, matrix products, backward_y(): jnp.einsum('yk,ckzl->cyzl', y_back, with_turned(returned, 1), preferred_e...  67.8 us
    optimization_barrier x6, local copies, waits for them, and re-layouts, after(): return lax.optimization_barrier((value,) + tuple(others))[0]  66.5 us
    convert_element_type x2, other arithmetic, forward_y(): coil_image = (sens_real * pixels + sens_imag * turned(pixels)).astype(BF16)  65.7 us
  transfers between devices with their start and end apart: 9, of which 8 were waited for; matrix products, arithmetic and copies ran while one was open for 22% of the time, Pallas kernels for 0%

profile of v3, /device:TPU:0, one launch (start us, length us, event | category | flops | bytes accessed | tf_op | source)
XLA Modules:
  0.0 1477.0 jit_solution(10957178758233238264)
XLA Ops:
  15.9 9.0 slice_negate_fusion.2
  51.8 14.7 copy_convert_fusion
  66.6 30.7 %fusion.211 = (f32[4,320,32,64]{3,1,2,0:T(8,128)}, f32[4,320,32,64]{3,1,2,0:T(8,128)}) fusion(f32[4,320,32,128]{3,1,2,0:T(8,128)} %copy_convert_fusion), kind=kLoop, calls=%fused_computation.241 | loop fusion | bytes 41943040 | tf_op jit(solution)/shard_map/slice | solution.py:32
  97.3 52.0 %add_convert_fusion = (bf16[2,320,32,128]{3,1,2,0:T(8,128)(2,1)}, f32[2,320,32,128]{3,1,2,0:T(8,128)}, f32[2,320,32,128]{3,1,2,0:T(8,128)}, bf16[2,320,32,128]{3...) fusion(f32[320,32,128]{2,0,1:T(8,128)} %copy.154, f32[320,32,128]{2,0,1:T(8,128)} %copy.153, ...), kind=kLoop, calls=%fused_computation.97 | loop fusion | flops 31457280 | bytes 94371840 | tf_op jit(solution)/shard_map/convert_element_type | solution.py:44
  149.3 13.7 add_convert_fusion.2
  163.0 10.0 slice_negate_fusion.3
  194.9 10.1 slice_negate_fusion.4
  219.3 91.3 %all-to-all-done.1 = bf16[2,320,32,128]{3,2,0,1:T(8,128)(2,1)} async-done(((bf16[2,320,32,128]{3,2,0,1:T(8,128)(2,1)}), bf16[2,320,32,128]{3,2,0,1:T(8,128)(2,1)}, u32[]{:S(2)}, u32[]{:S(2)}) %all-to-all-start.1) | async-done | bytes 5242912 | tf_op jit(solution)/shard_map/all_to_all | solution.py:83
  341.5 89.2 %all-to-all-done = bf16[2,320,32,128]{3,2,0,1:T(8,128)(2,1)} async-done(((bf16[2,320,32,128]{3,2,0,1:T(8,128)(2,1)}), bf16[2,320,32,128]{3,2,0,1:T(8,128)(2,1)}, u32[]{:S(2)}, u32[]{:S(2)}) %all-to-all-start) | async-done | bytes 5242912 | tf_op jit(solution)/shard_map/all_to_all | solution.py:83
  466.3 13.8 copy.142
  480.1 119.6 %all_to_all.144 = bf16[2,40,256,128]{3,0,1,2:T(2,128)(2,1)S(1)} all-to-all(bf16[2,40,256,128]{3,0,1,2:T(2,128)(2,1)} %copy.142), channel_id=1, replica_groups=mesh['slab'=8,'coil'=4] {'slab'}, dimensions={2} | all-to-all | bytes 10485760 | tf_op jit(solution)/shard_map/all_to_all | solution.py:87
  618.3 17.0 %fusion.91 = f32[2,640,32,128]{3,1,2,0:T(8,128)} fusion(bf16[2,320,32,64]{1,3,2,0:T(8,128)(2,1)} %get-tuple-element.41, bf16[2,320,32,64]{1,3,2,0:T(8,128)(2,1)S(1)} %get-tuple-element.40, bf16[2,320,32,128]{1,3,2,0:T(8,128)(2,1)} %copy.147, bf16[320,320]{1,0:T(8,128)(2,1)} %copy-done.20, bf16[320,320]{1,0:T(8,128)(2,1)} %copy-done.22, ...), kind=kOutput, calls=%fused_computation.104 | convolution fusion | flops 6745620480 | bytes 32071680 | tf_op jit(solution)/shard_map/yk,ckzl->cyzl/dot_general | solution.py:74
  635.3 23.0 %fusion.9 = (f32[320,32,128]{2,0,1:T(8,128)}, bf16[2,320,32,128]{3,1,2,0:T(8,128)(2,1)}) fusion(f32[2,320,32,128]{3,1,2,0:T(8,128)} %get-tuple-element.24, f32[2,640,32,128]{3,1,2,0:T(8,128)} %fusion.91, f32[2,320,32,128]{3,1,2,0:T(8,128)} %get-tuple-element.25, f32[320,32,128]{2,0,1:T(8,128)} %copy.154, f32[320,32,128]{2,0,1:T(8,128)} %copy.153), kind=kLoop, calls=%fused_computation.20 | loop fusion | flops 19660800 | bytes 62914560 | tf_op jit(solution)/shard_map/reduce_sum | solution.py:79
  658.3 10.0 slice_negate_fusion.1
  719.4 83.0 %all-to-all-done.3 = bf16[2,320,32,128]{3,2,0,1:T(8,128)(2,1)} async-done(((bf16[2,320,32,128]{3,2,0,1:T(8,128)(2,1)}), bf16[2,320,32,128]{3,2,0,1:T(8,128)(2,1)}, u32[]{:S(2)}, u32[]{:S(2)}) %all-to-all-start.3) | async-done | bytes 5242912 | tf_op jit(solution)/shard_map/all_to_all | solution.py:83
  808.8 13.7 copy.158
  827.6 10.0 slice_negate_fusion
  837.6 10.1 convert_bitcast_fusion.1
  847.7 94.8 %all-to-all-done.4 = bf16[2,40,256,128]{3,0,1,2:T(2,128)(2,1)} async-done(((bf16[2,40,256,128]{3,0,1,2:T(2,128)(2,1)}), bf16[2,40,256,128]{3,0,1,2:T(2,128)(2,1)}, u32[]{:S(2)}, u32[]{:S(2)}) %all-to-all-start.4) | async-done | bytes 5242912 | tf_op jit(solution)/shard_map/all_to_all | solution.py:87
  1013.9 17.0 %fusion.88 = f32[2,640,32,128]{3,1,2,0:T(8,128)} fusion(bf16[2,320,32,64]{1,3,2,0:T(8,128)(2,1)} %get-tuple-element.39, bf16[2,320,32,64]{1,3,2,0:T(8,128)(2,1)S(1)} %get-tuple-element.38, bf16[2,320,32,128]{1,3,2,0:T(8,128)(2,1)} %copy.163, bf16[320,320]{1,0:T(8,128)(2,1)} %copy-done.20, bf16[320,320]{1,0:T(8,128)(2,1)} %copy-done.22, ...), kind=kOutput, calls=%fused_computation.103 | convolution fusion | flops 6745620480 | bytes 32071680 | tf_op jit(solution)/shard_map/yk,ckzl->cyzl/dot_general | solution.py:74
  1030.9 17.4 %fusion.7 = f32[320,32,128]{2,0,1:T(8,128)} fusion(f32[2,320,32,128]{3,1,2,0:T(8,128)} %get-tuple-element.19, f32[2,640,32,128]{3,1,2,0:T(8,128)} %fusion.88, f32[2,320,32,128]{3,1,2,0:T(8,128)} %get-tuple-element.18), kind=kLoop, calls=%fused_computation.16 | loop fusion | flops 9175040 | bytes 47185920 | tf_op jit(solution)/shard_map/reduce_sum | solution.py:79
  1048.3 27.6 %all-to-all-done.5 = bf16[2,320,32,128]{3,2,0,1:T(8,128)(2,1)} async-done(((bf16[2,320,32,128]{3,2,0,1:T(8,128)(2,1)}), bf16[2,320,32,128]{3,2,0,1:T(8,128)(2,1)}, u32[]{:S(2)}, u32[]{:S(2)}) %all-to-all-start.5) | async-done | bytes 5242912 | tf_op jit(solution)/shard_map/all_to_all | solution.py:83
  1082.4 13.8 copy.172
  1132.7 83.3 %all-to-all-done.6 = bf16[2,40,256,128]{3,0,1,2:T(2,128)(2,1)} async-done(((bf16[2,40,256,128]{3,0,1,2:T(2,128)(2,1)}), bf16[2,40,256,128]{3,0,1,2:T(2,128)(2,1)}, u32[]{:S(2)}, u32[]{:S(2)}) %all-to-all-start.6) | async-done | bytes 5242912 | tf_op jit(solution)/shard_map/all_to_all | solution.py:87
  1223.6 13.8 copy.183
  1249.4 9.3 copy.177
  1264.8 16.9 %fusion.85 = f32[2,640,32,128]{3,1,2,0:T(8,128)} fusion(bf16[2,320,32,64]{1,3,2,0:T(8,128)(2,1)} %get-tuple-element.37, bf16[2,320,32,64]{1,3,2,0:T(8,128)(2,1)S(1)} %get-tuple-element.36, bf16[2,320,32,128]{1,3,2,0:T(8,128)(2,1)} %copy.177, bf16[320,320]{1,0:T(8,128)(2,1)} %copy-done.20, bf16[320,320]{1,0:T(8,128)(2,1)} %copy-done.22, ...), kind=kOutput, calls=%fused_computation.102 | convolution fusion | flops 6745620480 | bytes 32071680 | tf_op jit(solution)/shard_map/yk,ckzl->cyzl/dot_general | solution.py:74
  1281.7 17.3 %fusion.5 = f32[320,32,128]{2,0,1:T(8,128)} fusion(f32[2,320,32,128]{3,1,2,0:T(8,128)} %get-tuple-element.24, f32[2,640,32,128]{3,1,2,0:T(8,128)} %fusion.85, f32[2,320,32,128]{3,1,2,0:T(8,128)} %get-tuple-element.25), kind=kLoop, calls=%fused_computation.12 | loop fusion | flops 9175040 | bytes 47185920 | tf_op jit(solution)/shard_map/reduce_sum | solution.py:79
  1299.0 57.9 %all-to-all-done.7 = bf16[2,40,256,128]{3,0,1,2:T(2,128)(2,1)} async-done(((bf16[2,40,256,128]{3,0,1,2:T(2,128)(2,1)}), bf16[2,40,256,128]{3,0,1,2:T(2,128)(2,1)}, u32[]{:S(2)}, u32[]{:S(2)}) %all-to-all-start.7) | async-done | bytes 5242912 | tf_op jit(solution)/shard_map/all_to_all | solution.py:87
  1378.1 16.9 %fusion.82 = f32[2,640,32,128]{3,1,2,0:T(8,128)} fusion(bf16[2,320,32,64]{1,3,2,0:T(8,128)(2,1)} %get-tuple-element.35, bf16[2,320,32,64]{1,3,2,0:T(8,128)(2,1)S(1)} %get-tuple-element.34, bf16[2,320,32,128]{1,3,2,0:T(8,128)(2,1)} %copy.188, bf16[320,320]{1,0:T(8,128)(2,1)} %copy-done.20, bf16[320,320]{1,0:T(8,128)(2,1)} %copy-done.22, ...), kind=kOutput, calls=%fused_computation.101 | convolution fusion | flops 6745620480 | bytes 32071680 | tf_op jit(solution)/shard_map/yk,ckzl->cyzl/dot_general | solution.py:74
  1395.0 15.7 %fusion.3 = f32[320,32,128]{2,0,1:T(8,128)S(1)} fusion(f32[2,320,32,128]{3,1,2,0:T(8,128)} %get-tuple-element.19, f32[2,640,32,128]{3,1,2,0:T(8,128)} %fusion.82, f32[2,320,32,128]{3,1,2,0:T(8,128)} %get-tuple-element.18), kind=kLoop, calls=%fused_computation.8 | loop fusion | flops 9175040 | bytes 47185920 | tf_op jit(solution)/shard_map/reduce_sum | solution.py:79
  1417.9 49.1 %reduce-scatter.5.cloned.1.call-done = f32[80,32,128]{2,0,1:T(8,128)} async-done(((f32[320,32,128]{2,0,1:T(8,128)}), f32[80,32,128]{2,0,1:T(8,128)}) %reduce-scatter.5.cloned.1.call-update) | async-done | bytes 1310736 | tf_op jit(solution)/shard_map/reduce_scatter | solution.py:152
  (163 shorter events, 391.3 us)
Async XLA Ops:
  24.9 10.7 copy-start
  30.2 14.8 slice-start
  30.2 14.8 slice-start.2
  33.1 171.9 %copy-start.20 = (bf16[320,320]{1,0:T(8,128)(2,1)}, bf16[320,320]{1,0:T(8,128)(2,1)S(1)}, u32[]{:S(2)}) copy-start(bf16[320,320]{1,0:T(8,128)(2,1)S(1)} %get-tuple-element.83) | copy-start | bytes 614404
  35.5 169.4 %copy-start.22 = (bf16[320,320]{1,0:T(8,128)(2,1)}, bf16[320,320]{1,0:T(8,128)(2,1)S(1)}, u32[]{:S(2)}) copy-start(bf16[320,320]{1,0:T(8,128)(2,1)S(1)} %fusion.190) | copy-start | bytes 614404
  35.5 9.4 slice-start.1
  35.5 9.4 slice-start.3
  187.6 123.0 %all-to-all-start.1 = ((bf16[2,320,32,128]{3,2,0,1:T(8,128)(2,1)}), bf16[2,320,32,128]{3,2,0,1:T(8,128)(2,1)}, u32[]{:S(2)}, u32[]{:S(2)}) async-start(bf16[2,320,32,128]{3,2,0,1:T(8,128)(2,1)} %copy.139), calls=%async_computation.1 | async-start | bytes 10485760 | tf_op jit(solution)/shard_map/all_to_all | solution.py:83
  310.6 120.0 %all-to-all-start = ((bf16[2,320,32,128]{3,2,0,1:T(8,128)(2,1)}), bf16[2,320,32,128]{3,2,0,1:T(8,128)(2,1)}, u32[]{:S(2)}, u32[]{:S(2)}) async-start(bf16[2,320,32,128]{3,2,0,1:T(8,128)(2,1)} %copy.132), calls=%async_computation | async-start | bytes 10485760 | tf_op jit(solution)/shard_map/all_to_all | solution.py:83
  322.8 4.6 copy-start.24
  331.1 4.0 copy-start.8
  445.0 5.4 copy-start.3
  613.2 5.1 copy-start.18
  658.3 10.0 copy-start.21
  658.3 10.0 copy-start.23
  682.7 4.9 copy-start.7
  682.7 119.6 %all-to-all-start.3 = ((bf16[2,320,32,128]{3,2,0,1:T(8,128)(2,1)}), bf16[2,320,32,128]{3,2,0,1:T(8,128)(2,1)}, u32[]{:S(2)}, u32[]{:S(2)}) async-start(bf16[2,320,32,128]{3,2,0,1:T(8,128)(2,1)} %copy.155), calls=%async_computation.3 | async-start | bytes 10485760 | tf_op jit(solution)/shard_map/all_to_all | solution.py:83
  698.2 5.3 copy-start.1
  711.4 3.3 copy-start.13
  822.5 120.0 %all-to-all-start.4 = ((bf16[2,40,256,128]{3,0,1,2:T(2,128)(2,1)}), bf16[2,40,256,128]{3,0,1,2:T(2,128)(2,1)}, u32[]{:S(2)}, u32[]{:S(2)}) async-start(bf16[2,40,256,128]{3,0,1,2:T(2,128)(2,1)} %copy.158), calls=%async_computation.4 | async-start | bytes 10485760 | tf_op jit(solution)/shard_map/all_to_all | solution.py:87
  942.5 7.7 slice-start.4
  946.5 3.7 slice-start.5
  955.9 5.2 copy-start.6
  955.9 120.0 %all-to-all-start.5 = ((bf16[2,320,32,128]{3,2,0,1:T(8,128)(2,1)}), bf16[2,320,32,128]{3,2,0,1:T(8,128)(2,1)}, u32[]{:S(2)}, u32[]{:S(2)}) async-start(bf16[2,320,32,128]{3,2,0,1:T(8,128)(2,1)} %copy.169), calls=%async_computation.6 | async-start | bytes 10485760 | tf_op jit(solution)/shard_map/all_to_all | solution.py:83
  979.1 5.3 copy-start.4
  1008.9 5.1 copy-start.19
  1096.2 4.9 copy-start.5
  1096.2 119.8 %all-to-all-start.6 = ((bf16[2,40,256,128]{3,0,1,2:T(2,128)(2,1)}), bf16[2,40,256,128]{3,0,1,2:T(2,128)(2,1)}, u32[]{:S(2)}, u32[]{:S(2)}) async-start(bf16[2,40,256,128]{3,0,1,2:T(2,128)(2,1)} %copy.172), calls=%async_computation.7 | async-start | bytes 10485760 | tf_op jit(solution)/shard_map/all_to_all | solution.py:87
  1111.6 5.3 copy-start.2
  1237.4 119.6 %all-to-all-start.7 = ((bf16[2,40,256,128]{3,0,1,2:T(2,128)(2,1)}), bf16[2,40,256,128]{3,0,1,2:T(2,128)(2,1)}, u32[]{:S(2)}, u32[]{:S(2)}) async-start(bf16[2,40,256,128]{3,0,1,2:T(2,128)(2,1)} %copy.183), calls=%async_computation.8 | async-start | bytes 10485760 | tf_op jit(solution)/shard_map/all_to_all | solution.py:87
  1242.0 174.4 %reduce-scatter.3.cloned.1.call-start = ((), (), s32[]{:S(2)}) async-start(), calls=%async_computation.10 | async-start | bytes 6553600 | tf_op jit(solution)/shard_map/reduce_scatter | solution.py:152
  1249.3 217.7 %reduce-scatter.5.cloned.1.call-start = ((), (), s32[]{:S(2)}) async-start(), calls=%async_computation.11 | async-start | bytes 6553600 | tf_op jit(solution)/shard_map/reduce_scatter | solution.py:152
  (14 other events, 36.5 us)
Sparse Core Ops, SparseCore 0:
  1249.5 52.6 reduce-scatter.2
  1416.6 50.4 reduce-scatter.4

commit v4 on v2

--- a/solution.py
+++ b/solution.py
@@ -40,13 +40,14 @@
     return jnp.concatenate([values, turned(values)], axis=axis)
 
 
-def chunk_gradient(pixels, sens_real, sens_imag, measured, kz_lines, y_fwd, y_back):
-    y_count = pixels.shape[0]
+def forward_y(pixels, sens_real, sens_imag, y_fwd):
     coil_image = (sens_real * pixels + sens_imag * turned(pixels)).astype(BF16)
-    spectrum = jnp.einsum(
+    return jnp.einsum(
         "ky,cyzl->ckzl", y_fwd, with_turned(coil_image, 1), preferred_element_type=F32
     ).astype(BF16)
-    gathered = lax.all_to_all(spectrum, "slab", split_axis=1, concat_axis=2, tiled=True)
+
+
+def middle_z(gathered, measured, kz_lines):
     z_count = gathered.shape[2]
     z_cos, z_sin = cos_sin(z_count)
     sampled = kz_lines >= 0
@@ -62,19 +63,34 @@
     residual = jnp.where(
         sampled[None, :, :, None], kspace - measured.astype(F32), F32(0.0)
     ).astype(BF16)
-    rows_back = jnp.concatenate(
-        [rows_fwd[..., :z_count], -rows_fwd[..., z_count:]], axis=1
-    )
-    adjoint_z = jnp.einsum(
+    rows_back = jnp.concatenate([rows_fwd[..., :z_count], -rows_fwd[..., z_count:]], axis=1)
+    return jnp.einsum(
         "kjz,ckjl->ckzl", rows_back, with_turned(residual, 2), preferred_element_type=F32
     ).astype(BF16)
-    returned = lax.all_to_all(adjoint_z, "slab", split_axis=2, concat_axis=1, tiled=True)
+
+
+def backward_y(returned, sens_real, sens_imag, y_back):
+    y_count = returned.shape[1]
     both = jnp.einsum(
         "yk,ckzl->cyzl", y_back, with_turned(returned, 1), preferred_element_type=F32
     )
     coil_back = both[:, :y_count]
     turned_back = both[:, y_count:]
     return jnp.sum(sens_real * coil_back - sens_imag * turned_back, axis=0)
+
+
+def to_ky_blocks(values):
+    return lax.all_to_all(values, "slab", split_axis=1, concat_axis=2, tiled=True)
+
+
+def to_z_slabs(values):
+    return lax.all_to_all(values, "slab", split_axis=2, concat_axis=1, tiled=True)
+
+
+def after(value, *others):
+    if not others:
+        return value
+    return lax.optimization_barrier((value,) + tuple(others))[0]
 
 
 def shards(image, coil_maps, y_data, kz_lines):
@@ -87,23 +103,25 @@
         [jnp.concatenate([y_cos, y_sin], axis=1), jnp.concatenate([-y_sin, y_cos], axis=1)],
         axis=0,
     )
-    sens_real, sens_imag = dup_halves(coil_maps.astype(F32))
+    sens_real, sens_imag = dup_halves(coil_maps)
     outputs = []
+    previous = None
     for state in range(state_count):
         pixels = image[state].astype(F32)
         total = None
         for first in range(0, coil_count, group):
-            part = chunk_gradient(
-                pixels,
-                sens_real[first : first + group],
-                sens_imag[first : first + group],
-                y_data[state, first : first + group],
-                kz_lines[state],
-                y_fwd,
-                y_back,
+            chunk_real = sens_real[first : first + group].astype(F32)
+            chunk_imag = sens_imag[first : first + group].astype(F32)
+            spectrum = forward_y(pixels, chunk_real, chunk_imag, y_fwd)
+            adjoint_z = middle_z(
+                to_ky_blocks(spectrum), y_data[state, first : first + group], kz_lines[state]
             )
+            if previous is not None and first + group >= coil_count:
+                adjoint_z = after(adjoint_z, previous)
+            part = backward_y(to_z_slabs(adjoint_z), chunk_real, chunk_imag, y_back)
             total = part if total is None else total + part
         summed = lax.psum_scatter(total, "coil", scatter_dimension=0, tiled=True)
+        previous = summed
         outputs.append(summed.astype(BF16))
     return jnp.stack(outputs)
 

time: 1400 us -> 1370 us (0.979)
  blocking collectives: 0 us -> 119 us
  waiting for transfers between devices: 614 us -> 510 us
  other arithmetic: 276 us -> 230 us
    all_to_all x0 -> x1, blocking collectives: none -> 119 us  [to_z_slabs(): lax.all_to_all(values, 'slab', split_axis=2, concat_axis=1, tiled=True)]
    all_to_all x8 -> x7, waiting for transfers between devices: 518 us -> 461 us  [the longest x4 267 us: to_ky_blocks(): lax.all_to_all(values, 'slab', split_axis=1, concat_axis=2, tiled=True)]
    reduce_scatter x2, waiting for transfers between devices: 96 us -> 49.2 us  [shards(): summed = lax.psum_scatter(total, 'coil', scatter_dimension=0, tiled=True)]
    convert_element_type x3 -> x2, other arithmetic: 86.2 us -> 42 us  [forward_y(): coil_image = (sens_real * pixels + sens_imag * turned(pixels)).astype(BF16)]
    unnamed x66 -> x78, local copies, waits for them, and re-layouts: 17.4 us -> 44.6 us
    slice x1, local copies, waits for them, and re-layouts: 30.7 us -> 9.54 us  [dup_halves(): real = values[..., :half]]
    convert_element_type x8 -> x7, local copies, waits for them, and re-layouts: 77.7 us -> 64.2 us  [the longest x3 41.4 us: middle_z(): return jnp.einsum('kjz,ckjl->ckzl', rows_back, with_turned(residual, 2),...]
    all_to_all x8 -> x7, starting transfers between devices: 41.8 us -> 36.4 us  [the longest x4 21.8 us: to_ky_blocks(): lax.all_to_all(values, 'slab', split_axis=1, concat_axis=2, tiled=True)]
  transfers between devices with their start and end apart: 10 -> 9, of which waited for: 10 -> 8; matrix products, arithmetic and copies ran while one was open for 29% -> 27% of each run, Pallas kernels for 0% -> 0%
where the time goes in v4:
time: 1370 us; the launch traced here: 1350 us
  waiting for transfers between devices  510 us (37%)
  local copies, waits for them, and re-layouts  284 us (21%)
  other arithmetic  230 us (17%)
  matrix products  159 us (12%)
  blocking collectives  119 us (9%)
  starting transfers between devices  36.5 us (3%)
  between operations  14 us (1%)
    all_to_all x4, waiting for transfers between devices, to_ky_blocks(): lax.all_to_all(values, 'slab', split_axis=1, concat_axis=2, tiled=True)  267 us
    all_to_all x3, waiting for transfers between devices, to_z_slabs(): lax.all_to_all(values, 'slab', split_axis=2, concat_axis=1, tiled=True)  194 us
    all_to_all x1, blocking collectives, to_z_slabs(): lax.all_to_all(values, 'slab', split_axis=2, concat_axis=1, tiled=True)  119 us
    neg x17, other arithmetic, turned(): return jnp.concatenate([-values[..., half:], values[..., :half]], axis=-1)  98 us
    dot_general x4, matrix products, backward_y(): jnp.einsum('yk,ckzl->cyzl', y_back, with_turned(returned, 1), preferred_e...  69.5 us
    all_to_all x12, local copies, waits for them, and re-layouts, to_z_slabs(): lax.all_to_all(values, 'slab', split_axis=2, concat_axis=1, tiled=True)  61.8 us
    all_to_all x8, local copies, waits for them, and re-layouts, to_ky_blocks(): lax.all_to_all(values, 'slab', split_axis=1, concat_axis=2, tiled=True)  57.6 us
    reduce_sum x3, other arithmetic, backward_y(): return jnp.sum(sens_real * coil_back - sens_imag * turned_back, axis=0)  55.5 us
  transfers between devices with their start and end apart: 9, of which 8 were waited for; matrix products, arithmetic and copies ran while one was open for 27% of the time, Pallas kernels for 0%

profile of v4, /device:TPU:0, one launch (start us, length us, event | category | flops | bytes accessed | tf_op | source)
XLA Modules:
  0.0 1353.2 jit_solution(5193855917808876676)
XLA Ops:
  15.9 8.8 slice_negate_fusion.2
  53.8 9.5 fusion.220
  63.3 12.0 copy.209
  75.4 11.9 copy.210
  87.2 31.9 %fusion.9 = (bf16[2,320,32,128]{3,1,2,0:T(8,128)(2,1)}, bf16[2,320,32,128]{3,1,2,0:T(8,128)(2,1)}, bf16[2,320,32,128]{3,1,2,0:T(8,128)(2,1)}, bf16[2,320,32,128]...) fusion(f32[320,32,128]{2,0,1:T(8,128)} %copy.135, ...), kind=kLoop, calls=%fused_computation.25 | loop fusion | flops 73400320 | bytes 62914560 | tf_op jit(solution)/shard_map/convert_element_type | solution.py:44
  119.2 10.1 slice_negate_fusion.3
  129.2 8.9 convert_bitcast_fusion.5
  151.1 9.9 slice_negate_fusion.1
  175.4 91.5 %all-to-all-done.2 = bf16[2,320,32,128]{3,2,0,1:T(8,128)(2,1)} async-done(((bf16[2,320,32,128]{3,2,0,1:T(8,128)(2,1)}), bf16[2,320,32,128]{3,2,0,1:T(8,128)(2,1)}, u32[]{:S(2)}, u32[]{:S(2)}) %all-to-all-start.2) | async-done | bytes 5242912 | tf_op jit(solution)/shard_map/all_to_all | solution.py:83
  271.9 10.0 fusion.1
  281.9 9.9 slice_negate_fusion.4
  306.2 80.6 %all-to-all-done.4 = bf16[2,320,32,128]{3,2,0,1:T(8,128)(2,1)} async-done(((bf16[2,320,32,128]{3,2,0,1:T(8,128)(2,1)}), bf16[2,320,32,128]{3,2,0,1:T(8,128)(2,1)}, u32[]{:S(2)}, u32[]{:S(2)}) %all-to-all-start.4) | async-done | bytes 5242912 | tf_op jit(solution)/shard_map/all_to_all | solution.py:83
  445.4 13.8 %copy.157 = bf16[2,40,256,128]{3,0,1,2:T(2,128)(2,1)} copy(bf16[2,40,256,128]{2,3,0,1:T(8,128)(2,1)} %convert_bitcast_fusion.4) | data formatting | bytes 10485760 | tf_op jit(solution)/shard_map/convert_element_type | solution.py:69
  459.2 47.4 %all-to-all-done = bf16[2,320,32,128]{3,2,0,1:T(8,128)(2,1)} async-done(((bf16[2,320,32,128]{3,2,0,1:T(8,128)(2,1)}), bf16[2,320,32,128]{3,2,0,1:T(8,128)(2,1)}, u32[]{:S(2)}, u32[]{:S(2)}) %all-to-all-start) | async-done | bytes 5242912 | tf_op jit(solution)/shard_map/all_to_all | solution.py:83
  556.2 13.8 %copy.173 = bf16[2,40,256,128]{3,0,1,2:T(2,128)(2,1)} copy(bf16[2,40,256,128]{2,3,0,1:T(8,128)(2,1)} %convert_bitcast_fusion.2) | data formatting | bytes 10485760 | tf_op jit(solution)/shard_map/convert_element_type | solution.py:69
  570.0 56.3 %all-to-all-done.3 = bf16[2,40,256,128]{3,0,1,2:T(2,128)(2,1)} async-done(((bf16[2,40,256,128]{3,0,1,2:T(2,128)(2,1)}), bf16[2,40,256,128]{3,0,1,2:T(2,128)(2,1)}, u32[]{:S(2)}, u32[]{:S(2)}) %all-to-all-start.3) | async-done | bytes 5242912 | tf_op jit(solution)/shard_map/all_to_all | solution.py:87
  669.1 13.8 %copy.143 = bf16[2,40,256,128]{3,0,1,2:T(2,128)(2,1)} copy(bf16[2,40,256,128]{2,3,0,1:T(8,128)(2,1)} %convert_bitcast_fusion.6) | data formatting | bytes 10485760 | tf_op jit(solution)/shard_map/convert_element_type | solution.py:69
  682.9 63.1 %all-to-all-done.5 = bf16[2,40,256,128]{3,0,1,2:T(2,128)(2,1)} async-done(((bf16[2,40,256,128]{3,0,1,2:T(2,128)(2,1)}), bf16[2,40,256,128]{3,0,1,2:T(2,128)(2,1)}, u32[]{:S(2)}, u32[]{:S(2)}) %all-to-all-start.5) | async-done | bytes 5242912 | tf_op jit(solution)/shard_map/all_to_all | solution.py:87
  791.6 74.3 %all-to-all-done.1 = bf16[2,40,256,128]{3,0,1,2:T(2,128)(2,1)} async-done(((bf16[2,40,256,128]{3,0,1,2:T(2,128)(2,1)}), bf16[2,40,256,128]{3,0,1,2:T(2,128)(2,1)}, u32[]{:S(2)}, u32[]{:S(2)}) %all-to-all-start.1) | async-done | bytes 5242912 | tf_op jit(solution)/shard_map/all_to_all | solution.py:87
  888.0 17.7 %fusion.94 = f32[2,640,32,128]{3,1,2,0:T(8,128)} fusion(bf16[2,320,32,64]{1,3,2,0:T(8,128)(2,1)} %get-tuple-element.29, bf16[2,320,32,64]{1,3,2,0:T(8,128)(2,1)} %get-tuple-element.28, bf16[2,320,32,128]{1,3,2,0:T(8,128)(2,1)} %copy.162, bf16[320,320]{1,0:T(8,128)(2,1)} %copy-done.22, bf16[320,320]{1,0:T(8,128)(2,1)} %copy-done.23, ...), kind=kOutput, calls=%fused_computation.110 | convolution fusion | flops 6745620480 | bytes 32071680 | tf_op jit(solution)/shard_map/yk,ckzl->cyzl/dot_general | solution.py:74
  905.8 19.8 %fusion.11 = (f32[320,32,128]{2,0,1:T(8,128)}, bf16[2,320,32,128]{3,1,2,0:T(8,128)(2,1)}) fusion(bf16[2,320,32,128]{3,1,2,0:T(8,128)(2,1)} %get-tuple-element.11, bf16[2,320,32,128]{3,1,2,0:T(8,128)(2,1)} %get-tuple-element.10, f32[2,640,32,128]{3,1,2,0:T(8,128)} %fusion.94, f32[320,32,128]{2,0,1:T(8,128)} %copy.165, f32[320,32,128]{2,0,1:T(8,128)} %copy.164), kind=kLoop, calls=%fused_computation.27 | loop fusion | flops 24903680 | bytes 52428800 | tf_op jit(solution)/shard_map/reduce_sum | solution.py:79
  925.6 10.0 slice_negate_fusion
  935.5 8.8 convert_bitcast_fusion.1
  954.7 17.3 %fusion.91 = f32[2,640,32,128]{3,1,2,0:T(8,128)} fusion(bf16[2,320,32,64]{1,3,2,0:T(8,128)(2,1)} %get-tuple-element.31, bf16[2,320,32,64]{1,3,2,0:T(8,128)(2,1)S(1)} %get-tuple-element.30, bf16[2,320,32,128]{1,3,2,0:T(8,128)(2,1)} %copy.178, bf16[320,320]{1,0:T(8,128)(2,1)} %copy-done.22, bf16[320,320]{1,0:T(8,128)(2,1)} %copy-done.23, ...), kind=kOutput, calls=%fused_computation.109 | convolution fusion | flops 6745620480 | bytes 32071680 | tf_op jit(solution)/shard_map/yk,ckzl->cyzl/dot_general | solution.py:74
  972.0 17.7 %fusion.97 = f32[2,640,32,128]{3,1,2,0:T(8,128)} fusion(bf16[2,320,32,64]{1,3,2,0:T(8,128)(2,1)} %get-tuple-element.33, bf16[2,320,32,64]{1,3,2,0:T(8,128)(2,1)} %get-tuple-element.32, bf16[2,320,32,128]{1,3,2,0:T(8,128)(2,1)} %copy.148, bf16[320,320]{1,0:T(8,128)(2,1)} %copy-done.22, bf16[320,320]{1,0:T(8,128)(2,1)} %copy-done.23, ...), kind=kOutput, calls=%fused_computation.111 | convolution fusion | flops 6745620480 | bytes 32071680 | tf_op jit(solution)/shard_map/yk,ckzl->cyzl/dot_general | solution.py:74
  989.7 22.6 %fusion.3 = (f32[320,32,128]{2,0,1:T(8,128)}, f32[320,32,128]{2,0,1:T(8,128)}) fusion(bf16[2,320,32,128]{3,1,2,0:T(8,128)(2,1)} %get-tuple-element.17, bf16[2,320,32,128]{3,1,2,0:T(8,128)(2,1)} %get-tuple-element.16, f32[2,640,32,128]{3,1,2,0:T(8,128)} %fusion.97, f32[2,640,32,128]{3,1,2,0:T(8,128)} %fusion.91), kind=kLoop, calls=%fused_computation.19 | loop fusion | flops 23592960 | bytes 62914560 | tf_op jit(solution)/shard_map/reduce_sum | solution.py:79
  1022.3 47.3 %all-to-all-done.6 = bf16[2,320,32,128]{3,2,0,1:T(8,128)(2,1)} async-done(((bf16[2,320,32,128]{3,2,0,1:T(8,128)(2,1)}), bf16[2,320,32,128]{3,2,0,1:T(8,128)(2,1)}, u32[]{:S(2)}, u32[]{:S(2)}) %all-to-all-start.6) | async-done | bytes 5242912 | tf_op jit(solution)/shard_map/all_to_all | solution.py:83
  1105.2 13.8 %copy.187 = bf16[2,40,256,128]{3,0,1,2:T(2,128)(2,1)} copy(bf16[2,40,256,128]{2,3,0,1:T(8,128)(2,1)} %convert_bitcast_fusion) | data formatting | bytes 10485760 | tf_op jit(solution)/shard_map/optimization_barrier | solution.py:93
  1119.0 119.4 %all_to_all.144 = bf16[2,40,256,128]{3,0,1,2:T(2,128)(2,1)S(1)} all-to-all(bf16[2,40,256,128]{3,0,1,2:T(2,128)(2,1)} %copy.187), channel_id=1, replica_groups=mesh['slab'=8,'coil'=4] {'slab'}, dimensions={2} | all-to-all | bytes 10485760 | tf_op jit(solution)/shard_map/all_to_all | solution.py:87
  1257.1 16.8 %fusion.88 = f32[2,640,32,128]{3,1,2,0:T(8,128)} fusion(bf16[2,320,32,64]{1,3,2,0:T(8,128)(2,1)} %get-tuple-element.27, bf16[2,320,32,64]{1,3,2,0:T(8,128)(2,1)S(1)} %get-tuple-element.26, bf16[2,320,32,128]{1,3,2,0:T(8,128)(2,1)} %copy.192, bf16[320,320]{1,0:T(8,128)(2,1)} %copy-done.22, bf16[320,320]{1,0:T(8,128)(2,1)} %copy-done.23, ...), kind=kOutput, calls=%fused_computation.108 | convolution fusion | flops 6745620480 | bytes 32071680 | tf_op jit(solution)/shard_map/yk,ckzl->cyzl/dot_general | solution.py:74
  1273.8 13.1 fusion.15
  1294.0 49.2 %reduce-scatter.5.cloned.1.call-done = f32[80,32,128]{2,0,1:T(8,128)} async-done(((f32[320,32,128]{2,0,1:T(8,128)}), f32[80,32,128]{2,0,1:T(8,128)}) %reduce-scatter.5.cloned.1.call-update) | async-done | bytes 1310736 | tf_op jit(solution)/shard_map/reduce_scatter | solution.py:123
  (162 shorter events, 388.3 us)
Async XLA Ops:
  24.7 10.4 copy-start.1
  24.7 10.4 copy-start.2
  30.0 16.7 %slice-start.5 = ((s8[5242880]{0:T(1024)(128)(4,1)}), s8[4194304]{0:T(1024)(128)(4,1)S(1)}, s32[]{:S(2)}) async-start(s8[5242880]{0:T(1024)(128)(4,1)} %bitcast.160), calls=%async_computation.17 | async-start | bytes 8388608
  30.0 16.7 %slice-start.7 = ((s8[5242880]{0:T(1024)(128)(4,1)}), s8[4194304]{0:T(1024)(128)(4,1)S(1)}, s32[]{:S(2)}) async-start(s8[5242880]{0:T(1024)(128)(4,1)} %bitcast.162), calls=%async_computation.19 | async-start | bytes 8388608
  32.9 259.0 %copy-start.22 = (bf16[320,320]{1,0:T(8,128)(2,1)}, bf16[320,320]{1,0:T(8,128)(2,1)S(1)}, u32[]{:S(2)}) copy-start(bf16[320,320]{1,0:T(8,128)(2,1)S(1)} %get-tuple-element.75) | copy-start | bytes 614404
  35.1 256.8 %copy-start.23 = (bf16[320,320]{1,0:T(8,128)(2,1)}, bf16[320,320]{1,0:T(8,128)(2,1)S(1)}, u32[]{:S(2)}) copy-start(bf16[320,320]{1,0:T(8,128)(2,1)S(1)} %fusion.198) | copy-start | bytes 614404
  35.1 11.6 slice-start.6
  35.1 11.6 slice-start.8
  46.7 7.0 slice-start
  46.8 7.0 slice-start.1
  48.2 5.5 slice-start.2
  143.8 123.0 %all-to-all-start.2 = ((bf16[2,320,32,128]{3,2,0,1:T(8,128)(2,1)}), bf16[2,320,32,128]{3,2,0,1:T(8,128)(2,1)}, u32[]{:S(2)}, u32[]{:S(2)}) async-start(bf16[2,320,32,128]{3,2,0,1:T(8,128)(2,1)} %copy.150), calls=%async_computation.2 | async-start | bytes 10485760 | tf_op jit(solution)/shard_map/all_to_all | solution.py:83
  266.9 120.0 %all-to-all-start.4 = ((bf16[2,320,32,128]{3,2,0,1:T(8,128)(2,1)}), bf16[2,320,32,128]{3,2,0,1:T(8,128)(2,1)}, u32[]{:S(2)}, u32[]{:S(2)}) async-start(bf16[2,320,32,128]{3,2,0,1:T(8,128)(2,1)} %copy.166), calls=%async_computation.5 | async-start | bytes 10485760 | tf_op jit(solution)/shard_map/all_to_all | solution.py:83
  386.8 119.7 %all-to-all-start = ((bf16[2,320,32,128]{3,2,0,1:T(8,128)(2,1)}), bf16[2,320,32,128]{3,2,0,1:T(8,128)(2,1)}, u32[]{:S(2)}, u32[]{:S(2)}) async-start(bf16[2,320,32,128]{3,2,0,1:T(8,128)(2,1)} %copy.136), calls=%async_computation | async-start | bytes 10485760 | tf_op jit(solution)/shard_map/all_to_all | solution.py:83
  403.5 137.0 %copy-start.25 = (pred[40,128]{1,0:T(8,128)(4,1)}, pred[40,128]{1,0:T(8,128)(4,1)S(1)}, u32[]{:S(2)}) copy-start(pred[40,128]{1,0:T(8,128)(4,1)S(1)} %get-tuple-element.68) | copy-start | bytes 15364
  424.3 5.3 copy-start.5
  459.2 52.2 %copy-start.9 = (bf16[1,2,40,128,128]{4,3,2,1,0:T(8,128)(2,1)S(1)}, bf16[1,2,40,128,128]{4,3,2,1,0:T(8,128)(2,1)}, u32[]{:S(2)}) copy-start(bf16[1,2,40,128,128]{4,3,2,1,0:T(8,128)(2,1)} %get-tuple-element.21) | copy-start | bytes 7864324
  506.6 119.8 %all-to-all-start.3 = ((bf16[2,40,256,128]{3,0,1,2:T(2,128)(2,1)}), bf16[2,40,256,128]{3,0,1,2:T(2,128)(2,1)}, u32[]{:S(2)}, u32[]{:S(2)}) async-start(bf16[2,40,256,128]{3,0,1,2:T(2,128)(2,1)} %copy.157), calls=%async_computation.3 | async-start | bytes 10485760 | tf_op jit(solution)/shard_map/all_to_all | solution.py:87
  535.1 5.4 copy-start.6
  570.0 61.0 %copy-start.8 = (bf16[1,2,40,128,128]{4,3,2,1,0:T(8,128)(2,1)S(1)}, bf16[1,2,40,128,128]{4,3,2,1,0:T(8,128)(2,1)}, u32[]{:S(2)}) copy-start(bf16[1,2,40,128,128]{4,3,2,1,0:T(8,128)(2,1)} %get-tuple-element.22) | copy-start | bytes 7864324
  626.4 119.6 %all-to-all-start.5 = ((bf16[2,40,256,128]{3,0,1,2:T(2,128)(2,1)}), bf16[2,40,256,128]{3,0,1,2:T(2,128)(2,1)}, u32[]{:S(2)}, u32[]{:S(2)}) async-start(bf16[2,40,256,128]{3,0,1,2:T(2,128)(2,1)} %copy.173), calls=%async_computation.6 | async-start | bytes 10485760 | tf_op jit(solution)/shard_map/all_to_all | solution.py:87
  648.0 5.3 copy-start.3
  745.9 120.0 %all-to-all-start.1 = ((bf16[2,40,256,128]{3,0,1,2:T(2,128)(2,1)}), bf16[2,40,256,128]{3,0,1,2:T(2,128)(2,1)}, u32[]{:S(2)}, u32[]{:S(2)}) async-start(bf16[2,40,256,128]{3,0,1,2:T(2,128)(2,1)} %copy.143), calls=%async_computation.1 | async-start | bytes 10485760 | tf_op jit(solution)/shard_map/all_to_all | solution.py:87
  783.2 6.2 copy-start
  881.9 6.1 copy-start.21
  950.0 119.6 %all-to-all-start.6 = ((bf16[2,320,32,128]{3,2,0,1:T(8,128)(2,1)}), bf16[2,320,32,128]{3,2,0,1:T(8,128)(2,1)}, u32[]{:S(2)}, u32[]{:S(2)}) async-start(bf16[2,320,32,128]{3,2,0,1:T(8,128)(2,1)} %copy.180), calls=%async_computation.7 | async-start | bytes 10485760 | tf_op jit(solution)/shard_map/all_to_all | solution.py:83
  954.7 150.5 %reduce-scatter.3.cloned.1.call-start = ((), (), s32[]{:S(2)}) async-start(), calls=%async_computation.10 | async-start | bytes 6553600 | tf_op jit(solution)/shard_map/reduce_scatter | solution.py:123
  972.0 40.3 %slice-start.3 = ((s8[5242880]{0:T(1024)(128)(4,1)}), s8[1048576]{0:T(1024)(128)(4,1)S(1)}, s32[]{:S(2)}) async-start(s8[5242880]{0:T(1024)(128)(4,1)} %bitcast.158), calls=%async_computation.15 | async-start | bytes 2097152
  989.7 22.6 %slice-start.4 = ((s8[5242880]{0:T(1024)(128)(4,1)}), s8[4194304]{0:T(1024)(128)(4,1)S(1)}, s32[]{:S(2)}) async-start(s8[5242880]{0:T(1024)(128)(4,1)} %bitcast.158), calls=%async_computation.16 | async-start | bytes 8388608
  1017.8 325.5 %reduce-scatter.5.cloned.1.call-start = ((), (), s32[]{:S(2)}) async-start(), calls=%async_computation.11 | async-start | bytes 6553600 | tf_op jit(solution)/shard_map/reduce_scatter | solution.py:123
  1084.1 5.3 copy-start.4
  1084.1 5.3 copy-start.26
  (13 other events, 39.2 us)
Sparse Core Ops, SparseCore 0:
  1017.9 52.6 reduce-scatter.2
  1292.7 50.4 reduce-scatter.4

commit v5 on v4

--- a/solution.py
+++ b/solution.py
@@ -104,26 +104,41 @@
         axis=0,
     )
     sens_real, sens_imag = dup_halves(coil_maps)
-    outputs = []
-    previous = None
-    for state in range(state_count):
-        pixels = image[state].astype(F32)
-        total = None
-        for first in range(0, coil_count, group):
-            chunk_real = sens_real[first : first + group].astype(F32)
-            chunk_imag = sens_imag[first : first + group].astype(F32)
-            spectrum = forward_y(pixels, chunk_real, chunk_imag, y_fwd)
-            adjoint_z = middle_z(
-                to_ky_blocks(spectrum), y_data[state, first : first + group], kz_lines[state]
-            )
-            if previous is not None and first + group >= coil_count:
-                adjoint_z = after(adjoint_z, previous)
-            part = backward_y(to_z_slabs(adjoint_z), chunk_real, chunk_imag, y_back)
-            total = part if total is None else total + part
-        summed = lax.psum_scatter(total, "coil", scatter_dimension=0, tiled=True)
-        previous = summed
-        outputs.append(summed.astype(BF16))
-    return jnp.stack(outputs)
+    chunks = [(state, first) for state in range(state_count) for first in range(0, coil_count, group)]
+    count = len(chunks)
+
+    def sens_of(index):
+        first = chunks[index][1]
+        return (
+            sens_real[first : first + group].astype(F32),
+            sens_imag[first : first + group].astype(F32),
+        )
+
+    gathered = []
+    for index, (state, first) in enumerate(chunks):
+        spectrum = forward_y(image[state].astype(F32), *sens_of(index), y_fwd)
+        if gathered:
+            spectrum = after(spectrum, gathered[-1])
+        gathered.append(to_ky_blocks(spectrum))
+    adjoints = [
+        middle_z(gathered[index], y_data[state, first : first + group], kz_lines[state])
+        for index, (state, first) in enumerate(chunks)
+    ]
+    returned = []
+    totals = {}
+    outputs = {}
+    for index, (state, first) in enumerate(chunks):
+        holds = [returned[-1]] if returned else [gathered[-1]]
+        if index + 1 < count:
+            holds.append(adjoints[index + 1])
+        else:
+            holds.extend(totals[done] for done in outputs)
+        returned.append(to_z_slabs(after(adjoints[index], *holds)))
+        part = backward_y(returned[-1], *sens_of(index), y_back)
+        totals[state] = part if state not in totals else totals[state] + part
+        if first + group >= coil_count:
+            outputs[state] = lax.psum_scatter(totals[state], "coil", scatter_dimension=0, tiled=True)
+    return jnp.stack([outputs[state].astype(BF16) for state in range(state_count)])
 
 
 def solution(mesh):

time: 1370 us -> 1430 us (1.044)
  waiting for transfers between devices: 510 us -> 671 us
  blocking collectives: 119 us -> 0 us
    all_to_all x1 -> x0, blocking collectives: 119 us -> none  [to_z_slabs(): lax.all_to_all(values, 'slab', split_axis=2, concat_axis=1, tiled=True)]
    all_to_all x3 -> x4, waiting for transfers between devices: 194 us -> 313 us  [to_z_slabs(): lax.all_to_all(values, 'slab', split_axis=2, concat_axis=1, tiled=True)]
    optimization_barrier x1 -> x7, local copies, waits for them, and re-layouts: 13.8 us -> 72.2 us  [after(): return lax.optimization_barrier((value,) + tuple(others))[0]]
    convert_element_type x3 -> x0, local copies, waits for them, and re-layouts: 41.4 us -> none  [middle_z(): return jnp.einsum('kjz,ckjl->ckzl', rows_back, with_turned(residual, 2),...]
    all_to_all x4, waiting for transfers between devices: 267 us -> 308 us  [to_ky_blocks(): lax.all_to_all(values, 'slab', split_axis=1, concat_axis=2, tiled=True)]
    convert_element_type x4 -> x1, local copies, waits for them, and re-layouts: 22.8 us -> 5.77 us  [forward_y(): return jnp.einsum('ky,cyzl->ckzl', y_fwd, with_turned(coil_image, 1), pre...]
    convert_element_type x2 -> x3, other arithmetic: 42 us -> 52.1 us  [forward_y(): coil_image = (sens_real * pixels + sens_imag * turned(pixels)).astype(BF16)]
  transfers between devices with their start and end apart: 9 -> 10, of which waited for: 8 -> 9; matrix products, arithmetic and copies ran while one was open for 27% -> 25% of each run, Pallas kernels for 0% -> 0%
where the time goes in v5:
time: 1430 us; the launch traced here: 1410 us
  waiting for transfers between devices  671 us (47%)
  local copies, waits for them, and re-layouts  288 us (20%)
  other arithmetic  238 us (17%)
  matrix products  160 us (11%)
  starting transfers between devices  42.4 us (3%)
  between operations  14.3 us (1%)
    all_to_all x4, waiting for transfers between devices, to_z_slabs(): lax.all_to_all(values, 'slab', split_axis=2, concat_axis=1, tiled=True)  313 us
    all_to_all x4, waiting for transfers between devices, to_ky_blocks(): lax.all_to_all(values, 'slab', split_axis=1, concat_axis=2, tiled=True)  308 us
    neg x17, other arithmetic, turned(): return jnp.concatenate([-values[..., half:], values[..., :half]], axis=-1)  100 us
    optimization_barrier x7, local copies, waits for them, and re-layouts, after(): return lax.optimization_barrier((value,) + tuple(others))[0]  72.2 us
    dot_general x4, matrix products, backward_y(): jnp.einsum('yk,ckzl->cyzl', y_back, with_turned(returned, 1), preferred_e...  66.3 us
    all_to_all x12, local copies, waits for them, and re-layouts, to_z_slabs(): lax.all_to_all(values, 'slab', split_axis=2, concat_axis=1, tiled=True)  64.2 us
    all_to_all x8, local copies, waits for them, and re-layouts, to_ky_blocks(): lax.all_to_all(values, 'slab', split_axis=1, concat_axis=2, tiled=True)  58.3 us
    convert_element_type x3, other arithmetic, forward_y(): coil_image = (sens_real * pixels + sens_imag * turned(pixels)).astype(BF16)  52.1 us
  transfers between devices with their start and end apart: 10, of which 9 were waited for; matrix products, arithmetic and copies ran while one was open for 25% of the time, Pallas kernels for 0%

profile of v5, /device:TPU:0, one launch (start us, length us, event | category | flops | bytes accessed | tf_op | source)
XLA Modules:
  0.0 1413.4 jit_solution(18024099507708162952)
XLA Ops:
  63.2 12.0 copy.209
  75.2 11.9 copy.210
  87.1 32.0 %fusion.11 = (bf16[2,320,32,128]{3,1,2,0:T(8,128)(2,1)}, bf16[2,320,32,128]{3,1,2,0:T(8,128)(2,1)}, bf16[2,320,32,128]{3,1,2,0:T(8,128)(2,1)}, bf16[2,320,32,128...) fusion(f32[320,32,128]{2,0,1:T(8,128)} %copy.135, ...), kind=kLoop, calls=%fused_computation.27 | loop fusion | flops 73400320 | bytes 62914560 | tf_op jit(solution)/shard_map/convert_element_type | solution.py:44
  119.1 10.1 fusion.1
  129.2 10.0 slice_negate_fusion.4
  161.1 9.9 slice_negate_fusion
  171.0 10.2 convert_bitcast_fusion.3
  181.2 95.6 %all-to-all-done = bf16[2,320,32,128]{3,2,0,1:T(8,128)(2,1)} async-done(((bf16[2,320,32,128]{3,2,0,1:T(8,128)(2,1)}), bf16[2,320,32,128]{3,2,0,1:T(8,128)(2,1)}, u32[]{:S(2)}, u32[]{:S(2)}) %all-to-all-start) | async-done | bytes 5242912 | tf_op jit(solution)/shard_map/all_to_all | solution.py:83
  294.3 9.9 slice_negate_fusion.1
  304.2 10.1 convert_bitcast_fusion.4
  314.3 94.9 %all-to-all-done.1 = bf16[2,320,32,128]{3,2,0,1:T(8,128)(2,1)} async-done(((bf16[2,320,32,128]{3,2,0,1:T(8,128)(2,1)}), bf16[2,320,32,128]{3,2,0,1:T(8,128)(2,1)}, u32[]{:S(2)}, u32[]{:S(2)}) %all-to-all-start.1) | async-done | bytes 5242912 | tf_op jit(solution)/shard_map/all_to_all | solution.py:83
  426.4 10.1 fusion.9
  436.4 10.0 slice_negate_fusion.2
  446.4 10.2 convert_bitcast_fusion.5
  456.6 84.7 %all-to-all-done.2 = bf16[2,320,32,128]{3,2,0,1:T(8,128)(2,1)} async-done(((bf16[2,320,32,128]{3,2,0,1:T(8,128)(2,1)}), bf16[2,320,32,128]{3,2,0,1:T(8,128)(2,1)}, u32[]{:S(2)}, u32[]{:S(2)}) %all-to-all-start.2) | async-done | bytes 5242912 | tf_op jit(solution)/shard_map/all_to_all | solution.py:83
  640.5 32.9 %all-to-all-done.3 = bf16[2,320,32,128]{3,2,0,1:T(8,128)(2,1)} async-done(((bf16[2,320,32,128]{3,2,0,1:T(8,128)(2,1)}), bf16[2,320,32,128]{3,2,0,1:T(8,128)(2,1)}, u32[]{:S(2)}, u32[]{:S(2)}) %all-to-all-start.3) | async-done | bytes 5242912 | tf_op jit(solution)/shard_map/all_to_all | solution.py:83
  679.9 13.8 copy.158
  738.1 75.8 %all-to-all-done.4 = bf16[2,40,256,128]{3,0,1,2:T(2,128)(2,1)} async-done(((bf16[2,40,256,128]{3,0,1,2:T(2,128)(2,1)}), bf16[2,40,256,128]{3,0,1,2:T(2,128)(2,1)}, u32[]{:S(2)}, u32[]{:S(2)}) %all-to-all-start.4) | async-done | bytes 5242912 | tf_op jit(solution)/shard_map/all_to_all | solution.py:87
  821.4 13.8 copy.169
  872.0 83.0 %all-to-all-done.5 = bf16[2,40,256,128]{3,0,1,2:T(2,128)(2,1)} async-done(((bf16[2,40,256,128]{3,0,1,2:T(2,128)(2,1)}), bf16[2,40,256,128]{3,0,1,2:T(2,128)(2,1)}, u32[]{:S(2)}, u32[]{:S(2)}) %all-to-all-start.5) | async-done | bytes 5242912 | tf_op jit(solution)/shard_map/all_to_all | solution.py:87
  962.6 13.7 copy.180
  994.9 16.8 %fusion.97 = f32[2,640,32,128]{3,1,2,0:T(8,128)} fusion(bf16[2,320,32,64]{1,3,2,0:T(8,128)(2,1)} %get-tuple-element.43, bf16[2,320,32,64]{1,3,2,0:T(8,128)(2,1)S(1)} %get-tuple-element.42, bf16[2,320,32,128]{1,3,2,0:T(8,128)(2,1)} %copy.163, bf16[320,320]{1,0:T(8,128)(2,1)} %copy-done.22, bf16[320,320]{1,0:T(8,128)(2,1)} %copy-done.24, ...), kind=kOutput, calls=%fused_computation.111 | convolution fusion | flops 6745620480 | bytes 32071680 | tf_op jit(solution)/shard_map/yk,ckzl->cyzl/dot_general | solution.py:74
  1025.3 16.8 %fusion.94 = f32[2,640,32,128]{3,1,2,0:T(8,128)} fusion(bf16[2,320,32,64]{1,3,2,0:T(8,128)(2,1)} %get-tuple-element.39, bf16[2,320,32,64]{1,3,2,0:T(8,128)(2,1)S(1)} %get-tuple-element.38, bf16[2,320,32,128]{1,3,2,0:T(8,128)(2,1)} %copy.174, bf16[320,320]{1,0:T(8,128)(2,1)} %copy-done.22, bf16[320,320]{1,0:T(8,128)(2,1)} %copy-done.24, ...), kind=kOutput, calls=%fused_computation.110 | convolution fusion | flops 6745620480 | bytes 32071680 | tf_op jit(solution)/shard_map/yk,ckzl->cyzl/dot_general | solution.py:74
  1042.1 14.3 %fusion.13 = f32[320,32,128]{2,0,1:T(8,128)} fusion(bf16[2,320,32,128]{3,1,2,0:T(8,128)(2,1)} %get-tuple-element.23, bf16[2,320,32,128]{3,1,2,0:T(8,128)(2,1)} %get-tuple-element.22, f32[2,640,32,128]{3,1,2,0:T(8,128)} %fusion.94), kind=kLoop, calls=%fused_computation.29 | loop fusion | flops 14417920 | bytes 36700160 | tf_op jit(solution)/shard_map/reduce_sum | solution.py:79
  1056.4 39.7 %all-to-all-done.6 = bf16[2,40,256,128]{3,0,1,2:T(2,128)(2,1)} async-done(((bf16[2,40,256,128]{3,0,1,2:T(2,128)(2,1)}), bf16[2,40,256,128]{3,0,1,2:T(2,128)(2,1)}, u32[]{:S(2)}, u32[]{:S(2)}) %all-to-all-start.6) | async-done | bytes 5242912 | tf_op jit(solution)/shard_map/all_to_all | solution.py:87
  1118.2 16.0 %fusion.91 = f32[2,640,32,128]{3,1,2,0:T(8,128)} fusion(bf16[2,320,32,64]{1,3,2,0:T(8,128)(2,1)} %get-tuple-element.41, bf16[2,320,32,64]{1,3,2,0:T(8,128)(2,1)} %get-tuple-element.40, bf16[2,320,32,128]{1,3,2,0:T(8,128)(2,1)} %copy.185, bf16[320,320]{1,0:T(8,128)(2,1)S(1)} %copy-done.23, bf16[320,320]{1,0:T(8,128)(2,1)S(1)} %copy-done.25, ...), kind=kOutput, calls=%fused_computation.109 | convolution fusion | flops 6745620480 | bytes 32071680 | tf_op jit(solution)/shard_map/yk,ckzl->cyzl/dot_general | solution.py:74
  1134.2 22.7 %fusion.5 = (f32[320,32,128]{2,0,1:T(8,128)}, f32[320,32,128]{2,0,1:T(8,128)}) fusion(bf16[2,320,32,128]{3,1,2,0:T(8,128)(2,1)} %get-tuple-element.29, bf16[2,320,32,128]{3,1,2,0:T(8,128)(2,1)} %get-tuple-element.28, f32[2,640,32,128]{3,1,2,0:T(8,128)} %fusion.97, f32[2,640,32,128]{3,1,2,0:T(8,128)} %fusion.91), kind=kLoop, calls=%fused_computation.21 | loop fusion | flops 23592960 | bytes 62914560 | tf_op jit(solution)/shard_map/reduce_sum | solution.py:79
  1162.4 13.8 copy.187
  1181.9 114.1 %all-to-all-done.7 = bf16[2,40,256,128]{3,0,1,2:T(2,128)(2,1)} async-done(((bf16[2,40,256,128]{3,0,1,2:T(2,128)(2,1)}), bf16[2,40,256,128]{3,0,1,2:T(2,128)(2,1)}, u32[]{:S(2)}, u32[]{:S(2)}) %all-to-all-start.7) | async-done | bytes 5242912 | tf_op jit(solution)/shard_map/all_to_all | solution.py:87
  1317.1 16.7 %fusion.88 = f32[2,640,32,128]{3,1,2,0:T(8,128)} fusion(bf16[2,320,32,64]{1,3,2,0:T(8,128)(2,1)} %get-tuple-element.37, bf16[2,320,32,64]{1,3,2,0:T(8,128)(2,1)S(1)} %get-tuple-element.36, bf16[2,320,32,128]{1,3,2,0:T(8,128)(2,1)} %copy.192, bf16[320,320]{1,0:T(8,128)(2,1)} %copy-done.22, bf16[320,320]{1,0:T(8,128)(2,1)} %copy-done.24, ...), kind=kOutput, calls=%fused_computation.108 | convolution fusion | flops 6745620480 | bytes 32071680 | tf_op jit(solution)/shard_map/yk,ckzl->cyzl/dot_general | solution.py:74
  1333.9 13.1 fusion.15
  1354.0 49.1 %reduce-scatter.5.cloned.1.call-done = f32[80,32,128]{2,0,1:T(8,128)} async-done(((f32[320,32,128]{2,0,1:T(8,128)}), f32[80,32,128]{2,0,1:T(8,128)}) %reduce-scatter.5.cloned.1.call-update) | async-done | bytes 1310736 | tf_op jit(solution)/shard_map/reduce_scatter | solution.py:140
  (164 shorter events, 411.5 us)
Async XLA Ops:
  24.7 10.5 copy-start
  24.7 10.5 copy-start.1
  30.1 16.7 %slice-start.5 = ((s8[5242880]{0:T(1024)(128)(4,1)}), s8[4194304]{0:T(1024)(128)(4,1)S(1)}, s32[]{:S(2)}) async-start(s8[5242880]{0:T(1024)(128)(4,1)} %bitcast.166), calls=%async_computation.17 | async-start | bytes 8388608
  30.1 16.7 %slice-start.7 = ((s8[5242880]{0:T(1024)(128)(4,1)}), s8[4194304]{0:T(1024)(128)(4,1)S(1)}, s32[]{:S(2)}) async-start(s8[5242880]{0:T(1024)(128)(4,1)} %bitcast.168), calls=%async_computation.19 | async-start | bytes 8388608
  33.0 413.4 %copy-start.22 = (bf16[320,320]{1,0:T(8,128)(2,1)}, bf16[320,320]{1,0:T(8,128)(2,1)S(1)}, u32[]{:S(2)}) copy-start(bf16[320,320]{1,0:T(8,128)(2,1)S(1)} %get-tuple-element.85) | copy-start | bytes 614404
  35.2 411.2 %copy-start.24 = (bf16[320,320]{1,0:T(8,128)(2,1)}, bf16[320,320]{1,0:T(8,128)(2,1)S(1)}, u32[]{:S(2)}) copy-start(bf16[320,320]{1,0:T(8,128)(2,1)S(1)} %fusion.198) | copy-start | bytes 614404
  35.2 11.6 slice-start.6
  35.2 11.6 slice-start.8
  46.9 6.8 slice-start
  46.9 6.8 slice-start.1
  153.6 123.2 %all-to-all-start = ((bf16[2,320,32,128]{3,2,0,1:T(8,128)(2,1)}), bf16[2,320,32,128]{3,2,0,1:T(8,128)(2,1)}, u32[]{:S(2)}, u32[]{:S(2)}) async-start(bf16[2,320,32,128]{3,2,0,1:T(8,128)(2,1)} %copy.136), calls=%async_computation | async-start | bytes 10485760 | tf_op jit(solution)/shard_map/all_to_all | solution.py:83
  276.8 6.7 copy-start.10
  289.2 120.0 %all-to-all-start.1 = ((bf16[2,320,32,128]{3,2,0,1:T(8,128)(2,1)}), bf16[2,320,32,128]{3,2,0,1:T(8,128)(2,1)}, u32[]{:S(2)}, u32[]{:S(2)}) async-start(bf16[2,320,32,128]{3,2,0,1:T(8,128)(2,1)} %copy.145), calls=%async_computation.1 | async-start | bytes 10485760 | tf_op jit(solution)/shard_map/all_to_all | solution.py:83
  409.2 6.7 copy-start.11
  421.6 119.7 %all-to-all-start.2 = ((bf16[2,320,32,128]{3,2,0,1:T(8,128)(2,1)}), bf16[2,320,32,128]{3,2,0,1:T(8,128)(2,1)}, u32[]{:S(2)}, u32[]{:S(2)}) async-start(bf16[2,320,32,128]{3,2,0,1:T(8,128)(2,1)} %copy.148), calls=%async_computation.2 | async-start | bytes 10485760 | tf_op jit(solution)/shard_map/all_to_all | solution.py:83
  541.3 6.6 copy-start.12
  553.6 119.8 %all-to-all-start.3 = ((bf16[2,320,32,128]{3,2,0,1:T(8,128)(2,1)}), bf16[2,320,32,128]{3,2,0,1:T(8,128)(2,1)}, u32[]{:S(2)}, u32[]{:S(2)}) async-start(bf16[2,320,32,128]{3,2,0,1:T(8,128)(2,1)} %copy.151), calls=%async_computation.3 | async-start | bytes 10485760 | tf_op jit(solution)/shard_map/all_to_all | solution.py:83
  565.6 9.0 copy-start.26
  590.1 5.4 copy-start.4
  619.2 5.5 copy-start.2
  693.7 5.3 copy-start.7
  693.7 120.2 %all-to-all-start.4 = ((bf16[2,40,256,128]{3,0,1,2:T(2,128)(2,1)}), bf16[2,40,256,128]{3,0,1,2:T(2,128)(2,1)}, u32[]{:S(2)}, u32[]{:S(2)}) async-start(bf16[2,40,256,128]{3,0,1,2:T(2,128)(2,1)} %copy.158), calls=%async_computation.4 | async-start | bytes 10485760 | tf_op jit(solution)/shard_map/all_to_all | solution.py:87
  835.2 119.8 %all-to-all-start.5 = ((bf16[2,40,256,128]{3,0,1,2:T(2,128)(2,1)}), bf16[2,40,256,128]{3,0,1,2:T(2,128)(2,1)}, u32[]{:S(2)}, u32[]{:S(2)}) async-start(bf16[2,40,256,128]{3,0,1,2:T(2,128)(2,1)} %copy.169), calls=%async_computation.5 | async-start | bytes 10485760 | tf_op jit(solution)/shard_map/all_to_all | solution.py:87
  850.7 5.4 copy-start.3
  976.3 119.7 %all-to-all-start.6 = ((bf16[2,40,256,128]{3,0,1,2:T(2,128)(2,1)}), bf16[2,40,256,128]{3,0,1,2:T(2,128)(2,1)}, u32[]{:S(2)}, u32[]{:S(2)}) async-start(bf16[2,40,256,128]{3,0,1,2:T(2,128)(2,1)} %copy.180), calls=%async_computation.7 | async-start | bytes 10485760 | tf_op jit(solution)/shard_map/all_to_all | solution.py:87
  1112.1 6.1 copy-start.23
  1112.1 6.1 copy-start.25
  1118.2 38.7 %slice-start.3 = ((s8[5242880]{0:T(1024)(128)(4,1)}), s8[1048576]{0:T(1024)(128)(4,1)S(1)}, s32[]{:S(2)}) async-start(s8[5242880]{0:T(1024)(128)(4,1)} %bitcast.163), calls=%async_computation.15 | async-start | bytes 2097152
  1134.2 22.7 %slice-start.4 = ((s8[5242880]{0:T(1024)(128)(4,1)}), s8[4194304]{0:T(1024)(128)(4,1)S(1)}, s32[]{:S(2)}) async-start(s8[5242880]{0:T(1024)(128)(4,1)} %bitcast.163), calls=%async_computation.16 | async-start | bytes 8388608
  1176.2 119.8 %all-to-all-start.7 = ((bf16[2,40,256,128]{3,0,1,2:T(2,128)(2,1)}), bf16[2,40,256,128]{3,0,1,2:T(2,128)(2,1)}, u32[]{:S(2)}, u32[]{:S(2)}) async-start(bf16[2,40,256,128]{3,0,1,2:T(2,128)(2,1)} %copy.187), calls=%async_computation.8 | async-start | bytes 10485760 | tf_op jit(solution)/shard_map/all_to_all | solution.py:87
  1181.1 171.5 %reduce-scatter.3.cloned.1.call-start = ((), (), s32[]{:S(2)}) async-start(), calls=%async_computation.10 | async-start | bytes 6553600 | tf_op jit(solution)/shard_map/reduce_scatter | solution.py:140
  1181.8 221.3 %reduce-scatter.5.cloned.1.call-start = ((), (), s32[]{:S(2)}) async-start(), calls=%async_computation.11 | async-start | bytes 6553600 | tf_op jit(solution)/shard_map/reduce_scatter | solution.py:140
  (14 other events, 48.8 us)
Sparse Core Ops, SparseCore 0:
  1184.5 52.6 reduce-scatter.2
  1352.7 50.4 reduce-scatter.4

commit v6 on v4

--- a/solution.py
+++ b/solution.py
@@ -120,9 +120,9 @@
                 adjoint_z = after(adjoint_z, previous)
             part = backward_y(to_z_slabs(adjoint_z), chunk_real, chunk_imag, y_back)
             total = part if total is None else total + part
-        summed = lax.psum_scatter(total, "coil", scatter_dimension=0, tiled=True)
+        summed = lax.psum_scatter(total.astype(BF16), "coil", scatter_dimension=0, tiled=True)
         previous = summed
-        outputs.append(summed.astype(BF16))
+        outputs.append(summed)
     return jnp.stack(outputs)
 
 

time: 1370 us -> 1260 us (0.920)
  waiting for transfers between devices: 510 us -> 412 us
    all_to_all x3, waiting for transfers between devices: 194 us -> 152 us  [to_z_slabs(): lax.all_to_all(values, 'slab', split_axis=2, concat_axis=1, tiled=True)]
    all_to_all x4, waiting for transfers between devices: 267 us -> 227 us  [to_ky_blocks(): lax.all_to_all(values, 'slab', split_axis=1, concat_axis=2, tiled=True)]
    reduce_scatter x2, waiting for transfers between devices: 49.2 us -> 33.8 us  [shards(): lax.psum_scatter(total.astype(BF16), 'coil', scatter_dimension=0, tiled=T...]
    unnamed x78 -> x80, local copies, waits for them, and re-layouts: 44.6 us -> 43.3 us
  transfers between devices with their start and end apart: 9 -> 9, of which waited for: 8 -> 8; matrix products, arithmetic and copies ran while one was open for 27% -> 36% of each run, Pallas kernels for 0% -> 0%
where the time goes in v6:
time: 1260 us; the launch traced here: 1250 us
  waiting for transfers between devices  412 us (33%)
  local copies, waits for them, and re-layouts  283 us (22%)
  other arithmetic  228 us (18%)
  matrix products  158 us (13%)
  blocking collectives  120 us (10%)
  starting transfers between devices  36.3 us (3%)
  between operations  14.3 us (1%)
    all_to_all x4, waiting for transfers between devices, to_ky_blocks(): lax.all_to_all(values, 'slab', split_axis=1, concat_axis=2, tiled=True)  227 us
    all_to_all x3, waiting for transfers between devices, to_z_slabs(): lax.all_to_all(values, 'slab', split_axis=2, concat_axis=1, tiled=True)  152 us
    all_to_all x1, blocking collectives, to_z_slabs(): lax.all_to_all(values, 'slab', split_axis=2, concat_axis=1, tiled=True)  120 us
    neg x17, other arithmetic, turned(): return jnp.concatenate([-values[..., half:], values[..., :half]], axis=-1)  97.3 us
    dot_general x4, matrix products, backward_y(): jnp.einsum('yk,ckzl->cyzl', y_back, with_turned(returned, 1), preferred_e...  68.1 us
    all_to_all x12, local copies, waits for them, and re-layouts, to_z_slabs(): lax.all_to_all(values, 'slab', split_axis=2, concat_axis=1, tiled=True)  62 us
    all_to_all x8, local copies, waits for them, and re-layouts, to_ky_blocks(): lax.all_to_all(values, 'slab', split_axis=1, concat_axis=2, tiled=True)  57.7 us
    reduce_sum x3, other arithmetic, backward_y(): return jnp.sum(sens_real * coil_back - sens_imag * turned_back, axis=0)  56 us
  transfers between devices with their start and end apart: 9, of which 8 were waited for; matrix products, arithmetic and copies ran while one was open for 36% of the time, Pallas kernels for 0%

profile of v6, /device:TPU:0, one launch (start us, length us, event | category | flops | bytes accessed | tf_op | source)
XLA Modules:
  0.0 1251.5 jit_solution(13018492210112098461)
XLA Ops:
  16.0 8.7 slice_negate_fusion.2
  53.6 9.3 fusion.220
  62.9 12.0 copy.209
  75.0 11.9 copy.210
  86.9 32.2 %fusion.9 = (bf16[2,320,32,128]{3,1,2,0:T(8,128)(2,1)}, bf16[2,320,32,128]{3,1,2,0:T(8,128)(2,1)}, bf16[2,320,32,128]{3,1,2,0:T(8,128)(2,1)}, bf16[2,320,32,128]...) fusion(f32[320,32,128]{2,0,1:T(8,128)} %copy.135, ...), kind=kLoop, calls=%fused_computation.25 | loop fusion | flops 73400320 | bytes 62914560 | tf_op jit(solution)/shard_map/convert_element_type | solution.py:44
  119.1 10.1 slice_negate_fusion.3
  129.2 8.8 convert_bitcast_fusion.5
  151.0 9.9 slice_negate_fusion.1
  175.2 91.5 %all-to-all-done.2 = bf16[2,320,32,128]{3,2,0,1:T(8,128)(2,1)} async-done(((bf16[2,320,32,128]{3,2,0,1:T(8,128)(2,1)}), bf16[2,320,32,128]{3,2,0,1:T(8,128)(2,1)}, u32[]{:S(2)}, u32[]{:S(2)}) %all-to-all-start.2) | async-done | bytes 5242912 | tf_op jit(solution)/shard_map/all_to_all | solution.py:83
  271.6 10.0 fusion.1
  281.7 9.9 slice_negate_fusion.4
  291.6 8.7 convert_bitcast_fusion.7
  306.0 80.6 %all-to-all-done.4 = bf16[2,320,32,128]{3,2,0,1:T(8,128)(2,1)} async-done(((bf16[2,320,32,128]{3,2,0,1:T(8,128)(2,1)}), bf16[2,320,32,128]{3,2,0,1:T(8,128)(2,1)}, u32[]{:S(2)}, u32[]{:S(2)}) %all-to-all-start.4) | async-done | bytes 5242912 | tf_op jit(solution)/shard_map/all_to_all | solution.py:83
  445.5 13.8 %copy.157 = bf16[2,40,256,128]{3,0,1,2:T(2,128)(2,1)} copy(bf16[2,40,256,128]{2,3,0,1:T(8,128)(2,1)} %convert_bitcast_fusion.4) | data formatting | bytes 10485760 | tf_op jit(solution)/shard_map/convert_element_type | solution.py:69
  459.2 47.3 %all-to-all-done = bf16[2,320,32,128]{3,2,0,1:T(8,128)(2,1)} async-done(((bf16[2,320,32,128]{3,2,0,1:T(8,128)(2,1)}), bf16[2,320,32,128]{3,2,0,1:T(8,128)(2,1)}, u32[]{:S(2)}, u32[]{:S(2)}) %all-to-all-start) | async-done | bytes 5242912 | tf_op jit(solution)/shard_map/all_to_all | solution.py:83
  556.1 13.7 %copy.173 = bf16[2,40,256,128]{3,0,1,2:T(2,128)(2,1)} copy(bf16[2,40,256,128]{2,3,0,1:T(8,128)(2,1)} %convert_bitcast_fusion.2) | data formatting | bytes 10485760 | tf_op jit(solution)/shard_map/convert_element_type | solution.py:69
  569.9 56.4 %all-to-all-done.3 = bf16[2,40,256,128]{3,0,1,2:T(2,128)(2,1)} async-done(((bf16[2,40,256,128]{3,0,1,2:T(2,128)(2,1)}), bf16[2,40,256,128]{3,0,1,2:T(2,128)(2,1)}, u32[]{:S(2)}, u32[]{:S(2)}) %all-to-all-start.3) | async-done | bytes 5242912 | tf_op jit(solution)/shard_map/all_to_all | solution.py:87
  669.1 13.8 %copy.143 = bf16[2,40,256,128]{3,0,1,2:T(2,128)(2,1)} copy(bf16[2,40,256,128]{2,3,0,1:T(8,128)(2,1)} %convert_bitcast_fusion.6) | data formatting | bytes 10485760 | tf_op jit(solution)/shard_map/convert_element_type | solution.py:69
  682.9 62.9 %all-to-all-done.5 = bf16[2,40,256,128]{3,0,1,2:T(2,128)(2,1)} async-done(((bf16[2,40,256,128]{3,0,1,2:T(2,128)(2,1)}), bf16[2,40,256,128]{3,0,1,2:T(2,128)(2,1)}, u32[]{:S(2)}, u32[]{:S(2)}) %all-to-all-start.5) | async-done | bytes 5242912 | tf_op jit(solution)/shard_map/all_to_all | solution.py:87
  771.9 16.8 %fusion.94 = f32[2,640,32,128]{3,1,2,0:T(8,128)} fusion(bf16[2,320,32,64]{1,3,2,0:T(8,128)(2,1)} %get-tuple-element.29, bf16[2,320,32,64]{1,3,2,0:T(8,128)(2,1)S(1)} %get-tuple-element.28, bf16[2,320,32,128]{1,3,2,0:T(8,128)(2,1)} %copy.162, bf16[320,320]{1,0:T(8,128)(2,1)} %copy-done.21, bf16[320,320]{1,0:T(8,128)(2,1)} %copy-done.23, ...), kind=kOutput, calls=%fused_computation.110 | convolution fusion | flops 6745620480 | bytes 32071680 | tf_op jit(solution)/shard_map/yk,ckzl->cyzl/dot_general | solution.py:74
  788.7 20.2 %fusion.11 = (f32[320,32,128]{2,0,1:T(8,128)}, bf16[2,320,32,128]{3,1,2,0:T(8,128)(2,1)}) fusion(bf16[2,320,32,128]{3,1,2,0:T(8,128)(2,1)} %get-tuple-element.11, bf16[2,320,32,128]{3,1,2,0:T(8,128)(2,1)} %get-tuple-element.10, f32[2,640,32,128]{3,1,2,0:T(8,128)} %fusion.94, f32[320,32,128]{2,0,1:T(8,128)} %copy.165, f32[320,32,128]{2,0,1:T(8,128)} %copy.164), kind=kLoop, calls=%fused_computation.27 | loop fusion | flops 24903680 | bytes 52428800 | tf_op jit(solution)/shard_map/reduce_sum | solution.py:79
  808.9 10.0 slice_negate_fusion
  833.3 32.4 %all-to-all-done.1 = bf16[2,40,256,128]{3,0,1,2:T(2,128)(2,1)} async-done(((bf16[2,40,256,128]{3,0,1,2:T(2,128)(2,1)}), bf16[2,40,256,128]{3,0,1,2:T(2,128)(2,1)}, u32[]{:S(2)}, u32[]{:S(2)}) %all-to-all-start.1) | async-done | bytes 5242912 | tf_op jit(solution)/shard_map/all_to_all | solution.py:87
  877.9 8.7 copy.178
  911.2 16.8 %fusion.91 = f32[2,640,32,128]{3,1,2,0:T(8,128)} fusion(bf16[2,320,32,64]{1,3,2,0:T(8,128)(2,1)} %get-tuple-element.31, bf16[2,320,32,64]{1,3,2,0:T(8,128)(2,1)S(1)} %get-tuple-element.30, bf16[2,320,32,128]{1,3,2,0:T(8,128)(2,1)} %copy.178, bf16[320,320]{1,0:T(8,128)(2,1)} %copy-done.21, bf16[320,320]{1,0:T(8,128)(2,1)} %copy-done.23, ...), kind=kOutput, calls=%fused_computation.109 | convolution fusion | flops 6745620480 | bytes 32071680 | tf_op jit(solution)/shard_map/yk,ckzl->cyzl/dot_general | solution.py:74
  928.0 17.7 %fusion.97 = f32[2,640,32,128]{3,1,2,0:T(8,128)} fusion(bf16[2,320,32,64]{1,3,2,0:T(8,128)(2,1)} %get-tuple-element.33, bf16[2,320,32,64]{1,3,2,0:T(8,128)(2,1)} %get-tuple-element.32, bf16[2,320,32,128]{1,3,2,0:T(8,128)(2,1)} %copy.148, bf16[320,320]{1,0:T(8,128)(2,1)} %copy-done.21, bf16[320,320]{1,0:T(8,128)(2,1)} %copy-done.23, ...), kind=kOutput, calls=%fused_computation.111 | convolution fusion | flops 6745620480 | bytes 32071680 | tf_op jit(solution)/shard_map/yk,ckzl->cyzl/dot_general | solution.py:74
  945.7 22.7 %fusion.3 = (f32[320,32,128]{2,0,1:T(8,128)}, f32[320,32,128]{2,0,1:T(8,128)}) fusion(bf16[2,320,32,128]{3,1,2,0:T(8,128)(2,1)} %get-tuple-element.17, bf16[2,320,32,128]{3,1,2,0:T(8,128)(2,1)} %get-tuple-element.16, f32[2,640,32,128]{3,1,2,0:T(8,128)} %fusion.97, f32[2,640,32,128]{3,1,2,0:T(8,128)} %fusion.91), kind=kLoop, calls=%fused_computation.19 | loop fusion | flops 23592960 | bytes 62914560 | tf_op jit(solution)/shard_map/reduce_sum | solution.py:79
  1021.0 13.7 %copy.187 = bf16[2,40,256,128]{3,0,1,2:T(2,128)(2,1)} copy(bf16[2,40,256,128]{2,3,0,1:T(8,128)(2,1)} %convert_bitcast_fusion) | data formatting | bytes 10485760 | tf_op jit(solution)/shard_map/optimization_barrier | solution.py:93
  1034.7 119.7 %all_to_all.144 = bf16[2,40,256,128]{3,0,1,2:T(2,128)(2,1)S(1)} all-to-all(bf16[2,40,256,128]{3,0,1,2:T(2,128)(2,1)} %copy.187), channel_id=1, replica_groups=mesh['slab'=8,'coil'=4] {'slab'}, dimensions={2} | all-to-all | bytes 10485760 | tf_op jit(solution)/shard_map/all_to_all | solution.py:87
  1173.0 16.8 %fusion.88 = f32[2,640,32,128]{3,1,2,0:T(8,128)} fusion(bf16[2,320,32,64]{1,3,2,0:T(8,128)(2,1)} %get-tuple-element.27, bf16[2,320,32,64]{1,3,2,0:T(8,128)(2,1)S(1)} %get-tuple-element.26, bf16[2,320,32,128]{1,3,2,0:T(8,128)(2,1)} %copy.192, bf16[320,320]{1,0:T(8,128)(2,1)} %copy-done.21, bf16[320,320]{1,0:T(8,128)(2,1)} %copy-done.23, ...), kind=kOutput, calls=%fused_computation.108 | convolution fusion | flops 6745620480 | bytes 32071680 | tf_op jit(solution)/shard_map/yk,ckzl->cyzl/dot_general | solution.py:74
  1189.8 13.1 %fusion.15 = f32[320,32,128]{2,0,1:T(8,128)S(1)} fusion(bf16[2,320,32,128]{3,1,2,0:T(8,128)(2,1)} %get-tuple-element.11, bf16[2,320,32,128]{3,1,2,0:T(8,128)(2,1)} %get-tuple-element.10, f32[2,640,32,128]{3,1,2,0:T(8,128)} %fusion.88), kind=kLoop, calls=%fused_computation.31 | loop fusion | flops 14417920 | bytes 36700160 | tf_op jit(solution)/shard_map/reduce_sum | solution.py:79
  1207.8 33.8 %reduce-scatter.5.cloned.1.call-done = bf16[80,32,128]{2,0,1:T(8,128)(2,1)} async-done(((bf16[320,32,128]{2,0,1:T(8,128)(2,1)}), bf16[80,32,128]{2,0,1:T(8,128)(2,1)}) %reduce-scatter.5.cloned.1.call-update) | async-done | bytes 655376 | tf_op jit(solution)/shard_map/reduce_scatter | solution.py:123
  (162 shorter events, 383.3 us)
Async XLA Ops:
  24.7 10.5 copy-start.1
  24.7 10.5 copy-start.2
  30.1 16.6 %slice-start.5 = ((s8[5242880]{0:T(1024)(128)(4,1)}), s8[4194304]{0:T(1024)(128)(4,1)S(1)}, s32[]{:S(2)}) async-start(s8[5242880]{0:T(1024)(128)(4,1)} %bitcast.158), calls=%async_computation.17 | async-start | bytes 8388608
  30.1 16.6 %slice-start.7 = ((s8[5242880]{0:T(1024)(128)(4,1)}), s8[4194304]{0:T(1024)(128)(4,1)S(1)}, s32[]{:S(2)}) async-start(s8[5242880]{0:T(1024)(128)(4,1)} %bitcast.160), calls=%async_computation.19 | async-start | bytes 8388608
  33.0 258.6 %copy-start.21 = (bf16[320,320]{1,0:T(8,128)(2,1)}, bf16[320,320]{1,0:T(8,128)(2,1)S(1)}, u32[]{:S(2)}) copy-start(bf16[320,320]{1,0:T(8,128)(2,1)S(1)} %get-tuple-element.75) | copy-start | bytes 614404
  35.2 256.5 %copy-start.23 = (bf16[320,320]{1,0:T(8,128)(2,1)}, bf16[320,320]{1,0:T(8,128)(2,1)S(1)}, u32[]{:S(2)}) copy-start(bf16[320,320]{1,0:T(8,128)(2,1)S(1)} %fusion.198) | copy-start | bytes 614404
  35.2 11.6 slice-start.6
  35.2 11.6 slice-start.8
  46.8 6.8 slice-start
  46.8 6.8 slice-start.1
  143.7 123.0 %all-to-all-start.2 = ((bf16[2,320,32,128]{3,2,0,1:T(8,128)(2,1)}), bf16[2,320,32,128]{3,2,0,1:T(8,128)(2,1)}, u32[]{:S(2)}, u32[]{:S(2)}) async-start(bf16[2,320,32,128]{3,2,0,1:T(8,128)(2,1)} %copy.150), calls=%async_computation.2 | async-start | bytes 10485760 | tf_op jit(solution)/shard_map/all_to_all | solution.py:83
  266.8 119.8 %all-to-all-start.4 = ((bf16[2,320,32,128]{3,2,0,1:T(8,128)(2,1)}), bf16[2,320,32,128]{3,2,0,1:T(8,128)(2,1)}, u32[]{:S(2)}, u32[]{:S(2)}) async-start(bf16[2,320,32,128]{3,2,0,1:T(8,128)(2,1)} %copy.166), calls=%async_computation.5 | async-start | bytes 10485760 | tf_op jit(solution)/shard_map/all_to_all | solution.py:83
  386.6 120.0 %all-to-all-start = ((bf16[2,320,32,128]{3,2,0,1:T(8,128)(2,1)}), bf16[2,320,32,128]{3,2,0,1:T(8,128)(2,1)}, u32[]{:S(2)}, u32[]{:S(2)}) async-start(bf16[2,320,32,128]{3,2,0,1:T(8,128)(2,1)} %copy.136), calls=%async_computation | async-start | bytes 10485760 | tf_op jit(solution)/shard_map/all_to_all | solution.py:83
  403.4 136.9 %copy-start.26 = (pred[40,128]{1,0:T(8,128)(4,1)}, pred[40,128]{1,0:T(8,128)(4,1)S(1)}, u32[]{:S(2)}) copy-start(pred[40,128]{1,0:T(8,128)(4,1)S(1)} %get-tuple-element.68) | copy-start | bytes 15364
  424.3 5.3 copy-start.5
  459.2 52.1 %copy-start.8 = (bf16[1,2,40,128,128]{4,3,2,1,0:T(8,128)(2,1)S(1)}, bf16[1,2,40,128,128]{4,3,2,1,0:T(8,128)(2,1)}, u32[]{:S(2)}) copy-start(bf16[1,2,40,128,128]{4,3,2,1,0:T(8,128)(2,1)} %get-tuple-element.21) | copy-start | bytes 7864324
  506.5 119.7 %all-to-all-start.3 = ((bf16[2,40,256,128]{3,0,1,2:T(2,128)(2,1)}), bf16[2,40,256,128]{3,0,1,2:T(2,128)(2,1)}, u32[]{:S(2)}, u32[]{:S(2)}) async-start(bf16[2,40,256,128]{3,0,1,2:T(2,128)(2,1)} %copy.157), calls=%async_computation.3 | async-start | bytes 10485760 | tf_op jit(solution)/shard_map/all_to_all | solution.py:87
  534.8 5.5 copy-start.6
  569.8 61.1 %copy-start.7 = (bf16[1,2,40,128,128]{4,3,2,1,0:T(8,128)(2,1)S(1)}, bf16[1,2,40,128,128]{4,3,2,1,0:T(8,128)(2,1)}, u32[]{:S(2)}) copy-start(bf16[1,2,40,128,128]{4,3,2,1,0:T(8,128)(2,1)} %get-tuple-element.22) | copy-start | bytes 7864324
  626.3 119.6 %all-to-all-start.5 = ((bf16[2,40,256,128]{3,0,1,2:T(2,128)(2,1)}), bf16[2,40,256,128]{3,0,1,2:T(2,128)(2,1)}, u32[]{:S(2)}, u32[]{:S(2)}) async-start(bf16[2,40,256,128]{3,0,1,2:T(2,128)(2,1)} %copy.173), calls=%async_computation.6 | async-start | bytes 10485760 | tf_op jit(solution)/shard_map/all_to_all | solution.py:87
  648.0 5.3 copy-start.3
  745.9 119.8 %all-to-all-start.1 = ((bf16[2,40,256,128]{3,0,1,2:T(2,128)(2,1)}), bf16[2,40,256,128]{3,0,1,2:T(2,128)(2,1)}, u32[]{:S(2)}, u32[]{:S(2)}) async-start(bf16[2,40,256,128]{3,0,1,2:T(2,128)(2,1)} %copy.143), calls=%async_computation.1 | async-start | bytes 10485760 | tf_op jit(solution)/shard_map/all_to_all | solution.py:87
  808.9 10.0 copy-start.22
  808.9 10.0 copy-start.24
  865.6 119.6 %all-to-all-start.6 = ((bf16[2,320,32,128]{3,2,0,1:T(8,128)(2,1)}), bf16[2,320,32,128]{3,2,0,1:T(8,128)(2,1)}, u32[]{:S(2)}, u32[]{:S(2)}) async-start(bf16[2,320,32,128]{3,2,0,1:T(8,128)(2,1)} %copy.180), calls=%async_computation.7 | async-start | bytes 10485760 | tf_op jit(solution)/shard_map/all_to_all | solution.py:83
  870.3 150.7 %reduce-scatter.3.cloned.1.call-start = ((), (), s32[]{:S(2)}) async-start(), calls=%async_computation.10 | async-start | bytes 3276800 | tf_op jit(solution)/shard_map/reduce_scatter | solution.py:123
  928.0 40.4 %slice-start.3 = ((s8[5242880]{0:T(1024)(128)(4,1)}), s8[1048576]{0:T(1024)(128)(4,1)S(1)}, s32[]{:S(2)}) async-start(s8[5242880]{0:T(1024)(128)(4,1)} %bitcast.156), calls=%async_computation.15 | async-start | bytes 2097152
  945.7 22.7 %slice-start.4 = ((s8[5242880]{0:T(1024)(128)(4,1)}), s8[4194304]{0:T(1024)(128)(4,1)S(1)}, s32[]{:S(2)}) async-start(s8[5242880]{0:T(1024)(128)(4,1)} %bitcast.156), calls=%async_computation.16 | async-start | bytes 8388608
  973.2 268.3 %reduce-scatter.5.cloned.1.call-start = ((), (), s32[]{:S(2)}) async-start(), calls=%async_computation.11 | async-start | bytes 3276800 | tf_op jit(solution)/shard_map/reduce_scatter | solution.py:123
  999.8 5.3 copy-start.4
  999.8 5.3 copy-start.27
  1202.9 38.7 %copy-start.19 = (bf16[80,32,128]{2,0,1:T(8,128)(2,1)S(1)}, bf16[80,32,128]{2,0,1:T(8,128)(2,1)}, u32[]{:S(2)}) copy-start(bf16[80,32,128]{2,0,1:T(8,128)(2,1)} %reduce-scatter.3.cloned.1.call-done) | copy-start | bytes 1966084
  (14 other events, 51.7 us)
Sparse Core Ops, SparseCore 0:
  973.4 35.9 reduce-scatter.2
  1207.9 33.5 reduce-scatter.4

commit v7 on v6

--- a/solution.py
+++ b/solution.py
@@ -106,12 +106,20 @@
     sens_real, sens_imag = dup_halves(coil_maps)
     outputs = []
     previous = None
+    spectrum = None
     for state in range(state_count):
-        pixels = image[state].astype(F32)
         total = None
         for first in range(0, coil_count, group):
-            chunk_real = sens_real[first : first + group].astype(F32)
-            chunk_imag = sens_imag[first : first + group].astype(F32)
+            pixels = image[state]
+            chunk_real = sens_real[first : first + group]
+            chunk_imag = sens_imag[first : first + group]
+            if spectrum is not None:
+                pixels, chunk_real, chunk_imag, _ = lax.optimization_barrier(
+                    (pixels, chunk_real, chunk_imag, spectrum)
+                )
+            pixels = pixels.astype(F32)
+            chunk_real = chunk_real.astype(F32)
+            chunk_imag = chunk_imag.astype(F32)
             spectrum = forward_y(pixels, chunk_real, chunk_imag, y_fwd)
             adjoint_z = middle_z(
                 to_ky_blocks(spectrum), y_data[state, first : first + group], kz_lines[state]

time: 1260 us -> 1240 us (0.984)
  blocking collectives: 120 us -> 0 us
  waiting for transfers between devices: 412 us -> 466 us
  local copies, waits for them, and re-layouts: 283 us -> 305 us
  other arithmetic: 228 us -> 243 us
    all_to_all x1 -> x0, blocking collectives: 120 us -> none  [to_z_slabs(): lax.all_to_all(values, 'slab', split_axis=2, concat_axis=1, tiled=True)]
    all_to_all x3 -> x4, waiting for transfers between devices: 152 us -> 209 us  [to_z_slabs(): lax.all_to_all(values, 'slab', split_axis=2, concat_axis=1, tiled=True)]
    convert_element_type x2 -> x4, other arithmetic: 42.3 us -> 25.4 us  [forward_y(): coil_image = (sens_real * pixels + sens_imag * turned(pixels)).astype(BF16)]
    concatenate x0 -> x1, other arithmetic: none -> 15.4 us  [dup_halves(): jnp.concatenate([imag, imag], axis=-1)]
    neg x17 -> x20, other arithmetic: 97.3 us -> 101 us  [turned(): return jnp.concatenate([-values[..., half:], values[..., :half]], axis=-1)]
    reduce_sum x3 -> x4, other arithmetic: 56 us -> 54.3 us  [backward_y(): return jnp.sum(sens_real * coil_back - sens_imag * turned_back, axis=0)]
    unnamed x80 -> x92, local copies, waits for them, and re-layouts: 43.3 us -> 44.5 us
  transfers between devices with their start and end apart: 9 -> 10, of which waited for: 8 -> 8; matrix products, arithmetic and copies ran while one was open for 36% -> 39% of each run, Pallas kernels for 0% -> 0%
where the time goes in v7:
time: 1240 us; the launch traced here: 1230 us
  waiting for transfers between devices  466 us (38%)
  local copies, waits for them, and re-layouts  305 us (25%)
  other arithmetic  243 us (20%)
  matrix products  162 us (13%)
  starting transfers between devices  42.3 us (3%)
  between operations  14.3 us (1%)
    all_to_all x4, waiting for transfers between devices, to_ky_blocks(): lax.all_to_all(values, 'slab', split_axis=1, concat_axis=2, tiled=True)  223 us
    all_to_all x4, waiting for transfers between devices, to_z_slabs(): lax.all_to_all(values, 'slab', split_axis=2, concat_axis=1, tiled=True)  209 us
    neg x20, other arithmetic, turned(): return jnp.concatenate([-values[..., half:], values[..., :half]], axis=-1)  101 us
    dot_general x4, matrix products, backward_y(): jnp.einsum('yk,ckzl->cyzl', y_back, with_turned(returned, 1), preferred_e...  68.4 us
    all_to_all x12, local copies, waits for them, and re-layouts, to_z_slabs(): lax.all_to_all(values, 'slab', split_axis=2, concat_axis=1, tiled=True)  64.9 us
    all_to_all x8, local copies, waits for them, and re-layouts, to_ky_blocks(): lax.all_to_all(values, 'slab', split_axis=1, concat_axis=2, tiled=True)  57.8 us
    reduce_sum x4, other arithmetic, backward_y(): return jnp.sum(sens_real * coil_back - sens_imag * turned_back, axis=0)  54.3 us
    unnamed x92, local copies, waits for them, and re-layouts  44.5 us
  transfers between devices with their start and end apart: 10, of which 8 were waited for; matrix products, arithmetic and copies ran while one was open for 39% of the time, Pallas kernels for 0%

profile of v7, /device:TPU:0, one launch (start us, length us, event | category | flops | bytes accessed | tf_op | source)
XLA Modules:
  0.0 1232.7 jit_solution(8502725904986862148)
XLA Ops:
  35.9 9.1 fusion.221
  45.1 12.0 copy.225
  57.1 11.9 copy.226
  69.0 15.4 %pad_maximum_fusion = (bf16[2,320,32,128]{3,1,2,0:T(8,128)(2,1)}, bf16[2,320,32,128]{3,1,2,0:T(8,128)(2,1)}) fusion(bf16[4,320,32,64]{3,1,2,0:T(8,128)(2,1)} %copy.226, bf16[4,320,32,64]{3,1,2,0:T(8,128)(2,1)} %copy.225), kind=kLoop, calls=%fused_computation.120 | loop fusion | flops 20971520 | bytes 20971520 | tf_op jit(solution)/shard_map/concatenate | solution.py:35
  85.9 13.1 %fusion.1 = (bf16[2,320,32,128]{3,1,2,0:T(8,128)(2,1)}, bf16[2,320,32,128]{3,1,2,0:T(8,128)(2,1)}, bf16[2,320,32,128]{3,1,2,0:T(8,128)(2,1)}) fusion(f32[320,32,128]{2,0,1:T(8,128)} %copy.147, f32[320,32,128]{2,0,1:T(8,128)} %copy.145, bf16[4,320,32,64]{3,1,2,0:T(8,128)(2,1)S(1)} %copy-done.1, bf16[4,320,32,64]{3,1,2,0:T(8,128)(2,1)S(1)} %copy-done), kind=kLoop, calls=%fused_computation.17 | loop fusion | flops 36700160 | bytes 36700160 | tf_op jit(solution)/shard_map/convert_element_type | solution.py:44
  99.0 10.0 slice_negate_fusion.6
  108.9 10.7 convert_bitcast_fusion.7
  144.0 10.0 slice_negate_fusion.4
  183.9 107.6 %all-to-all-done.2 = bf16[2,320,32,128]{3,2,0,1:T(8,128)(2,1)} async-done(((bf16[2,320,32,128]{3,2,0,1:T(8,128)(2,1)}), bf16[2,320,32,128]{3,2,0,1:T(8,128)(2,1)}, u32[]{:S(2)}, u32[]{:S(2)}) %all-to-all-start.2) | async-done | bytes 5242912 | tf_op jit(solution)/shard_map/all_to_all | solution.py:83
  316.4 9.9 slice_negate_fusion.2
  340.9 70.6 %all-to-all-done = bf16[2,320,32,128]{3,2,0,1:T(8,128)(2,1)} async-done(((bf16[2,320,32,128]{3,2,0,1:T(8,128)(2,1)}), bf16[2,320,32,128]{3,2,0,1:T(8,128)(2,1)}, u32[]{:S(2)}, u32[]{:S(2)}) %all-to-all-start) | async-done | bytes 5242912 | tf_op jit(solution)/shard_map/all_to_all | solution.py:83
  472.5 13.8 %copy.171 = bf16[2,40,256,128]{3,0,1,2:T(2,128)(2,1)} copy(bf16[2,40,256,128]{2,3,0,1:T(8,128)(2,1)} %convert_bitcast_fusion.4) | data formatting | bytes 10485760 | tf_op jit(solution)/shard_map/convert_element_type | solution.py:69
  486.3 44.8 %all-to-all-done.4 = bf16[2,320,32,128]{3,2,0,1:T(8,128)(2,1)} async-done(((bf16[2,320,32,128]{3,2,0,1:T(8,128)(2,1)}), bf16[2,320,32,128]{3,2,0,1:T(8,128)(2,1)}, u32[]{:S(2)}, u32[]{:S(2)}) %all-to-all-start.4) | async-done | bytes 5242912 | tf_op jit(solution)/shard_map/all_to_all | solution.py:83
  576.1 13.8 %copy.155 = bf16[2,40,256,128]{3,0,1,2:T(2,128)(2,1)} copy(bf16[2,40,256,128]{2,3,0,1:T(8,128)(2,1)} %convert_bitcast_fusion.6) | data formatting | bytes 10485760 | tf_op jit(solution)/shard_map/convert_element_type | solution.py:69
  589.9 60.7 %all-to-all-done.3 = bf16[2,40,256,128]{3,0,1,2:T(2,128)(2,1)} async-done(((bf16[2,40,256,128]{3,0,1,2:T(2,128)(2,1)}), bf16[2,40,256,128]{3,0,1,2:T(2,128)(2,1)}, u32[]{:S(2)}, u32[]{:S(2)}) %all-to-all-start.3) | async-done | bytes 5242912 | tf_op jit(solution)/shard_map/all_to_all | solution.py:87
  675.5 10.0 slice_negate_fusion
  685.5 8.9 convert_bitcast_fusion.1
  700.0 70.6 %all-to-all-done.1 = bf16[2,40,256,128]{3,0,1,2:T(2,128)(2,1)} async-done(((bf16[2,40,256,128]{3,0,1,2:T(2,128)(2,1)}), bf16[2,40,256,128]{3,0,1,2:T(2,128)(2,1)}, u32[]{:S(2)}, u32[]{:S(2)}) %all-to-all-start.1) | async-done | bytes 5242912 | tf_op jit(solution)/shard_map/all_to_all | solution.py:87
  820.0 13.9 %copy.187 = bf16[2,40,256,128]{3,0,1,2:T(2,128)(2,1)} copy(bf16[2,40,256,128]{2,3,0,1:T(8,128)(2,1)} %convert_bitcast_fusion.2) | data formatting | bytes 10485760 | tf_op jit(solution)/shard_map/convert_element_type | solution.py:69
  857.5 9.1 copy.160
  875.2 17.7 %fusion.94 = f32[2,640,32,128]{3,1,2,0:T(8,128)} fusion(bf16[2,320,32,64]{1,3,2,0:T(8,128)(2,1)} %get-tuple-element.37, bf16[2,320,32,64]{1,3,2,0:T(8,128)(2,1)} %get-tuple-element.36, bf16[2,320,32,128]{1,3,2,0:T(8,128)(2,1)} %copy.176, bf16[320,320]{1,0:T(8,128)(2,1)} %copy-done.23, bf16[320,320]{1,0:T(8,128)(2,1)} %copy-done.24, ...), kind=kOutput, calls=%fused_computation.110 | convolution fusion | flops 6745620480 | bytes 32071680 | tf_op jit(solution)/shard_map/yk,ckzl->cyzl/dot_general | solution.py:74
  898.9 14.0 %fusion.7 = f32[320,32,128]{2,0,1:T(8,128)} fusion(bf16[2,320,32,128]{3,1,2,0:T(8,128)(2,1)} %get-tuple-element.21, bf16[2,320,32,128]{3,1,2,0:T(8,128)(2,1)} %get-tuple-element.23, f32[2,640,32,128]{3,1,2,0:T(8,128)} %fusion.94), kind=kLoop, calls=%fused_computation.23 | loop fusion | flops 14417920 | bytes 36700160 | tf_op jit(solution)/shard_map/reduce_sum | solution.py:79
  912.8 16.8 %fusion.97 = f32[2,640,32,128]{3,1,2,0:T(8,128)} fusion(bf16[2,320,32,64]{1,3,2,0:T(8,128)(2,1)} %get-tuple-element.39, bf16[2,320,32,64]{1,3,2,0:T(8,128)(2,1)S(1)} %get-tuple-element.38, bf16[2,320,32,128]{1,3,2,0:T(8,128)(2,1)} %copy.160, bf16[320,320]{1,0:T(8,128)(2,1)} %copy-done.23, bf16[320,320]{1,0:T(8,128)(2,1)} %copy-done.24, ...), kind=kOutput, calls=%fused_computation.111 | convolution fusion | flops 6745620480 | bytes 32071680 | tf_op jit(solution)/shard_map/yk,ckzl->cyzl/dot_general | solution.py:74
  929.7 13.3 %fusion.3 = f32[320,32,128]{2,0,1:T(8,128)S(1)} fusion(bf16[2,320,32,128]{3,1,2,0:T(8,128)(2,1)} %get-tuple-element.18, bf16[2,320,32,128]{3,1,2,0:T(8,128)(2,1)} %get-tuple-element.20, f32[2,640,32,128]{3,1,2,0:T(8,128)} %fusion.97), kind=kLoop, calls=%fused_computation.19 | loop fusion | flops 14417920 | bytes 36700160 | tf_op jit(solution)/shard_map/reduce_sum | solution.py:79
  984.5 13.8 %copy.203 = bf16[2,40,256,128]{3,0,1,2:T(2,128)(2,1)} copy(bf16[2,40,256,128]{2,3,0,1:T(8,128)(2,1)} %convert_bitcast_fusion) | data formatting | bytes 10485760 | tf_op jit(solution)/shard_map/optimization_barrier | solution.py:93
  998.2 15.0 %all-to-all-done.5 = bf16[2,40,256,128]{3,0,1,2:T(2,128)(2,1)} async-done(((bf16[2,40,256,128]{3,0,1,2:T(2,128)(2,1)}), bf16[2,40,256,128]{3,0,1,2:T(2,128)(2,1)}, u32[]{:S(2)}, u32[]{:S(2)}) %all-to-all-start.5) | async-done | bytes 5242912 | tf_op jit(solution)/shard_map/all_to_all | solution.py:87
  1039.2 16.9 %fusion.91 = f32[2,640,32,128]{3,1,2,0:T(8,128)} fusion(bf16[2,320,32,64]{1,3,2,0:T(8,128)(2,1)} %get-tuple-element.41, bf16[2,320,32,64]{1,3,2,0:T(8,128)(2,1)S(1)} %get-tuple-element.40, bf16[2,320,32,128]{1,3,2,0:T(8,128)(2,1)} %copy.192, bf16[320,320]{1,0:T(8,128)(2,1)} %copy-done.23, bf16[320,320]{1,0:T(8,128)(2,1)} %copy-done.24, ...), kind=kOutput, calls=%fused_computation.109 | convolution fusion | flops 6745620480 | bytes 32071680 | tf_op jit(solution)/shard_map/yk,ckzl->cyzl/dot_general | solution.py:74
  1056.0 13.9 %fusion.11 = f32[320,32,128]{2,0,1:T(8,128)} fusion(bf16[2,320,32,128]{3,1,2,0:T(8,128)(2,1)} %get-tuple-element.18, bf16[2,320,32,128]{3,1,2,0:T(8,128)(2,1)} %get-tuple-element.20, f32[2,640,32,128]{3,1,2,0:T(8,128)} %fusion.91), kind=kLoop, calls=%fused_computation.27 | loop fusion | flops 14417920 | bytes 36700160 | tf_op jit(solution)/shard_map/reduce_sum | solution.py:79
  1070.0 62.9 %all-to-all-done.7 = bf16[2,40,256,128]{3,0,1,2:T(2,128)(2,1)} async-done(((bf16[2,40,256,128]{3,0,1,2:T(2,128)(2,1)}), bf16[2,40,256,128]{3,0,1,2:T(2,128)(2,1)}, u32[]{:S(2)}, u32[]{:S(2)}) %all-to-all-start.7) | async-done | bytes 5242912 | tf_op jit(solution)/shard_map/all_to_all | solution.py:87
  1154.1 17.1 %fusion.88 = f32[2,640,32,128]{3,1,2,0:T(8,128)} fusion(bf16[2,320,32,64]{1,3,2,0:T(8,128)(2,1)} %get-tuple-element.35, bf16[2,320,32,64]{1,3,2,0:T(8,128)(2,1)S(1)} %get-tuple-element.34, bf16[2,320,32,128]{1,3,2,0:T(8,128)(2,1)} %copy.208, bf16[320,320]{1,0:T(8,128)(2,1)} %copy-done.23, bf16[320,320]{1,0:T(8,128)(2,1)} %copy-done.24, ...), kind=kOutput, calls=%fused_computation.108 | convolution fusion | flops 6745620480 | bytes 32071680 | tf_op jit(solution)/shard_map/yk,ckzl->cyzl/dot_general | solution.py:74
  1171.1 13.1 %fusion.15 = f32[320,32,128]{2,0,1:T(8,128)S(1)} fusion(bf16[2,320,32,128]{3,1,2,0:T(8,128)(2,1)} %get-tuple-element.21, bf16[2,320,32,128]{3,1,2,0:T(8,128)(2,1)} %get-tuple-element.23, f32[2,640,32,128]{3,1,2,0:T(8,128)} %fusion.88), kind=kLoop, calls=%fused_computation.31 | loop fusion | flops 14417920 | bytes 36700160 | tf_op jit(solution)/shard_map/reduce_sum | solution.py:79
  1189.1 33.9 %reduce-scatter.5.cloned.1.call-done = bf16[80,32,128]{2,0,1:T(8,128)(2,1)} async-done(((bf16[320,32,128]{2,0,1:T(8,128)(2,1)}), bf16[80,32,128]{2,0,1:T(8,128)(2,1)}) %reduce-scatter.5.cloned.1.call-update) | async-done | bytes 655376 | tf_op jit(solution)/shard_map/reduce_scatter | solution.py:131
  (198 shorter events, 444.2 us)
Async XLA Ops:
  24.4 661.0 %copy-start.23 = (bf16[320,320]{1,0:T(8,128)(2,1)}, bf16[320,320]{1,0:T(8,128)(2,1)S(1)}, u32[]{:S(2)}) copy-start(bf16[320,320]{1,0:T(8,128)(2,1)S(1)} %get-tuple-element.82) | copy-start | bytes 614404
  26.4 659.1 %copy-start.24 = (bf16[320,320]{1,0:T(8,128)(2,1)}, bf16[320,320]{1,0:T(8,128)(2,1)S(1)}, u32[]{:S(2)}) copy-start(bf16[320,320]{1,0:T(8,128)(2,1)S(1)} %fusion.198) | copy-start | bytes 614404
  26.4 9.5 slice-start.12
  26.4 9.5 slice-start.13
  69.0 15.4 %copy-start = (bf16[4,320,32,64]{3,1,2,0:T(8,128)(2,1)S(1)}, bf16[4,320,32,64]{3,1,2,0:T(8,128)(2,1)}, u32[]{:S(2)}) copy-start(bf16[4,320,32,64]{3,1,2,0:T(8,128)(2,1)} %copy.225) | copy-start | bytes 15728644
  69.0 16.8 %copy-start.1 = (bf16[4,320,32,64]{3,1,2,0:T(8,128)(2,1)S(1)}, bf16[4,320,32,64]{3,1,2,0:T(8,128)(2,1)}, u32[]{:S(2)}) copy-start(bf16[4,320,32,64]{3,1,2,0:T(8,128)(2,1)} %copy.226) | copy-start | bytes 15728644
  108.9 10.7 copy-start.2
  126.7 13.2 %slice-start = ((s8[5242880]{0:T(1024)(128)(4,1)}), s8[4194304]{0:T(1024)(128)(4,1)S(1)}, s32[]{:S(2)}) async-start(s8[5242880]{0:T(1024)(128)(4,1)} %bitcast.154), calls=%async_computation.12 | async-start | bytes 8388608
  126.7 13.2 %slice-start.4 = ((s8[5242880]{0:T(1024)(128)(4,1)}), s8[4194304]{0:T(1024)(128)(4,1)S(1)}, s32[]{:S(2)}) async-start(s8[5242880]{0:T(1024)(128)(4,1)} %bitcast.158), calls=%async_computation.16 | async-start | bytes 8388608
  126.7 13.2 %slice-start.15 = ((s8[5242880]{0:T(1024)(128)(4,1)}), s8[1048576]{0:T(1024)(128)(4,1)S(1)}, s32[]{:S(2)}) async-start(s8[5242880]{0:T(1024)(128)(4,1)} %bitcast.180), calls=%async_computation.27 | async-start | bytes 2097152
  130.7 9.1 slice-start.16
  168.5 123.0 %all-to-all-start.2 = ((bf16[2,320,32,128]{3,2,0,1:T(8,128)(2,1)}), bf16[2,320,32,128]{3,2,0,1:T(8,128)(2,1)}, u32[]{:S(2)}, u32[]{:S(2)}) async-start(bf16[2,320,32,128]{3,2,0,1:T(8,128)(2,1)} %copy.164), calls=%async_computation.2 | async-start | bytes 10485760 | tf_op jit(solution)/shard_map/all_to_all | solution.py:83
  291.5 120.0 %all-to-all-start = ((bf16[2,320,32,128]{3,2,0,1:T(8,128)(2,1)}), bf16[2,320,32,128]{3,2,0,1:T(8,128)(2,1)}, u32[]{:S(2)}, u32[]{:S(2)}) async-start(bf16[2,320,32,128]{3,2,0,1:T(8,128)(2,1)} %copy.148), calls=%async_computation | async-start | bytes 10485760 | tf_op jit(solution)/shard_map/all_to_all | solution.py:83
  301.2 11.0 slice-start.8
  301.2 11.0 slice-start.10
  302.6 9.6 slice-start.9
  302.7 9.6 slice-start.11
  411.5 119.6 %all-to-all-start.4 = ((bf16[2,320,32,128]{3,2,0,1:T(8,128)(2,1)}), bf16[2,320,32,128]{3,2,0,1:T(8,128)(2,1)}, u32[]{:S(2)}, u32[]{:S(2)}) async-start(bf16[2,320,32,128]{3,2,0,1:T(8,128)(2,1)} %copy.180), calls=%async_computation.5 | async-start | bytes 10485760 | tf_op jit(solution)/shard_map/all_to_all | solution.py:83
  531.0 119.6 %all-to-all-start.3 = ((bf16[2,40,256,128]{3,0,1,2:T(2,128)(2,1)}), bf16[2,40,256,128]{3,0,1,2:T(2,128)(2,1)}, u32[]{:S(2)}, u32[]{:S(2)}) async-start(bf16[2,40,256,128]{3,0,1,2:T(2,128)(2,1)} %copy.171), calls=%async_computation.3 | async-start | bytes 10485760 | tf_op jit(solution)/shard_map/all_to_all | solution.py:87
  650.6 120.0 %all-to-all-start.1 = ((bf16[2,40,256,128]{3,0,1,2:T(2,128)(2,1)}), bf16[2,40,256,128]{3,0,1,2:T(2,128)(2,1)}, u32[]{:S(2)}, u32[]{:S(2)}) async-start(bf16[2,40,256,128]{3,0,1,2:T(2,128)(2,1)} %copy.155), calls=%async_computation.1 | async-start | bytes 10485760 | tf_op jit(solution)/shard_map/all_to_all | solution.py:87
  660.4 10.9 slice-start.2
  660.4 10.9 slice-start.6
  661.8 9.5 slice-start.3
  661.8 9.5 slice-start.7
  700.0 75.4 %copy-start.10 = (bf16[1,2,40,128,128]{4,3,2,1,0:T(8,128)(2,1)S(1)}, bf16[1,2,40,128,128]{4,3,2,1,0:T(8,128)(2,1)}, u32[]{:S(2)}) copy-start(bf16[1,2,40,128,128]{4,3,2,1,0:T(8,128)(2,1)} %get-tuple-element.29) | copy-start | bytes 7864324
  770.6 122.3 %all-to-all-start.6 = ((bf16[2,320,32,128]{3,2,0,1:T(8,128)(2,1)}), bf16[2,320,32,128]{3,2,0,1:T(8,128)(2,1)}, u32[]{:S(2)}, u32[]{:S(2)}) async-start(bf16[2,320,32,128]{3,2,0,1:T(8,128)(2,1)} %copy.196), calls=%async_computation.7 | async-start | bytes 10485760 | tf_op jit(solution)/shard_map/all_to_all | solution.py:83
  892.9 120.4 %all-to-all-start.5 = ((bf16[2,40,256,128]{3,0,1,2:T(2,128)(2,1)}), bf16[2,40,256,128]{3,0,1,2:T(2,128)(2,1)}, u32[]{:S(2)}, u32[]{:S(2)}) async-start(bf16[2,40,256,128]{3,0,1,2:T(2,128)(2,1)} %copy.187), calls=%async_computation.6 | async-start | bytes 10485760 | tf_op jit(solution)/shard_map/all_to_all | solution.py:87
  898.8 85.6 %reduce-scatter.3.cloned.1.call-start = ((), (), s32[]{:S(2)}) async-start(), calls=%async_computation.10 | async-start | bytes 3276800 | tf_op jit(solution)/shard_map/reduce_scatter | solution.py:131
  929.6 13.3 %copy-start.4 = (f32[320,32,128]{2,0,1:T(8,128)S(1)}, f32[320,32,128]{2,0,1:T(8,128)}, u32[]{:S(2)}) copy-start(f32[320,32,128]{2,0,1:T(8,128)} %fusion.7) | copy-start | bytes 15728644
  1013.3 119.6 %all-to-all-start.7 = ((bf16[2,40,256,128]{3,0,1,2:T(2,128)(2,1)}), bf16[2,40,256,128]{3,0,1,2:T(2,128)(2,1)}, u32[]{:S(2)}, u32[]{:S(2)}) async-start(bf16[2,40,256,128]{3,0,1,2:T(2,128)(2,1)} %copy.203), calls=%async_computation.8 | async-start | bytes 10485760 | tf_op jit(solution)/shard_map/all_to_all | solution.py:87
  1017.9 205.1 %reduce-scatter.5.cloned.1.call-start = ((), (), s32[]{:S(2)}) async-start(), calls=%async_computation.11 | async-start | bytes 3276800 | tf_op jit(solution)/shard_map/reduce_scatter | solution.py:131
  1184.2 38.8 %copy-start.21 = (bf16[80,32,128]{2,0,1:T(8,128)(2,1)S(1)}, bf16[80,32,128]{2,0,1:T(8,128)(2,1)}, u32[]{:S(2)}) copy-start(bf16[80,32,128]{2,0,1:T(8,128)(2,1)} %reduce-scatter.3.cloned.1.call-done) | copy-start | bytes 1966084
  (21 other events, 98.2 us)
Sparse Core Ops, SparseCore 0:
  945.5 36.0 reduce-scatter.2
  1189.3 33.7 reduce-scatter.4

commit v8 on v7

--- a/solution.py
+++ b/solution.py
@@ -107,6 +107,7 @@
     outputs = []
     previous = None
     spectrum = None
+    first_gathered = None
     for state in range(state_count):
         total = None
         for first in range(0, coil_count, group):
@@ -121,8 +122,13 @@
             chunk_real = chunk_real.astype(F32)
             chunk_imag = chunk_imag.astype(F32)
             spectrum = forward_y(pixels, chunk_real, chunk_imag, y_fwd)
+            if first_gathered is not None and state == 0 and first == group:
+                spectrum = after(spectrum, first_gathered)
+            gathered = to_ky_blocks(spectrum)
+            if first_gathered is None:
+                first_gathered = gathered
             adjoint_z = middle_z(
-                to_ky_blocks(spectrum), y_data[state, first : first + group], kz_lines[state]
+                gathered, y_data[state, first : first + group], kz_lines[state]
             )
             if previous is not None and first + group >= coil_count:
                 adjoint_z = after(adjoint_z, previous)

time: 1240 us -> 1200 us (0.968)
  waiting for transfers between devices: 466 us -> 428 us
    all_to_all x4, waiting for transfers between devices: 209 us -> 109 us  [to_z_slabs(): lax.all_to_all(values, 'slab', split_axis=2, concat_axis=1, tiled=True)]
    all_to_all x4, waiting for transfers between devices: 223 us -> 286 us  [to_ky_blocks(): lax.all_to_all(values, 'slab', split_axis=1, concat_axis=2, tiled=True)]
    convert_element_type x4 -> x3, local copies, waits for them, and re-layouts: 25.3 us -> 19.7 us  [forward_y(): return jnp.einsum('ky,cyzl->ckzl', y_fwd, with_turned(coil_image, 1), pre...]
    unnamed x92 -> x98, local copies, waits for them, and re-layouts: 44.5 us -> 44 us
  transfers between devices with their start and end apart: 10 -> 10, of which waited for: 8 -> 8; matrix products, arithmetic and copies ran while one was open for 39% -> 44% of each run, Pallas kernels for 0% -> 0%
where the time goes in v8:
time: 1200 us; the launch traced here: 1190 us
  waiting for transfers between devices  428 us (36%)
  local copies, waits for them, and re-layouts  305 us (25%)
  other arithmetic  243 us (20%)
  matrix products  161 us (13%)
  starting transfers between devices  42.4 us (4%)
  between operations  14.4 us (1%)
    all_to_all x4, waiting for transfers between devices, to_ky_blocks(): lax.all_to_all(values, 'slab', split_axis=1, concat_axis=2, tiled=True)  286 us
    all_to_all x4, waiting for transfers between devices, to_z_slabs(): lax.all_to_all(values, 'slab', split_axis=2, concat_axis=1, tiled=True)  109 us
    neg x20, other arithmetic, turned(): return jnp.concatenate([-values[..., half:], values[..., :half]], axis=-1)  99.1 us
    dot_general x4, matrix products, backward_y(): jnp.einsum('yk,ckzl->cyzl', y_back, with_turned(returned, 1), preferred_e...  67.8 us
    all_to_all x12, local copies, waits for them, and re-layouts, to_z_slabs(): lax.all_to_all(values, 'slab', split_axis=2, concat_axis=1, tiled=True)  64.9 us
    all_to_all x8, local copies, waits for them, and re-layouts, to_ky_blocks(): lax.all_to_all(values, 'slab', split_axis=1, concat_axis=2, tiled=True)  57.9 us
    reduce_sum x4, other arithmetic, backward_y(): return jnp.sum(sens_real * coil_back - sens_imag * turned_back, axis=0)  54.9 us
    unnamed x98, local copies, waits for them, and re-layouts  44 us
  transfers between devices with their start and end apart: 10, of which 8 were waited for; matrix products, arithmetic and copies ran while one was open for 44% of the time, Pallas kernels for 0%

profile of v8, /device:TPU:0, one launch (start us, length us, event | category | flops | bytes accessed | tf_op | source)
XLA Modules:
  0.0 1194.4 jit_solution(10059709808507334884)
XLA Ops:
  36.3 9.2 fusion.221
  45.5 12.0 %copy.225 = bf16[4,320,32,64]{3,1,2,0:T(8,128)(2,1)} copy(bf16[4,320,32,64]{3,2,1,0:T(8,128)(2,1)} %get-tuple-element.34) | data formatting | bytes 10485760
  57.5 11.9 copy.226
  69.5 17.9 %fusion.1 = (bf16[2,320,32,128]{3,1,2,0:T(8,128)(2,1)}, bf16[2,320,32,128]{3,1,2,0:T(8,128)(2,1)}, bf16[2,320,32,128]{3,1,2,0:T(8,128)(2,1)}) fusion(f32[320,32,128]{2,0,1:T(8,128)} %copy.147, f32[320,32,128]{2,0,1:T(8,128)} %copy.145, bf16[4,320,32,64]{3,1,2,0:T(8,128)(2,1)} %copy.226, bf16[4,320,32,64]{3,1,2,0:T(8,128)(2,1)} %copy.225), kind=kLoop, calls=%fused_computation.17 | loop fusion | flops 36700160 | bytes 36700160 | tf_op jit(solution)/shard_map/convert_element_type | solution.py:44
  87.4 10.0 slice_negate_fusion.6
  119.3 10.5 pad_maximum_fusion
  150.2 10.0 slice_negate_fusion.4
  160.2 10.1 convert_bitcast_fusion.5
  170.3 64.6 %all-to-all-done = bf16[2,320,32,128]{3,2,0,1:T(8,128)(2,1)} async-done(((bf16[2,320,32,128]{3,2,0,1:T(8,128)(2,1)}), bf16[2,320,32,128]{3,2,0,1:T(8,128)(2,1)}, u32[]{:S(2)}, u32[]{:S(2)}) %all-to-all-start) | async-done | bytes 5242912 | tf_op jit(solution)/shard_map/all_to_all | solution.py:83
  302.2 13.8 %copy.155 = bf16[2,40,256,128]{3,0,1,2:T(2,128)(2,1)} copy(bf16[2,40,256,128]{2,3,0,1:T(8,128)(2,1)} %convert_bitcast_fusion.6) | data formatting | bytes 10485760 | tf_op jit(solution)/shard_map/convert_element_type | solution.py:69
  316.0 51.3 %all-to-all-done.2 = bf16[2,320,32,128]{3,2,0,1:T(8,128)(2,1)} async-done(((bf16[2,320,32,128]{3,2,0,1:T(8,128)(2,1)}), bf16[2,320,32,128]{3,2,0,1:T(8,128)(2,1)}, u32[]{:S(2)}, u32[]{:S(2)}) %all-to-all-start.2) | async-done | bytes 5242912 | tf_op jit(solution)/shard_map/all_to_all | solution.py:83
  392.0 10.0 slice_negate_fusion.2
  402.0 10.3 convert_bitcast_fusion.3
  432.6 10.0 slice_negate_fusion
  457.0 30.0 %all-to-all-done.1 = bf16[2,40,256,128]{3,0,1,2:T(2,128)(2,1)} async-done(((bf16[2,40,256,128]{3,0,1,2:T(2,128)(2,1)}), bf16[2,40,256,128]{3,0,1,2:T(2,128)(2,1)}, u32[]{:S(2)}, u32[]{:S(2)}) %all-to-all-start.1) | async-done | bytes 5242912 | tf_op jit(solution)/shard_map/all_to_all | solution.py:87
  500.1 106.7 %all-to-all-done.6 = bf16[2,320,32,128]{3,2,0,1:T(8,128)(2,1)} async-done(((bf16[2,320,32,128]{3,2,0,1:T(8,128)(2,1)}), bf16[2,320,32,128]{3,2,0,1:T(8,128)(2,1)}, u32[]{:S(2)}, u32[]{:S(2)}) %all-to-all-start.6) | async-done | bytes 5242912 | tf_op jit(solution)/shard_map/all_to_all | solution.py:83
  649.7 13.8 %copy.171 = bf16[2,40,256,128]{3,0,1,2:T(2,128)(2,1)} copy(bf16[2,40,256,128]{2,3,0,1:T(8,128)(2,1)} %convert_bitcast_fusion.4) | data formatting | bytes 10485760 | tf_op jit(solution)/shard_map/convert_element_type | solution.py:69
  663.5 62.9 %all-to-all-done.4 = bf16[2,320,32,128]{3,2,0,1:T(8,128)(2,1)} async-done(((bf16[2,320,32,128]{3,2,0,1:T(8,128)(2,1)}), bf16[2,320,32,128]{3,2,0,1:T(8,128)(2,1)}, u32[]{:S(2)}, u32[]{:S(2)}) %all-to-all-start.4) | async-done | bytes 5242912 | tf_op jit(solution)/shard_map/all_to_all | solution.py:83
  793.5 13.8 %copy.187 = bf16[2,40,256,128]{3,0,1,2:T(2,128)(2,1)} copy(bf16[2,40,256,128]{2,3,0,1:T(8,128)(2,1)} %convert_bitcast_fusion.2) | data formatting | bytes 10485760 | tf_op jit(solution)/shard_map/convert_element_type | solution.py:69
  812.3 16.9 %fusion.97 = f32[2,640,32,128]{3,1,2,0:T(8,128)} fusion(bf16[2,320,32,64]{1,3,2,0:T(8,128)(2,1)} %get-tuple-element.41, bf16[2,320,32,64]{1,3,2,0:T(8,128)(2,1)S(1)} %get-tuple-element.40, bf16[2,320,32,128]{1,3,2,0:T(8,128)(2,1)} %copy.160, bf16[320,320]{1,0:T(8,128)(2,1)} %copy-done.26, bf16[320,320]{1,0:T(8,128)(2,1)} %copy-done.27, ...), kind=kOutput, calls=%fused_computation.111 | convolution fusion | flops 6745620480 | bytes 32071680 | tf_op jit(solution)/shard_map/yk,ckzl->cyzl/dot_general | solution.py:74
  829.2 16.9 %all-to-all-done.3 = bf16[2,40,256,128]{3,0,1,2:T(2,128)(2,1)} async-done(((bf16[2,40,256,128]{3,0,1,2:T(2,128)(2,1)}), bf16[2,40,256,128]{3,0,1,2:T(2,128)(2,1)}, u32[]{:S(2)}, u32[]{:S(2)}) %all-to-all-start.3) | async-done | bytes 5242912 | tf_op jit(solution)/shard_map/all_to_all | solution.py:87
  850.9 14.5 %fusion.3 = f32[320,32,128]{2,0,1:T(8,128)} fusion(bf16[2,320,32,128]{3,1,2,0:T(8,128)(2,1)} %get-tuple-element.20, bf16[2,320,32,128]{3,1,2,0:T(8,128)(2,1)} %get-tuple-element.22, f32[2,640,32,128]{3,1,2,0:T(8,128)} %fusion.97), kind=kLoop, calls=%fused_computation.19 | loop fusion | flops 14417920 | bytes 36700160 | tf_op jit(solution)/shard_map/reduce_sum | solution.py:79
  886.6 16.9 %fusion.94 = f32[2,640,32,128]{3,1,2,0:T(8,128)} fusion(bf16[2,320,32,64]{1,3,2,0:T(8,128)(2,1)} %get-tuple-element.39, bf16[2,320,32,64]{1,3,2,0:T(8,128)(2,1)S(1)} %get-tuple-element.38, bf16[2,320,32,128]{1,3,2,0:T(8,128)(2,1)} %copy.176, bf16[320,320]{1,0:T(8,128)(2,1)} %copy-done.26, bf16[320,320]{1,0:T(8,128)(2,1)} %copy-done.27, ...), kind=kOutput, calls=%fused_computation.110 | convolution fusion | flops 6745620480 | bytes 32071680 | tf_op jit(solution)/shard_map/yk,ckzl->cyzl/dot_general | solution.py:74
  903.5 13.3 %fusion.7 = f32[320,32,128]{2,0,1:T(8,128)S(1)} fusion(bf16[2,320,32,128]{3,1,2,0:T(8,128)(2,1)} %copy-done.2, bf16[2,320,32,128]{3,1,2,0:T(8,128)(2,1)} %copy-done.1, f32[2,640,32,128]{3,1,2,0:T(8,128)} %fusion.94), kind=kLoop, calls=%fused_computation.23 | loop fusion | flops 14417920 | bytes 36700160 | tf_op jit(solution)/shard_map/reduce_sum | solution.py:79
  960.8 13.8 %copy.203 = bf16[2,40,256,128]{3,0,1,2:T(2,128)(2,1)} copy(bf16[2,40,256,128]{2,3,0,1:T(8,128)(2,1)} %convert_bitcast_fusion) | data formatting | bytes 10485760 | tf_op jit(solution)/shard_map/optimization_barrier | solution.py:93
  988.0 8.9 copy.192
  1001.9 16.8 %fusion.91 = f32[2,640,32,128]{3,1,2,0:T(8,128)} fusion(bf16[2,320,32,64]{1,3,2,0:T(8,128)(2,1)} %get-tuple-element.43, bf16[2,320,32,64]{1,3,2,0:T(8,128)(2,1)S(1)} %get-tuple-element.42, bf16[2,320,32,128]{1,3,2,0:T(8,128)(2,1)} %copy.192, bf16[320,320]{1,0:T(8,128)(2,1)} %copy-done.26, bf16[320,320]{1,0:T(8,128)(2,1)} %copy-done.27, ...), kind=kOutput, calls=%fused_computation.109 | convolution fusion | flops 6745620480 | bytes 32071680 | tf_op jit(solution)/shard_map/yk,ckzl->cyzl/dot_general | solution.py:74
  1018.7 14.0 %fusion.11 = f32[320,32,128]{2,0,1:T(8,128)} fusion(bf16[2,320,32,128]{3,1,2,0:T(8,128)(2,1)} %get-tuple-element.20, bf16[2,320,32,128]{3,1,2,0:T(8,128)(2,1)} %get-tuple-element.22, f32[2,640,32,128]{3,1,2,0:T(8,128)} %fusion.91), kind=kLoop, calls=%fused_computation.27 | loop fusion | flops 14417920 | bytes 36700160 | tf_op jit(solution)/shard_map/reduce_sum | solution.py:79
  1032.7 61.6 %all-to-all-done.7 = bf16[2,40,256,128]{3,0,1,2:T(2,128)(2,1)} async-done(((bf16[2,40,256,128]{3,0,1,2:T(2,128)(2,1)}), bf16[2,40,256,128]{3,0,1,2:T(2,128)(2,1)}, u32[]{:S(2)}, u32[]{:S(2)}) %all-to-all-start.7) | async-done | bytes 5242912 | tf_op jit(solution)/shard_map/all_to_all | solution.py:87
  1115.5 17.2 %fusion.88 = f32[2,640,32,128]{3,1,2,0:T(8,128)} fusion(bf16[2,320,32,64]{1,3,2,0:T(8,128)(2,1)} %get-tuple-element.37, bf16[2,320,32,64]{1,3,2,0:T(8,128)(2,1)S(1)} %get-tuple-element.36, bf16[2,320,32,128]{1,3,2,0:T(8,128)(2,1)} %copy.208, bf16[320,320]{1,0:T(8,128)(2,1)} %copy-done.26, bf16[320,320]{1,0:T(8,128)(2,1)} %copy-done.27, ...), kind=kOutput, calls=%fused_computation.108 | convolution fusion | flops 6745620480 | bytes 32071680 | tf_op jit(solution)/shard_map/yk,ckzl->cyzl/dot_general | solution.py:74
  1132.7 13.1 %fusion.15 = f32[320,32,128]{2,0,1:T(8,128)S(1)} fusion(bf16[2,320,32,128]{3,1,2,0:T(8,128)(2,1)} %copy-done.2, bf16[2,320,32,128]{3,1,2,0:T(8,128)(2,1)} %copy-done.1, f32[2,640,32,128]{3,1,2,0:T(8,128)} %fusion.88), kind=kLoop, calls=%fused_computation.31 | loop fusion | flops 14417920 | bytes 36700160 | tf_op jit(solution)/shard_map/reduce_sum | solution.py:79
  1150.7 34.0 %reduce-scatter.5.cloned.1.call-done = bf16[80,32,128]{2,0,1:T(8,128)(2,1)} async-done(((bf16[320,32,128]{2,0,1:T(8,128)(2,1)}), bf16[80,32,128]{2,0,1:T(8,128)(2,1)}) %reduce-scatter.5.cloned.1.call-update) | async-done | bytes 655376 | tf_op jit(solution)/shard_map/reduce_scatter | solution.py:137
  (201 shorter events, 443.3 us)
Async XLA Ops:
  24.8 417.8 %copy-start.26 = (bf16[320,320]{1,0:T(8,128)(2,1)}, bf16[320,320]{1,0:T(8,128)(2,1)S(1)}, u32[]{:S(2)}) copy-start(bf16[320,320]{1,0:T(8,128)(2,1)S(1)} %get-tuple-element.84) | copy-start | bytes 614404
  26.7 415.9 %copy-start.27 = (bf16[320,320]{1,0:T(8,128)(2,1)}, bf16[320,320]{1,0:T(8,128)(2,1)S(1)}, u32[]{:S(2)}) copy-start(bf16[320,320]{1,0:T(8,128)(2,1)S(1)} %fusion.198) | copy-start | bytes 614404
  26.7 9.6 slice-start.8
  26.7 9.5 slice-start.9
  111.8 123.2 %all-to-all-start = ((bf16[2,320,32,128]{3,2,0,1:T(8,128)(2,1)}), bf16[2,320,32,128]{3,2,0,1:T(8,128)(2,1)}, u32[]{:S(2)}, u32[]{:S(2)}) async-start(bf16[2,320,32,128]{3,2,0,1:T(8,128)(2,1)} %copy.148), calls=%async_computation | async-start | bytes 10485760 | tf_op jit(solution)/shard_map/all_to_all | solution.py:83
  129.8 16.1 %copy-start.1 = (bf16[2,320,32,128]{3,1,2,0:T(8,128)(2,1)}, bf16[2,320,32,128]{3,1,2,0:T(8,128)(2,1)S(1)}, u32[]{:S(2)}) copy-start(bf16[2,320,32,128]{3,1,2,0:T(8,128)(2,1)S(1)} %get-tuple-element.25) | copy-start | bytes 15728644
  129.8 16.1 %copy-start.2 = (bf16[2,320,32,128]{3,1,2,0:T(8,128)(2,1)}, bf16[2,320,32,128]{3,1,2,0:T(8,128)(2,1)S(1)}, u32[]{:S(2)}) copy-start(bf16[2,320,32,128]{3,1,2,0:T(8,128)(2,1)S(1)} %get-tuple-element.23) | copy-start | bytes 15728644
  235.0 6.6 copy-start.15
  247.3 120.0 %all-to-all-start.2 = ((bf16[2,320,32,128]{3,2,0,1:T(8,128)(2,1)}), bf16[2,320,32,128]{3,2,0,1:T(8,128)(2,1)}, u32[]{:S(2)}, u32[]{:S(2)}) async-start(bf16[2,320,32,128]{3,2,0,1:T(8,128)(2,1)} %copy.164), calls=%async_computation.2 | async-start | bytes 10485760 | tf_op jit(solution)/shard_map/all_to_all | solution.py:83
  316.0 56.2 %copy-start = (bf16[320,32,128]{2,1,0:T(8,128)(2,1)S(1)}, bf16[320,32,128]{2,1,0:T(8,128)(2,1)}, u32[]{:S(2)}) copy-start(bf16[320,32,128]{2,1,0:T(8,128)(2,1)} %get-tuple-element.24) | copy-start | bytes 7864324
  367.3 119.7 %all-to-all-start.1 = ((bf16[2,40,256,128]{3,0,1,2:T(2,128)(2,1)}), bf16[2,40,256,128]{3,0,1,2:T(2,128)(2,1)}, u32[]{:S(2)}, u32[]{:S(2)}) async-start(bf16[2,40,256,128]{3,0,1,2:T(2,128)(2,1)} %copy.155), calls=%async_computation.1 | async-start | bytes 10485760 | tf_op jit(solution)/shard_map/all_to_all | solution.py:87
  376.9 11.0 slice-start.4
  376.9 11.0 slice-start.6
  378.3 9.6 slice-start.5
  378.3 9.6 slice-start.7
  382.2 5.7 copy-start.9
  417.0 11.0 slice-start
  417.0 11.0 slice-start.2
  418.5 9.6 slice-start.1
  418.5 9.6 slice-start.3
  422.3 5.7 copy-start.8
  487.1 119.7 %all-to-all-start.6 = ((bf16[2,320,32,128]{3,2,0,1:T(8,128)(2,1)}), bf16[2,320,32,128]{3,2,0,1:T(8,128)(2,1)}, u32[]{:S(2)}, u32[]{:S(2)}) async-start(bf16[2,320,32,128]{3,2,0,1:T(8,128)(2,1)} %copy.196), calls=%async_computation.7 | async-start | bytes 10485760 | tf_op jit(solution)/shard_map/all_to_all | solution.py:83
  500.1 111.4 %copy-start.12 = (bf16[1,2,40,128,128]{4,3,2,1,0:T(8,128)(2,1)S(1)}, bf16[1,2,40,128,128]{4,3,2,1,0:T(8,128)(2,1)}, u32[]{:S(2)}) copy-start(bf16[1,2,40,128,128]{4,3,2,1,0:T(8,128)(2,1)} %get-tuple-element.30) | copy-start | bytes 7864324
  606.8 119.6 %all-to-all-start.4 = ((bf16[2,320,32,128]{3,2,0,1:T(8,128)(2,1)}), bf16[2,320,32,128]{3,2,0,1:T(8,128)(2,1)}, u32[]{:S(2)}, u32[]{:S(2)}) async-start(bf16[2,320,32,128]{3,2,0,1:T(8,128)(2,1)} %copy.180), calls=%async_computation.5 | async-start | bytes 10485760 | tf_op jit(solution)/shard_map/all_to_all | solution.py:83
  663.5 67.8 %copy-start.11 = (bf16[1,2,40,128,128]{4,3,2,1,0:T(8,128)(2,1)S(1)}, bf16[1,2,40,128,128]{4,3,2,1,0:T(8,128)(2,1)}, u32[]{:S(2)}) copy-start(bf16[1,2,40,128,128]{4,3,2,1,0:T(8,128)(2,1)} %get-tuple-element.31) | copy-start | bytes 7864324
  726.4 119.8 %all-to-all-start.3 = ((bf16[2,40,256,128]{3,0,1,2:T(2,128)(2,1)}), bf16[2,40,256,128]{3,0,1,2:T(2,128)(2,1)}, u32[]{:S(2)}, u32[]{:S(2)}) async-start(bf16[2,40,256,128]{3,0,1,2:T(2,128)(2,1)} %copy.171), calls=%async_computation.3 | async-start | bytes 10485760 | tf_op jit(solution)/shard_map/all_to_all | solution.py:87
  846.2 128.4 %all-to-all-start.5 = ((bf16[2,40,256,128]{3,0,1,2:T(2,128)(2,1)}), bf16[2,40,256,128]{3,0,1,2:T(2,128)(2,1)}, u32[]{:S(2)}, u32[]{:S(2)}) async-start(bf16[2,40,256,128]{3,0,1,2:T(2,128)(2,1)} %copy.187), calls=%async_computation.6 | async-start | bytes 10485760 | tf_op jit(solution)/shard_map/all_to_all | solution.py:87
  850.8 110.0 %reduce-scatter.3.cloned.1.call-start = ((), (), s32[]{:S(2)}) async-start(), calls=%async_computation.10 | async-start | bytes 3276800 | tf_op jit(solution)/shard_map/reduce_scatter | solution.py:137
  939.0 5.8 copy-start.4
  974.6 119.7 %all-to-all-start.7 = ((bf16[2,40,256,128]{3,0,1,2:T(2,128)(2,1)}), bf16[2,40,256,128]{3,0,1,2:T(2,128)(2,1)}, u32[]{:S(2)}, u32[]{:S(2)}) async-start(bf16[2,40,256,128]{3,0,1,2:T(2,128)(2,1)} %copy.203), calls=%async_computation.8 | async-start | bytes 10485760 | tf_op jit(solution)/shard_map/all_to_all | solution.py:87
  980.4 204.2 %reduce-scatter.5.cloned.1.call-start = ((), (), s32[]{:S(2)}) async-start(), calls=%async_computation.11 | async-start | bytes 3276800 | tf_op jit(solution)/shard_map/reduce_scatter | solution.py:137
  1145.8 38.9 %copy-start.24 = (bf16[80,32,128]{2,0,1:T(8,128)(2,1)S(1)}, bf16[80,32,128]{2,0,1:T(8,128)(2,1)}, u32[]{:S(2)}) copy-start(bf16[80,32,128]{2,0,1:T(8,128)(2,1)} %reduce-scatter.3.cloned.1.call-done) | copy-start | bytes 1966084
  (24 other events, 84.5 us)
Sparse Core Ops, SparseCore 0:
  922.0 35.9 reduce-scatter.2
  1150.8 33.7 reduce-scatter.4

commit v9 on v8

--- a/solution.py
+++ b/solution.py
@@ -103,7 +103,6 @@
         [jnp.concatenate([y_cos, y_sin], axis=1), jnp.concatenate([-y_sin, y_cos], axis=1)],
         axis=0,
     )
-    sens_real, sens_imag = dup_halves(coil_maps)
     outputs = []
     previous = None
     spectrum = None
@@ -112,8 +111,7 @@
         total = None
         for first in range(0, coil_count, group):
             pixels = image[state]
-            chunk_real = sens_real[first : first + group]
-            chunk_imag = sens_imag[first : first + group]
+            chunk_real, chunk_imag = dup_halves(coil_maps[first : first + group])
             if spectrum is not None:
                 pixels, chunk_real, chunk_imag, _ = lax.optimization_barrier(
                     (pixels, chunk_real, chunk_imag, spectrum)

time: 1200 us -> 1180 us (0.983)
  waiting for transfers between devices: 428 us -> 412 us
    unnamed x98 -> x100, local copies, waits for them, and re-layouts: 44 us -> 38.1 us
  transfers between devices with their start and end apart: 10 -> 10, of which waited for: 8 -> 8; matrix products, arithmetic and copies ran while one was open for 44% -> 46% of each run, Pallas kernels for 0% -> 0%
where the time goes in v9:
time: 1180 us; the launch traced here: 1170 us
  waiting for transfers between devices  412 us (35%)
  local copies, waits for them, and re-layouts  299 us (25%)
  other arithmetic  246 us (21%)
  matrix products  161 us (14%)
  starting transfers between devices  42.3 us (4%)
  between operations  14.3 us (1%)
    all_to_all x4, waiting for transfers between devices, to_ky_blocks(): lax.all_to_all(values, 'slab', split_axis=1, concat_axis=2, tiled=True)  281 us
    neg x20, other arithmetic, turned(): return jnp.concatenate([-values[..., half:], values[..., :half]], axis=-1)  99.2 us
    all_to_all x4, waiting for transfers between devices, to_z_slabs(): lax.all_to_all(values, 'slab', split_axis=2, concat_axis=1, tiled=True)  97.2 us
    dot_general x4, matrix products, backward_y(): jnp.einsum('yk,ckzl->cyzl', y_back, with_turned(returned, 1), preferred_e...  68.1 us
    all_to_all x12, local copies, waits for them, and re-layouts, to_z_slabs(): lax.all_to_all(values, 'slab', split_axis=2, concat_axis=1, tiled=True)  64.8 us
    reduce_sum x4, other arithmetic, backward_y(): return jnp.sum(sens_real * coil_back - sens_imag * turned_back, axis=0)  58.3 us
    all_to_all x8, local copies, waits for them, and re-layouts, to_ky_blocks(): lax.all_to_all(values, 'slab', split_axis=1, concat_axis=2, tiled=True)  58 us
    convert_element_type x3, local copies, waits for them, and re-layouts, middle_z(): return jnp.einsum('kjz,ckjl->ckzl', rows_back, with_turned(residual, 2),...  41.4 us
  transfers between devices with their start and end apart: 10, of which 8 were waited for; matrix products, arithmetic and copies ran while one was open for 46% of the time, Pallas kernels for 0%

profile of v9, /device:TPU:0, one launch (start us, length us, event | category | flops | bytes accessed | tf_op | source)
XLA Modules:
  0.0 1174.9 jit_solution(9560694799131459566)
XLA Ops:
  36.2 8.8 fusion.217
  54.2 10.4 fusion.1
  64.6 10.0 slice_negate_fusion.6
  74.7 8.8 convert_bitcast_fusion.7
  132.0 10.1 slice_negate_fusion.4
  142.1 10.3 convert_bitcast_fusion.5
  152.4 59.8 %all-to-all-done = bf16[2,320,32,128]{3,2,0,1:T(8,128)(2,1)} async-done(((bf16[2,320,32,128]{3,2,0,1:T(8,128)(2,1)}), bf16[2,320,32,128]{3,2,0,1:T(8,128)(2,1)}, u32[]{:S(2)}, u32[]{:S(2)}) %all-to-all-start) | async-done | bytes 5242912 | tf_op jit(solution)/shard_map/all_to_all | solution.py:83
  279.5 13.7 %copy.161 = bf16[2,40,256,128]{3,0,1,2:T(2,128)(2,1)} copy(bf16[2,40,256,128]{2,3,0,1:T(8,128)(2,1)} %convert_bitcast_fusion.6) | data formatting | bytes 10485760 | tf_op jit(solution)/shard_map/convert_element_type | solution.py:69
  293.3 51.4 %all-to-all-done.2 = bf16[2,320,32,128]{3,2,0,1:T(8,128)(2,1)} async-done(((bf16[2,320,32,128]{3,2,0,1:T(8,128)(2,1)}), bf16[2,320,32,128]{3,2,0,1:T(8,128)(2,1)}, u32[]{:S(2)}, u32[]{:S(2)}) %all-to-all-start.2) | async-done | bytes 5242912 | tf_op jit(solution)/shard_map/all_to_all | solution.py:83
  349.5 10.4 pad_maximum_fusion
  380.6 10.0 slice_negate_fusion.2
  390.6 10.2 convert_bitcast_fusion.3
  420.7 10.0 slice_negate_fusion
  430.7 8.8 convert_bitcast_fusion.1
  445.2 19.2 %all-to-all-done.1 = bf16[2,40,256,128]{3,0,1,2:T(2,128)(2,1)} async-done(((bf16[2,40,256,128]{3,0,1,2:T(2,128)(2,1)}), bf16[2,40,256,128]{3,0,1,2:T(2,128)(2,1)}, u32[]{:S(2)}, u32[]{:S(2)}) %all-to-all-start.1) | async-done | bytes 5242912 | tf_op jit(solution)/shard_map/all_to_all | solution.py:87
  477.3 106.7 %all-to-all-done.6 = bf16[2,320,32,128]{3,2,0,1:T(8,128)(2,1)} async-done(((bf16[2,320,32,128]{3,2,0,1:T(8,128)(2,1)}), bf16[2,320,32,128]{3,2,0,1:T(8,128)(2,1)}, u32[]{:S(2)}, u32[]{:S(2)}) %all-to-all-start.6) | async-done | bytes 5242912 | tf_op jit(solution)/shard_map/all_to_all | solution.py:83
  627.2 13.8 %copy.179 = bf16[2,40,256,128]{3,0,1,2:T(2,128)(2,1)} copy(bf16[2,40,256,128]{2,3,0,1:T(8,128)(2,1)} %convert_bitcast_fusion.4) | data formatting | bytes 10485760 | tf_op jit(solution)/shard_map/convert_element_type | solution.py:69
  641.0 63.0 %all-to-all-done.4 = bf16[2,320,32,128]{3,2,0,1:T(8,128)(2,1)} async-done(((bf16[2,320,32,128]{3,2,0,1:T(8,128)(2,1)}), bf16[2,320,32,128]{3,2,0,1:T(8,128)(2,1)}, u32[]{:S(2)}, u32[]{:S(2)}) %all-to-all-start.4) | async-done | bytes 5242912 | tf_op jit(solution)/shard_map/all_to_all | solution.py:83
  770.6 13.9 %copy.195 = bf16[2,40,256,128]{3,0,1,2:T(2,128)(2,1)} copy(bf16[2,40,256,128]{2,3,0,1:T(8,128)(2,1)} %convert_bitcast_fusion.2) | data formatting | bytes 10485760 | tf_op jit(solution)/shard_map/convert_element_type | solution.py:69
  789.6 17.2 %fusion.97 = f32[2,640,32,128]{3,1,2,0:T(8,128)} fusion(bf16[2,320,32,64]{1,3,2,0:T(8,128)(2,1)} %get-tuple-element.40, bf16[2,320,32,64]{1,3,2,0:T(8,128)(2,1)S(1)} %get-tuple-element.39, bf16[2,320,32,128]{1,3,2,0:T(8,128)(2,1)} %copy.166, bf16[320,320]{1,0:T(8,128)(2,1)} %copy-done.30, bf16[320,320]{1,0:T(8,128)(2,1)} %copy-done.31, ...), kind=kOutput, calls=%fused_computation.107 | convolution fusion | flops 6745620480 | bytes 32071680 | tf_op jit(solution)/shard_map/yk,ckzl->cyzl/dot_general | solution.py:74
  806.8 16.7 %all-to-all-done.3 = bf16[2,40,256,128]{3,0,1,2:T(2,128)(2,1)} async-done(((bf16[2,40,256,128]{3,0,1,2:T(2,128)(2,1)}), bf16[2,40,256,128]{3,0,1,2:T(2,128)(2,1)}, u32[]{:S(2)}, u32[]{:S(2)}) %all-to-all-start.3) | async-done | bytes 5242912 | tf_op jit(solution)/shard_map/all_to_all | solution.py:87
  828.3 18.0 %fusion.3 = f32[320,32,128]{2,0,1:T(8,128)} fusion(f32[2,640,32,128]{3,1,2,0:T(8,128)} %fusion.97, bf16[2,320,32,64]{3,1,2,0:T(8,128)(2,1)} %copy-done.4, bf16[2,320,32,64]{3,1,2,0:T(8,128)(2,1)} %copy-done.3), kind=kLoop, calls=%fused_computation.19 | loop fusion | flops 30146560 | bytes 31457280 | tf_op jit(solution)/shard_map/reduce_sum | solution.py:79
  867.4 16.9 %fusion.94 = f32[2,640,32,128]{3,1,2,0:T(8,128)} fusion(bf16[2,320,32,64]{1,3,2,0:T(8,128)(2,1)} %get-tuple-element.38, bf16[2,320,32,64]{1,3,2,0:T(8,128)(2,1)S(1)} %get-tuple-element.37, bf16[2,320,32,128]{1,3,2,0:T(8,128)(2,1)} %copy.184, bf16[320,320]{1,0:T(8,128)(2,1)} %copy-done.30, bf16[320,320]{1,0:T(8,128)(2,1)} %copy-done.31, ...), kind=kOutput, calls=%fused_computation.106 | convolution fusion | flops 6745620480 | bytes 32071680 | tf_op jit(solution)/shard_map/yk,ckzl->cyzl/dot_general | solution.py:74
  884.3 13.3 %fusion.7 = f32[320,32,128]{2,0,1:T(8,128)S(1)} fusion(bf16[2,320,32,128]{3,1,2,0:T(8,128)(2,1)} %copy-done.1, bf16[2,320,32,128]{3,1,2,0:T(8,128)(2,1)} %copy-done.2, f32[2,640,32,128]{3,1,2,0:T(8,128)} %fusion.94), kind=kLoop, calls=%fused_computation.23 | loop fusion | flops 14417920 | bytes 36700160 | tf_op jit(solution)/shard_map/reduce_sum | solution.py:79
  941.6 13.8 %copy.211 = bf16[2,40,256,128]{3,0,1,2:T(2,128)(2,1)} copy(bf16[2,40,256,128]{2,3,0,1:T(8,128)(2,1)} %convert_bitcast_fusion) | data formatting | bytes 10485760 | tf_op jit(solution)/shard_map/optimization_barrier | solution.py:93
  968.7 9.0 copy.200
  982.8 17.0 %fusion.91 = f32[2,640,32,128]{3,1,2,0:T(8,128)} fusion(bf16[2,320,32,64]{1,3,2,0:T(8,128)(2,1)} %get-tuple-element.42, bf16[2,320,32,64]{1,3,2,0:T(8,128)(2,1)S(1)} %get-tuple-element.41, bf16[2,320,32,128]{1,3,2,0:T(8,128)(2,1)} %copy.200, bf16[320,320]{1,0:T(8,128)(2,1)} %copy-done.30, bf16[320,320]{1,0:T(8,128)(2,1)} %copy-done.31, ...), kind=kOutput, calls=%fused_computation.105 | convolution fusion | flops 6745620480 | bytes 32071680 | tf_op jit(solution)/shard_map/yk,ckzl->cyzl/dot_general | solution.py:74
  999.8 14.0 %fusion.11 = f32[320,32,128]{2,0,1:T(8,128)} fusion(bf16[2,320,32,128]{3,1,2,0:T(8,128)(2,1)} %copy-done.5, bf16[2,320,32,128]{3,1,2,0:T(8,128)(2,1)} %copy-done.6, f32[2,640,32,128]{3,1,2,0:T(8,128)} %fusion.91), kind=kLoop, calls=%fused_computation.27 | loop fusion | flops 14417920 | bytes 36700160 | tf_op jit(solution)/shard_map/reduce_sum | solution.py:79
  1013.7 61.3 %all-to-all-done.7 = bf16[2,40,256,128]{3,0,1,2:T(2,128)(2,1)} async-done(((bf16[2,40,256,128]{3,0,1,2:T(2,128)(2,1)}), bf16[2,40,256,128]{3,0,1,2:T(2,128)(2,1)}, u32[]{:S(2)}, u32[]{:S(2)}) %all-to-all-start.7) | async-done | bytes 5242912 | tf_op jit(solution)/shard_map/all_to_all | solution.py:87
  1096.3 17.0 %fusion.88 = f32[2,640,32,128]{3,1,2,0:T(8,128)} fusion(bf16[2,320,32,64]{1,3,2,0:T(8,128)(2,1)} %get-tuple-element.36, bf16[2,320,32,64]{1,3,2,0:T(8,128)(2,1)S(1)} %get-tuple-element.35, bf16[2,320,32,128]{1,3,2,0:T(8,128)(2,1)} %copy.216, bf16[320,320]{1,0:T(8,128)(2,1)} %copy-done.30, bf16[320,320]{1,0:T(8,128)(2,1)} %copy-done.31, ...), kind=kOutput, calls=%fused_computation.104 | convolution fusion | flops 6745620480 | bytes 32071680 | tf_op jit(solution)/shard_map/yk,ckzl->cyzl/dot_general | solution.py:74
  1113.4 13.1 %fusion.15 = f32[320,32,128]{2,0,1:T(8,128)S(1)} fusion(bf16[2,320,32,128]{3,1,2,0:T(8,128)(2,1)} %copy-done.1, bf16[2,320,32,128]{3,1,2,0:T(8,128)(2,1)} %copy-done.2, f32[2,640,32,128]{3,1,2,0:T(8,128)} %fusion.88), kind=kLoop, calls=%fused_computation.31 | loop fusion | flops 14417920 | bytes 36700160 | tf_op jit(solution)/shard_map/reduce_sum | solution.py:79
  1131.4 34.0 %reduce-scatter.5.cloned.1.call-done = bf16[80,32,128]{2,0,1:T(8,128)(2,1)} async-done(((bf16[320,32,128]{2,0,1:T(8,128)(2,1)}), bf16[80,32,128]{2,0,1:T(8,128)(2,1)}) %reduce-scatter.5.cloned.1.call-update) | async-done | bytes 655376 | tf_op jit(solution)/shard_map/reduce_scatter | solution.py:135
  (202 shorter events, 450.2 us)
Async XLA Ops:
  24.7 406.0 %copy-start.30 = (bf16[320,320]{1,0:T(8,128)(2,1)}, bf16[320,320]{1,0:T(8,128)(2,1)S(1)}, u32[]{:S(2)}) copy-start(bf16[320,320]{1,0:T(8,128)(2,1)S(1)} %get-tuple-element.85) | copy-start | bytes 614404
  26.7 404.0 %copy-start.31 = (bf16[320,320]{1,0:T(8,128)(2,1)}, bf16[320,320]{1,0:T(8,128)(2,1)S(1)}, u32[]{:S(2)}) copy-start(bf16[320,320]{1,0:T(8,128)(2,1)S(1)} %fusion.196) | copy-start | bytes 614404
  26.7 9.6 slice-start.4
  26.7 9.6 slice-start.5
  30.8 5.4 slice-start.6
  89.2 123.0 %all-to-all-start = ((bf16[2,320,32,128]{3,2,0,1:T(8,128)(2,1)}), bf16[2,320,32,128]{3,2,0,1:T(8,128)(2,1)}, u32[]{:S(2)}, u32[]{:S(2)}) async-start(bf16[2,320,32,128]{3,2,0,1:T(8,128)(2,1)} %copy.154), calls=%async_computation | async-start | bytes 10485760 | tf_op jit(solution)/shard_map/all_to_all | solution.py:83
  111.9 16.0 %copy-start.1 = (bf16[2,320,32,128]{3,1,2,0:T(8,128)(2,1)}, bf16[2,320,32,128]{3,1,2,0:T(8,128)(2,1)S(1)}, u32[]{:S(2)}) copy-start(bf16[2,320,32,128]{3,1,2,0:T(8,128)(2,1)S(1)} %get-tuple-element.23) | copy-start | bytes 15728644
  111.9 16.0 %copy-start.2 = (bf16[2,320,32,128]{3,1,2,0:T(8,128)(2,1)}, bf16[2,320,32,128]{3,1,2,0:T(8,128)(2,1)S(1)}, u32[]{:S(2)}) copy-start(bf16[2,320,32,128]{3,1,2,0:T(8,128)(2,1)S(1)} %get-tuple-element.25) | copy-start | bytes 15728644
  122.2 5.7 copy-start.11
  212.3 6.6 copy-start.19
  224.6 120.0 %all-to-all-start.2 = ((bf16[2,320,32,128]{3,2,0,1:T(8,128)(2,1)}), bf16[2,320,32,128]{3,2,0,1:T(8,128)(2,1)}, u32[]{:S(2)}, u32[]{:S(2)}) async-start(bf16[2,320,32,128]{3,2,0,1:T(8,128)(2,1)} %copy.172), calls=%async_computation.2 | async-start | bytes 10485760 | tf_op jit(solution)/shard_map/all_to_all | solution.py:83
  344.6 119.7 %all-to-all-start.1 = ((bf16[2,40,256,128]{3,0,1,2:T(2,128)(2,1)}), bf16[2,40,256,128]{3,0,1,2:T(2,128)(2,1)}, u32[]{:S(2)}, u32[]{:S(2)}) async-start(bf16[2,40,256,128]{3,0,1,2:T(2,128)(2,1)} %copy.161), calls=%async_computation.1 | async-start | bytes 10485760 | tf_op jit(solution)/shard_map/all_to_all | solution.py:87
  349.5 10.5 copy-start
  359.9 16.2 %copy-start.5 = (bf16[2,320,32,128]{3,1,2,0:T(8,128)(2,1)}, bf16[2,320,32,128]{3,1,2,0:T(8,128)(2,1)S(1)}, u32[]{:S(2)}) copy-start(bf16[2,320,32,128]{3,1,2,0:T(8,128)(2,1)S(1)} %get-tuple-element.20) | copy-start | bytes 15728644
  359.9 16.2 %copy-start.6 = (bf16[2,320,32,128]{3,1,2,0:T(8,128)(2,1)}, bf16[2,320,32,128]{3,1,2,0:T(8,128)(2,1)S(1)}, u32[]{:S(2)}) copy-start(bf16[2,320,32,128]{3,1,2,0:T(8,128)(2,1)S(1)} %get-tuple-element.22) | copy-start | bytes 15728644
  370.4 5.7 copy-start.13
  405.5 11.0 slice-start
  405.5 11.0 slice-start.2
  406.9 9.6 slice-start.1
  407.0 9.6 slice-start.3
  410.8 5.7 copy-start.12
  464.4 119.6 %all-to-all-start.6 = ((bf16[2,320,32,128]{3,2,0,1:T(8,128)(2,1)}), bf16[2,320,32,128]{3,2,0,1:T(8,128)(2,1)}, u32[]{:S(2)}, u32[]{:S(2)}) async-start(bf16[2,320,32,128]{3,2,0,1:T(8,128)(2,1)} %copy.204), calls=%async_computation.7 | async-start | bytes 10485760 | tf_op jit(solution)/shard_map/all_to_all | solution.py:83
  477.3 111.8 %copy-start.16 = (bf16[1,2,40,128,128]{4,3,2,1,0:T(8,128)(2,1)S(1)}, bf16[1,2,40,128,128]{4,3,2,1,0:T(8,128)(2,1)}, u32[]{:S(2)}) copy-start(bf16[1,2,40,128,128]{4,3,2,1,0:T(8,128)(2,1)} %get-tuple-element.27) | copy-start | bytes 7864324
  584.0 120.0 %all-to-all-start.4 = ((bf16[2,320,32,128]{3,2,0,1:T(8,128)(2,1)}), bf16[2,320,32,128]{3,2,0,1:T(8,128)(2,1)}, u32[]{:S(2)}, u32[]{:S(2)}) async-start(bf16[2,320,32,128]{3,2,0,1:T(8,128)(2,1)} %copy.188), calls=%async_computation.5 | async-start | bytes 10485760 | tf_op jit(solution)/shard_map/all_to_all | solution.py:83
  641.0 67.7 %copy-start.15 = (bf16[1,2,40,128,128]{4,3,2,1,0:T(8,128)(2,1)S(1)}, bf16[1,2,40,128,128]{4,3,2,1,0:T(8,128)(2,1)}, u32[]{:S(2)}) copy-start(bf16[1,2,40,128,128]{4,3,2,1,0:T(8,128)(2,1)} %get-tuple-element.28) | copy-start | bytes 7864324
  703.9 119.6 %all-to-all-start.3 = ((bf16[2,40,256,128]{3,0,1,2:T(2,128)(2,1)}), bf16[2,40,256,128]{3,0,1,2:T(2,128)(2,1)}, u32[]{:S(2)}, u32[]{:S(2)}) async-start(bf16[2,40,256,128]{3,0,1,2:T(2,128)(2,1)} %copy.179), calls=%async_computation.3 | async-start | bytes 10485760 | tf_op jit(solution)/shard_map/all_to_all | solution.py:87
  823.5 131.8 %all-to-all-start.5 = ((bf16[2,40,256,128]{3,0,1,2:T(2,128)(2,1)}), bf16[2,40,256,128]{3,0,1,2:T(2,128)(2,1)}, u32[]{:S(2)}, u32[]{:S(2)}) async-start(bf16[2,40,256,128]{3,0,1,2:T(2,128)(2,1)} %copy.195), calls=%async_computation.6 | async-start | bytes 10485760 | tf_op jit(solution)/shard_map/all_to_all | solution.py:87
  828.2 113.3 %reduce-scatter.3.cloned.1.call-start = ((), (), s32[]{:S(2)}) async-start(), calls=%async_computation.10 | async-start | bytes 3276800 | tf_op jit(solution)/shard_map/reduce_scatter | solution.py:135
  919.8 5.8 copy-start.8
  955.3 119.7 %all-to-all-start.7 = ((bf16[2,40,256,128]{3,0,1,2:T(2,128)(2,1)}), bf16[2,40,256,128]{3,0,1,2:T(2,128)(2,1)}, u32[]{:S(2)}, u32[]{:S(2)}) async-start(bf16[2,40,256,128]{3,0,1,2:T(2,128)(2,1)} %copy.211), calls=%async_computation.8 | async-start | bytes 10485760 | tf_op jit(solution)/shard_map/all_to_all | solution.py:87
  961.2 204.1 %reduce-scatter.5.cloned.1.call-start = ((), (), s32[]{:S(2)}) async-start(), calls=%async_computation.11 | async-start | bytes 3276800 | tf_op jit(solution)/shard_map/reduce_scatter | solution.py:135
  1126.5 38.9 %copy-start.28 = (bf16[80,32,128]{2,0,1:T(8,128)(2,1)S(1)}, bf16[80,32,128]{2,0,1:T(8,128)(2,1)}, u32[]{:S(2)}) copy-start(bf16[80,32,128]{2,0,1:T(8,128)(2,1)} %reduce-scatter.3.cloned.1.call-done) | copy-start | bytes 1966084
  (24 other events, 77.8 us)
Sparse Core Ops, SparseCore 0:
  902.8 35.9 reduce-scatter.2
  1131.5 33.7 reduce-scatter.4

commit v10 on v9

--- a/solution.py
+++ b/solution.py
@@ -130,9 +130,29 @@
             )
             if previous is not None and first + group >= coil_count:
                 adjoint_z = after(adjoint_z, previous)
-            part = backward_y(to_z_slabs(adjoint_z), chunk_real, chunk_imag, y_back)
+            returned = to_z_slabs(adjoint_z)
+            z_local = returned.shape[2]
+            if total is not None and state == state_count - 1 and first + group >= coil_count and z_local % 2 == 0:
+                half = z_local // 2
+                pieces = []
+                sent = None
+                for low in (0, half):
+                    window = slice(low, low + half)
+                    piece_in = returned[:, :, window]
+                    if sent is not None:
+                        piece_in = after(piece_in, sent)
+                    part = backward_y(
+                        piece_in, chunk_real[:, :, window], chunk_imag[:, :, window], y_back
+                    )
+                    sent = (total[:, window] + part).astype(BF16)
+                    pieces.append(lax.psum_scatter(sent, "coil", scatter_dimension=0, tiled=True))
+                summed = jnp.concatenate(pieces, axis=1)
+                total = None
+                break
+            part = backward_y(returned, chunk_real, chunk_imag, y_back)
             total = part if total is None else total + part
-        summed = lax.psum_scatter(total.astype(BF16), "coil", scatter_dimension=0, tiled=True)
+        if total is not None:
+            summed = lax.psum_scatter(total.astype(BF16), "coil", scatter_dimension=0, tiled=True)
         previous = summed
         outputs.append(summed)
     return jnp.stack(outputs)

time: 1180 us -> 1230 us (1.042)
  other arithmetic: 246 us -> 270 us
    reduce_scatter x2 -> x1, waiting for transfers between devices: 34 us -> 0.01 us  [shards(): lax.psum_scatter(total.astype(BF16), 'coil', scatter_dimension=0, tiled=T...]
    reduce_scatter x0 -> x2, waiting for transfers between devices: none -> 25.9 us  [shards(): lax.psum_scatter(sent, 'coil', scatter_dimension=0, tiled=True)]
    convert_element_type x0 -> x4, other arithmetic: none -> 21.9 us  [the longest x1 7.76 us: shards(): chunk_imag = chunk_imag.astype(F32)]
    all_to_all x4, waiting for transfers between devices: 97.2 us -> 116 us  [to_z_slabs(): lax.all_to_all(values, 'slab', split_axis=2, concat_axis=1, tiled=True)]
    unnamed x100 -> x121, local copies, waits for them, and re-layouts: 38.1 us -> 53.9 us
    all_to_all x12 -> x11, local copies, waits for them, and re-layouts: 64.8 us -> 53.5 us  [to_z_slabs(): lax.all_to_all(values, 'slab', split_axis=2, concat_axis=1, tiled=True)]
    reduce_sum x4 -> x5, other arithmetic: 58.3 us -> 55.5 us  [backward_y(): return jnp.sum(sens_real * coil_back - sens_imag * turned_back, axis=0)]
    neg x20 -> x21, other arithmetic: 99.2 us -> 101 us  [turned(): return jnp.concatenate([-values[..., half:], values[..., :half]], axis=-1)]
  transfers between devices with their start and end apart: 10 -> 11, of which waited for: 8 -> 8; matrix products, arithmetic and copies ran while one was open for 46% -> 45% of each run, Pallas kernels for 0% -> 0%
where the time goes in v10:
time: 1230 us; the launch traced here: 1220 us
  waiting for transfers between devices  422 us (34%)
  local copies, waits for them, and re-layouts  310 us (25%)
  other arithmetic  270 us (22%)
  matrix products  159 us (13%)
  starting transfers between devices  42.8 us (3%)
  between operations  14.1 us (1%)
    all_to_all x4, waiting for transfers between devices, to_ky_blocks(): lax.all_to_all(values, 'slab', split_axis=1, concat_axis=2, tiled=True)  281 us
    all_to_all x4, waiting for transfers between devices, to_z_slabs(): lax.all_to_all(values, 'slab', split_axis=2, concat_axis=1, tiled=True)  116 us
    neg x21, other arithmetic, turned(): return jnp.concatenate([-values[..., half:], values[..., :half]], axis=-1)  101 us
    dot_general x5, matrix products, backward_y(): jnp.einsum('yk,ckzl->cyzl', y_back, with_turned(returned, 1), preferred_e...  68.1 us
    all_to_all x8, local copies, waits for them, and re-layouts, to_ky_blocks(): lax.all_to_all(values, 'slab', split_axis=1, concat_axis=2, tiled=True)  57.8 us
    reduce_sum x5, other arithmetic, backward_y(): return jnp.sum(sens_real * coil_back - sens_imag * turned_back, axis=0)  55.5 us
    unnamed x121, local copies, waits for them, and re-layouts  53.9 us
    all_to_all x11, local copies, waits for them, and re-layouts, to_z_slabs(): lax.all_to_all(values, 'slab', split_axis=2, concat_axis=1, tiled=True)  53.5 us
  transfers between devices with their start and end apart: 11, of which 8 were waited for; matrix products, arithmetic and copies ran while one was open for 45% of the time, Pallas kernels for 0%

profile of v10, /device:TPU:0, one launch (start us, length us, event | category | flops | bytes accessed | tf_op | source)
XLA Modules:
  0.0 1218.0 jit_solution(13716303757770935241)
XLA Ops:
  53.1 10.4 fusion.1
  63.5 10.0 slice_negate_fusion.6
  73.6 8.9 convert_bitcast_fusion.7
  118.6 92.9 %all-to-all-done = bf16[2,320,32,128]{3,2,0,1:T(8,128)(2,1)} async-done(((bf16[2,320,32,128]{3,2,0,1:T(8,128)(2,1)}), bf16[2,320,32,128]{3,2,0,1:T(8,128)(2,1)}, u32[]{:S(2)}, u32[]{:S(2)}) %all-to-all-start) | async-done | bytes 5242912 | tf_op jit(solution)/shard_map/all_to_all | solution.py:83
  247.5 13.8 %copy.166 = bf16[2,40,256,128]{3,0,1,2:T(2,128)(2,1)} copy(bf16[2,40,256,128]{2,3,0,1:T(8,128)(2,1)} %convert_bitcast_fusion.6) | data formatting | bytes 10485760 | tf_op jit(solution)/shard_map/convert_element_type | solution.py:69
  304.6 9.9 slice_negate_fusion.4
  314.5 8.9 convert_bitcast_fusion.5
  329.0 52.4 %all-to-all-done.1 = bf16[2,40,256,128]{3,0,1,2:T(2,128)(2,1)} async-done(((bf16[2,40,256,128]{3,0,1,2:T(2,128)(2,1)}), bf16[2,40,256,128]{3,0,1,2:T(2,128)(2,1)}, u32[]{:S(2)}, u32[]{:S(2)}) %all-to-all-start.1) | async-done | bytes 5242912 | tf_op jit(solution)/shard_map/all_to_all | solution.py:87
  386.4 10.5 pad_maximum_fusion
  420.0 9.9 slice_negate_fusion.2
  429.9 8.7 convert_bitcast_fusion.3
  444.2 57.1 %all-to-all-done.2 = bf16[2,320,32,128]{3,2,0,1:T(8,128)(2,1)} async-done(((bf16[2,320,32,128]{3,2,0,1:T(8,128)(2,1)}), bf16[2,320,32,128]{3,2,0,1:T(8,128)(2,1)}, u32[]{:S(2)}, u32[]{:S(2)}) %all-to-all-start.2) | async-done | bytes 5242912 | tf_op jit(solution)/shard_map/all_to_all | solution.py:83
  528.7 9.9 slice_negate_fusion
  538.6 9.1 convert_bitcast_fusion.1
  553.5 67.6 %all-to-all-done.4 = bf16[2,320,32,128]{3,2,0,1:T(8,128)(2,1)} async-done(((bf16[2,320,32,128]{3,2,0,1:T(8,128)(2,1)}), bf16[2,320,32,128]{3,2,0,1:T(8,128)(2,1)}, u32[]{:S(2)}, u32[]{:S(2)}) %all-to-all-start.4) | async-done | bytes 5242912 | tf_op jit(solution)/shard_map/all_to_all | solution.py:83
  663.9 13.8 %copy.184 = bf16[2,40,256,128]{3,0,1,2:T(2,128)(2,1)} copy(bf16[2,40,256,128]{2,3,0,1:T(8,128)(2,1)} %convert_bitcast_fusion.4) | data formatting | bytes 10485760 | tf_op jit(solution)/shard_map/convert_element_type | solution.py:69
  677.7 62.9 %all-to-all-done.6 = bf16[2,320,32,128]{3,2,0,1:T(8,128)(2,1)} async-done(((bf16[2,320,32,128]{3,2,0,1:T(8,128)(2,1)}), bf16[2,320,32,128]{3,2,0,1:T(8,128)(2,1)}, u32[]{:S(2)}, u32[]{:S(2)}) %all-to-all-start.6) | async-done | bytes 5242912 | tf_op jit(solution)/shard_map/all_to_all | solution.py:83
  763.1 8.6 copy.171
  807.3 13.8 %copy.200 = bf16[2,40,256,128]{3,0,1,2:T(2,128)(2,1)} copy(bf16[2,40,256,128]{2,3,0,1:T(8,128)(2,1)} %convert_bitcast_fusion.2) | data formatting | bytes 10485760 | tf_op jit(solution)/shard_map/convert_element_type | solution.py:69
  826.2 16.8 %fusion.84 = f32[2,640,32,128]{3,1,2,0:T(8,128)} fusion(bf16[2,320,32,64]{1,3,2,0:T(8,128)(2,1)} %get-tuple-element.42, bf16[2,320,32,64]{1,3,2,0:T(8,128)(2,1)S(1)} %get-tuple-element.41, bf16[2,320,32,128]{1,3,2,0:T(8,128)(2,1)} %copy.171, bf16[320,320]{1,0:T(8,128)(2,1)} %copy-done.26, bf16[320,320]{1,0:T(8,128)(2,1)S(1)} %fusion.207, ...), kind=kOutput, calls=%fused_computation.93 | convolution fusion | flops 6745620480 | bytes 32071680 | tf_op jit(solution)/shard_map/yk,ckzl->cyzl/dot_general | solution.py:74
  843.0 17.4 %all-to-all-done.3 = bf16[2,40,256,128]{3,0,1,2:T(2,128)(2,1)} async-done(((bf16[2,40,256,128]{3,0,1,2:T(2,128)(2,1)}), bf16[2,40,256,128]{3,0,1,2:T(2,128)(2,1)}, u32[]{:S(2)}, u32[]{:S(2)}) %all-to-all-start.3) | async-done | bytes 5242912 | tf_op jit(solution)/shard_map/all_to_all | solution.py:87
  865.2 17.9 %fusion.3 = f32[320,32,128]{2,0,1:T(8,128)} fusion(f32[2,640,32,128]{3,1,2,0:T(8,128)} %fusion.84, bf16[2,320,32,64]{3,1,2,0:T(8,128)(2,1)} %copy-done.3, bf16[2,320,32,64]{3,1,2,0:T(8,128)(2,1)} %copy-done.4), kind=kLoop, calls=%fused_computation.15 | loop fusion | flops 30146560 | bytes 31457280 | tf_op jit(solution)/shard_map/reduce_sum | solution.py:79
  890.5 8.6 copy.189
  904.2 16.8 %fusion.81 = f32[2,640,32,128]{3,1,2,0:T(8,128)} fusion(bf16[2,320,32,64]{1,3,2,0:T(8,128)(2,1)} %get-tuple-element.40, bf16[2,320,32,64]{1,3,2,0:T(8,128)(2,1)S(1)} %get-tuple-element.39, bf16[2,320,32,128]{1,3,2,0:T(8,128)(2,1)} %copy.189, bf16[320,320]{1,0:T(8,128)(2,1)} %copy-done.26, bf16[320,320]{1,0:T(8,128)(2,1)S(1)} %fusion.207, ...), kind=kOutput, calls=%fused_computation.92 | convolution fusion | flops 6745620480 | bytes 32071680 | tf_op jit(solution)/shard_map/yk,ckzl->cyzl/dot_general | solution.py:74
  921.0 13.5 %fusion.7 = f32[320,32,128]{2,0,1:T(8,128)S(1)} fusion(bf16[2,320,32,128]{3,1,2,0:T(8,128)(2,1)} %copy-done.2, bf16[2,320,32,128]{3,1,2,0:T(8,128)(2,1)} %copy-done.1, f32[2,640,32,128]{3,1,2,0:T(8,128)} %fusion.81), kind=kLoop, calls=%fused_computation.19 | loop fusion | flops 14417920 | bytes 36700160 | tf_op jit(solution)/shard_map/reduce_sum | solution.py:79
  978.3 13.8 %copy.216 = bf16[2,40,256,128]{3,0,1,2:T(2,128)(2,1)} copy(bf16[2,40,256,128]{2,3,0,1:T(8,128)(2,1)} %convert_bitcast_fusion) | data formatting | bytes 10485760 | tf_op jit(solution)/shard_map/optimization_barrier | solution.py:93
  1020.9 8.8 copy.205
  1034.7 16.8 %fusion.78 = f32[2,640,32,128]{3,1,2,0:T(8,128)} fusion(bf16[2,320,32,64]{1,3,2,0:T(8,128)(2,1)} %get-tuple-element.38, bf16[2,320,32,64]{1,3,2,0:T(8,128)(2,1)S(1)} %get-tuple-element.37, bf16[2,320,32,128]{1,3,2,0:T(8,128)(2,1)} %copy.205, bf16[320,320]{1,0:T(8,128)(2,1)} %copy-done.26, bf16[320,320]{1,0:T(8,128)(2,1)S(1)} %fusion.207, ...), kind=kOutput, calls=%fused_computation.91 | convolution fusion | flops 6745620480 | bytes 32071680 | tf_op jit(solution)/shard_map/yk,ckzl->cyzl/dot_general | solution.py:74
  1051.5 14.0 %fusion.11 = f32[320,32,128]{2,0,1:T(8,128)} fusion(bf16[2,320,32,128]{3,1,2,0:T(8,128)(2,1)} %copy-done.5, bf16[2,320,32,128]{3,1,2,0:T(8,128)(2,1)} %copy-done.6, f32[2,640,32,128]{3,1,2,0:T(8,128)} %fusion.78), kind=kLoop, calls=%fused_computation.23 | loop fusion | flops 14417920 | bytes 36700160 | tf_op jit(solution)/shard_map/reduce_sum | solution.py:79
  1065.5 46.3 %all-to-all-done.7 = bf16[2,40,256,128]{3,0,1,2:T(2,128)(2,1)} async-done(((bf16[2,40,256,128]{3,0,1,2:T(2,128)(2,1)}), bf16[2,40,256,128]{3,0,1,2:T(2,128)(2,1)}, u32[]{:S(2)}, u32[]{:S(2)}) %all-to-all-start.7) | async-done | bytes 5242912 | tf_op jit(solution)/shard_map/all_to_all | solution.py:87
  1160.6 10.6 fusion.145
  1182.7 25.8 %reduce-scatter.8.cloned.1.call-done = bf16[80,16,128]{2,0,1:T(8,128)(2,1)} async-done(((bf16[320,16,128]{2,0,1:T(8,128)(2,1)}), bf16[80,16,128]{2,0,1:T(8,128)(2,1)}) %reduce-scatter.8.cloned.1.call-update) | async-done | bytes 327696 | tf_op jit(solution)/shard_map/reduce_scatter | solution.py:148
  (239 shorter events, 497.8 us)
Async XLA Ops:
  11.4 527.3 %copy-start.26 = (bf16[320,320]{1,0:T(8,128)(2,1)}, bf16[320,320]{1,0:T(8,128)(2,1)S(1)}, u32[]{:S(2)}) copy-start(bf16[320,320]{1,0:T(8,128)(2,1)S(1)} %get-tuple-element.91) | copy-start | bytes 614404
  88.2 123.3 %all-to-all-start = ((bf16[2,320,32,128]{3,2,0,1:T(8,128)(2,1)}), bf16[2,320,32,128]{3,2,0,1:T(8,128)(2,1)}, u32[]{:S(2)}, u32[]{:S(2)}) async-start(bf16[2,320,32,128]{3,2,0,1:T(8,128)(2,1)} %copy.159), calls=%async_computation | async-start | bytes 10485760 | tf_op jit(solution)/shard_map/all_to_all | solution.py:83
  110.5 119.8 %copy-start.35 = (pred[40,128]{1,0:T(8,128)(4,1)}, pred[40,128]{1,0:T(8,128)(4,1)S(1)}, u32[]{:S(2)}) copy-start(pred[40,128]{1,0:T(8,128)(4,1)S(1)} %get-tuple-element.82) | copy-start | bytes 15364
  261.3 120.0 %all-to-all-start.1 = ((bf16[2,40,256,128]{3,0,1,2:T(2,128)(2,1)}), bf16[2,40,256,128]{3,0,1,2:T(2,128)(2,1)}, u32[]{:S(2)}, u32[]{:S(2)}) async-start(bf16[2,40,256,128]{3,0,1,2:T(2,128)(2,1)} %copy.166), calls=%async_computation.1 | async-start | bytes 10485760 | tf_op jit(solution)/shard_map/all_to_all | solution.py:87
  281.7 15.8 %copy-start.1 = (bf16[2,320,32,128]{3,1,2,0:T(8,128)(2,1)}, bf16[2,320,32,128]{3,1,2,0:T(8,128)(2,1)S(1)}, u32[]{:S(2)}) copy-start(bf16[2,320,32,128]{3,1,2,0:T(8,128)(2,1)S(1)} %get-tuple-element.26) | copy-start | bytes 15728644
  281.8 15.8 %copy-start.2 = (bf16[2,320,32,128]{3,1,2,0:T(8,128)(2,1)}, bf16[2,320,32,128]{3,1,2,0:T(8,128)(2,1)S(1)}, u32[]{:S(2)}) copy-start(bf16[2,320,32,128]{3,1,2,0:T(8,128)(2,1)S(1)} %get-tuple-element.24) | copy-start | bytes 15728644
  381.3 120.0 %all-to-all-start.2 = ((bf16[2,320,32,128]{3,2,0,1:T(8,128)(2,1)}), bf16[2,320,32,128]{3,2,0,1:T(8,128)(2,1)}, u32[]{:S(2)}, u32[]{:S(2)}) async-start(bf16[2,320,32,128]{3,2,0,1:T(8,128)(2,1)} %copy.177), calls=%async_computation.2 | async-start | bytes 10485760 | tf_op jit(solution)/shard_map/all_to_all | solution.py:83
  386.4 10.6 copy-start
  397.0 15.8 %copy-start.5 = (bf16[2,320,32,128]{3,1,2,0:T(8,128)(2,1)}, bf16[2,320,32,128]{3,1,2,0:T(8,128)(2,1)S(1)}, u32[]{:S(2)}) copy-start(bf16[2,320,32,128]{3,1,2,0:T(8,128)(2,1)S(1)} %get-tuple-element.21) | copy-start | bytes 15728644
  397.0 15.8 %copy-start.6 = (bf16[2,320,32,128]{3,1,2,0:T(8,128)(2,1)}, bf16[2,320,32,128]{3,1,2,0:T(8,128)(2,1)S(1)}, u32[]{:S(2)}) copy-start(bf16[2,320,32,128]{3,1,2,0:T(8,128)(2,1)S(1)} %get-tuple-element.23) | copy-start | bytes 15728644
  501.3 119.8 %all-to-all-start.4 = ((bf16[2,320,32,128]{3,2,0,1:T(8,128)(2,1)}), bf16[2,320,32,128]{3,2,0,1:T(8,128)(2,1)}, u32[]{:S(2)}, u32[]{:S(2)}) async-start(bf16[2,320,32,128]{3,2,0,1:T(8,128)(2,1)} %copy.193), calls=%async_computation.5 | async-start | bytes 10485760 | tf_op jit(solution)/shard_map/all_to_all | solution.py:83
  510.9 10.8 slice-start
  510.9 10.8 slice-start.2
  553.5 72.3 %copy-start.12 = (bf16[1,2,40,128,128]{4,3,2,1,0:T(8,128)(2,1)S(1)}, bf16[1,2,40,128,128]{4,3,2,1,0:T(8,128)(2,1)}, u32[]{:S(2)}) copy-start(bf16[1,2,40,128,128]{4,3,2,1,0:T(8,128)(2,1)} %get-tuple-element.30) | copy-start | bytes 7864324
  621.1 119.6 %all-to-all-start.6 = ((bf16[2,320,32,128]{3,2,0,1:T(8,128)(2,1)}), bf16[2,320,32,128]{3,2,0,1:T(8,128)(2,1)}, u32[]{:S(2)}, u32[]{:S(2)}) async-start(bf16[2,320,32,128]{3,2,0,1:T(8,128)(2,1)} %copy.209), calls=%async_computation.7 | async-start | bytes 10485760 | tf_op jit(solution)/shard_map/all_to_all | solution.py:83
  677.7 67.8 %copy-start.11 = (bf16[1,2,40,128,128]{4,3,2,1,0:T(8,128)(2,1)S(1)}, bf16[1,2,40,128,128]{4,3,2,1,0:T(8,128)(2,1)}, u32[]{:S(2)}) copy-start(bf16[1,2,40,128,128]{4,3,2,1,0:T(8,128)(2,1)} %get-tuple-element.29) | copy-start | bytes 7864324
  740.7 119.7 %all-to-all-start.3 = ((bf16[2,40,256,128]{3,0,1,2:T(2,128)(2,1)}), bf16[2,40,256,128]{3,0,1,2:T(2,128)(2,1)}, u32[]{:S(2)}, u32[]{:S(2)}) async-start(bf16[2,40,256,128]{3,0,1,2:T(2,128)(2,1)} %copy.184), calls=%async_computation.3 | async-start | bytes 10485760 | tf_op jit(solution)/shard_map/all_to_all | solution.py:87
  860.4 131.7 %all-to-all-start.5 = ((bf16[2,40,256,128]{3,0,1,2:T(2,128)(2,1)}), bf16[2,40,256,128]{3,0,1,2:T(2,128)(2,1)}, u32[]{:S(2)}, u32[]{:S(2)}) async-start(bf16[2,40,256,128]{3,0,1,2:T(2,128)(2,1)} %copy.200), calls=%async_computation.6 | async-start | bytes 10485760 | tf_op jit(solution)/shard_map/all_to_all | solution.py:87
  865.1 113.2 %reduce-scatter.4.cloned.1.call-start = ((), (), s32[]{:S(2)}) async-start(), calls=%async_computation.11 | async-start | bytes 3276800 | tf_op jit(solution)/shard_map/reduce_scatter | solution.py:155
  992.1 119.7 %all-to-all-start.7 = ((bf16[2,40,256,128]{3,0,1,2:T(2,128)(2,1)}), bf16[2,40,256,128]{3,0,1,2:T(2,128)(2,1)}, u32[]{:S(2)}, u32[]{:S(2)}) async-start(bf16[2,40,256,128]{3,0,1,2:T(2,128)(2,1)} %copy.216), calls=%async_computation.8 | async-start | bytes 10485760 | tf_op jit(solution)/shard_map/all_to_all | solution.py:87
  998.0 184.8 %reduce-scatter.6.cloned.1.call-start = ((), (), s32[]{:S(2)}) async-start(), calls=%async_computation.12 | async-start | bytes 1638400 | tf_op jit(solution)/shard_map/reduce_scatter | solution.py:148
  1134.1 12.1 slice-start.7
  1153.0 55.6 %reduce-scatter.8.cloned.1.call-start = ((), (), s32[]{:S(2)}) async-start(), calls=%async_computation.13 | async-start | bytes 1638400 | tf_op jit(solution)/shard_map/reduce_scatter | solution.py:148
  1156.3 14.9 %slice-start.10 = ((s8[10485760]{0:T(1024)(128)(4,1)}), s8[4194304]{0:T(1024)(128)(4,1)S(1)}, s32[]{:S(2)}) async-start(s8[10485760]{0:T(1024)(128)(4,1)} %bitcast.168), calls=%async_computation.24 | async-start | bytes 8388608
  1156.3 14.9 %slice-start.13 = ((s8[10485760]{0:T(1024)(128)(4,1)}), s8[4194304]{0:T(1024)(128)(4,1)S(1)}, s32[]{:S(2)}) async-start(s8[10485760]{0:T(1024)(128)(4,1)} %bitcast.170), calls=%async_computation.27 | async-start | bytes 8388608
  1156.3 23.2 %slice-start.16 = ((s8[5242880]{0:T(1024)(128)(4,1)}), s8[4194304]{0:T(1024)(128)(4,1)S(1)}, s32[]{:S(2)}) async-start(s8[5242880]{0:T(1024)(128)(4,1)} %bitcast.172), calls=%async_computation.30 | async-start | bytes 8388608
  1160.5 10.7 slice-start.11
  1160.6 10.7 slice-start.12
  1160.6 11.8 slice-start.14
  1160.6 12.4 %slice-start.15 = ((s8[10485760]{0:T(1024)(128)(4,1)}), s8[2097152]{0:T(1024)(128)(4,1)S(1)}, s32[]{:S(2)}) async-start(s8[10485760]{0:T(1024)(128)(4,1)} %bitcast.170), calls=%async_computation.29 | async-start | bytes 4194304
  1160.6 18.9 %slice-start.17 = ((s8[5242880]{0:T(1024)(128)(4,1)}), s8[1048576]{0:T(1024)(128)(4,1)S(1)}, s32[]{:S(2)}) async-start(s8[5242880]{0:T(1024)(128)(4,1)} %bitcast.172), calls=%async_computation.31 | async-start | bytes 2097152
  1179.5 30.2 %copy-start.24 = (bf16[80,32,128]{2,0,1:T(8,128)(2,1)S(1)}, bf16[80,32,128]{2,0,1:T(8,128)(2,1)}, u32[]{:S(2)}) copy-start(bf16[80,32,128]{2,0,1:T(8,128)(2,1)} %reduce-scatter.4.cloned.1.call-done) | copy-start | bytes 1966084
  (34 other events, 161.6 us)
Sparse Core Ops, SparseCore 0:
  939.7 35.9 reduce-scatter.3
  1153.1 25.6 reduce-scatter.5
  1182.8 25.7 reduce-scatter.7

commit v11 on v9

--- a/solution.py
+++ b/solution.py
@@ -96,7 +96,7 @@
 def shards(image, coil_maps, y_data, kz_lines):
     state_count, y_count = image.shape[0], image.shape[1]
     coil_count = coil_maps.shape[0]
-    group = 2 if coil_count % 2 == 0 else 1
+    group = 1
     y_cos, y_sin = cos_sin(y_count)
     y_fwd = jnp.concatenate([y_cos, -y_sin], axis=1)
     y_back = jnp.concatenate(

time: 1180 us -> 1230 us (1.042)
  waiting for transfers between devices: 412 us -> 488 us
  other arithmetic: 246 us -> 175 us
  starting transfers between devices: 42.3 us -> 79.8 us
    reduce_sum x4 -> x0, other arithmetic: 58.3 us -> none  [backward_y(): return jnp.sum(sens_real * coil_back - sens_imag * turned_back, axis=0)]
    all_to_all x4 -> x8, waiting for transfers between devices: 281 us -> 322 us  [to_ky_blocks(): lax.all_to_all(values, 'slab', split_axis=1, concat_axis=2, tiled=True)]
    all_to_all x4 -> x8, waiting for transfers between devices: 97.2 us -> 132 us  [to_z_slabs(): lax.all_to_all(values, 'slab', split_axis=2, concat_axis=1, tiled=True)]
    neg x20 -> x39, other arithmetic: 99.2 us -> 68.7 us  [turned(): return jnp.concatenate([-values[..., half:], values[..., :half]], axis=-1)]
    convert_element_type x2, other arithmetic: 9.87 us -> 38.5 us  [shards(): total.astype(BF16)]
    concatenate x4 -> x0, local copies, waits for them, and re-layouts: 22.4 us -> none  [turned(): return jnp.concatenate([-values[..., half:], values[..., :half]], axis=-1)]
    all_to_all x4 -> x8, starting transfers between devices: 20.1 us -> 40.4 us  [to_z_slabs(): lax.all_to_all(values, 'slab', split_axis=2, concat_axis=1, tiled=True)]
    unnamed x100 -> x196, local copies, waits for them, and re-layouts: 38.1 us -> 57.9 us
  transfers between devices with their start and end apart: 10 -> 18, of which waited for: 8 -> 14; matrix products, arithmetic and copies ran while one was open for 46% -> 40% of each run, Pallas kernels for 0% -> 0%
where the time goes in v11:
time: 1230 us; the launch traced here: 1220 us
  waiting for transfers between devices  488 us (40%)
  local copies, waits for them, and re-layouts  287 us (23%)
  other arithmetic  175 us (14%)
  matrix products  172 us (14%)
  starting transfers between devices  79.8 us (6%)
  between operations  15.1 us (1%)
    all_to_all x8, waiting for transfers between devices, to_ky_blocks(): lax.all_to_all(values, 'slab', split_axis=1, concat_axis=2, tiled=True)  322 us
    all_to_all x8, waiting for transfers between devices, to_z_slabs(): lax.all_to_all(values, 'slab', split_axis=2, concat_axis=1, tiled=True)  132 us
    all_to_all x24, local copies, waits for them, and re-layouts, to_z_slabs(): lax.all_to_all(values, 'slab', split_axis=2, concat_axis=1, tiled=True)  68.8 us
    neg x39, other arithmetic, turned(): return jnp.concatenate([-values[..., half:], values[..., :half]], axis=-1)  68.7 us
    all_to_all x16, local copies, waits for them, and re-layouts, to_ky_blocks(): lax.all_to_all(values, 'slab', split_axis=1, concat_axis=2, tiled=True)  66.2 us
    dot_general x8, matrix products, backward_y(): jnp.einsum('yk,ckzl->cyzl', y_back, with_turned(returned, 1), preferred_e...  63.4 us
    unnamed x196, local copies, waits for them, and re-layouts  57.9 us
    dot_general x8, matrix products, middle_z(): jnp.einsum('kjz,ckzl->ckjl', rows_fwd, with_turned(gathered, 2), preferre...  49.7 us
  transfers between devices with their start and end apart: 18, of which 14 were waited for; matrix products, arithmetic and copies ran while one was open for 40% of the time, Pallas kernels for 0%

profile of v11, /device:TPU:0, one launch (start us, length us, event | category | flops | bytes accessed | tf_op | source)
XLA Modules:
  0.0 1216.5 jit_solution(4050272550056663756)
XLA Ops:
  24.3 14.8 %fusion.284 = (bf16[1,320,32,64]{3,2,1,0:T(8,128)(2,1)}, bf16[1,320,32,64]{3,2,1,0:T(8,128)(2,1)}, bf16[1,320,32,64]{3,2,1,0:T(8,128)(2,1)}, bf16[1,320,32,64]{3...) fusion(bf16[4,320,32,128]{3,2,1,0:T(8,128)(2,1)} %param.5), kind=kLoop, calls=%fused_computation.447 | loop fusion | bytes 20971520 | tf_op jit(solution)/shard_map/slice | solution.py:32
  46.5 7.2 fusion.1
  61.2 7.7 all-to-all-start
  68.9 7.7 fusion.283
  89.8 38.6 %all-to-all-done = bf16[1,320,32,128]{3,2,0,1:T(8,128)(2,1)} async-done(((bf16[1,320,32,128]{3,2,0,1:T(8,128)(2,1)}), bf16[1,320,32,128]{3,2,0,1:T(8,128)(2,1)}, u32[]{:S(2)}, u32[]{:S(2)}) %all-to-all-start) | async-done | bytes 2621472 | tf_op jit(solution)/shard_map/all_to_all | solution.py:83
  140.5 6.4 fusion.228
  181.6 39.7 %all-to-all-done.1 = bf16[1,40,256,128]{3,1,0,2:T(8,128)(2,1)} async-done(((bf16[1,40,256,128]{3,1,0,2:T(8,128)(2,1)}), bf16[1,40,256,128]{3,1,0,2:T(8,128)(2,1)}, u32[]{:S(2)}, u32[]{:S(2)}) %all-to-all-start.1) | async-done | bytes 2621472 | tf_op jit(solution)/shard_map/all_to_all | solution.py:87
  245.2 39.7 %all-to-all-done.2 = bf16[1,320,32,128]{3,2,0,1:T(8,128)(2,1)} async-done(((bf16[1,320,32,128]{3,2,0,1:T(8,128)(2,1)}), bf16[1,320,32,128]{3,2,0,1:T(8,128)(2,1)}, u32[]{:S(2)}, u32[]{:S(2)}) %all-to-all-start.2) | async-done | bytes 2621472 | tf_op jit(solution)/shard_map/all_to_all | solution.py:83
  309.0 39.7 %all-to-all-done.4 = bf16[1,320,32,128]{3,2,0,1:T(8,128)(2,1)} async-done(((bf16[1,320,32,128]{3,2,0,1:T(8,128)(2,1)}), bf16[1,320,32,128]{3,2,0,1:T(8,128)(2,1)}, u32[]{:S(2)}, u32[]{:S(2)}) %all-to-all-start.4) | async-done | bytes 2621472 | tf_op jit(solution)/shard_map/all_to_all | solution.py:83
  353.3 7.3 pad_maximum_fusion.2
  372.9 39.3 %all-to-all-done.6 = bf16[1,320,32,128]{3,2,0,1:T(8,128)(2,1)} async-done(((bf16[1,320,32,128]{3,2,0,1:T(8,128)(2,1)}), bf16[1,320,32,128]{3,2,0,1:T(8,128)(2,1)}, u32[]{:S(2)}, u32[]{:S(2)}) %all-to-all-start.6) | async-done | bytes 2621472 | tf_op jit(solution)/shard_map/all_to_all | solution.py:83
  430.4 45.5 %all-to-all-done.8 = bf16[1,320,32,128]{3,2,0,1:T(8,128)(2,1)} async-done(((bf16[1,320,32,128]{3,2,0,1:T(8,128)(2,1)}), bf16[1,320,32,128]{3,2,0,1:T(8,128)(2,1)}, u32[]{:S(2)}, u32[]{:S(2)}) %all-to-all-start.8) | async-done | bytes 2621472 | tf_op jit(solution)/shard_map/all_to_all | solution.py:83
  494.1 45.5 %all-to-all-done.10 = bf16[1,320,32,128]{3,2,0,1:T(8,128)(2,1)} async-done(((bf16[1,320,32,128]{3,2,0,1:T(8,128)(2,1)}), bf16[1,320,32,128]{3,2,0,1:T(8,128)(2,1)}, u32[]{:S(2)}, u32[]{:S(2)}) %all-to-all-start.10) | async-done | bytes 2621472 | tf_op jit(solution)/shard_map/all_to_all | solution.py:83
  557.7 45.5 %all-to-all-done.12 = bf16[1,320,32,128]{3,2,0,1:T(8,128)(2,1)} async-done(((bf16[1,320,32,128]{3,2,0,1:T(8,128)(2,1)}), bf16[1,320,32,128]{3,2,0,1:T(8,128)(2,1)}, u32[]{:S(2)}, u32[]{:S(2)}) %all-to-all-start.12) | async-done | bytes 2621472 | tf_op jit(solution)/shard_map/all_to_all | solution.py:83
  621.3 6.4 fusion.226
  638.4 28.1 %all-to-all-done.14 = bf16[1,320,32,128]{3,2,0,1:T(8,128)(2,1)S(1)} async-done(((bf16[1,320,32,128]{3,2,0,1:T(8,128)(2,1)}), bf16[1,320,32,128]{3,2,0,1:T(8,128)(2,1)S(1)}, u32[]{:S(2)}, u32[]{:S(2)}) %all-to-all-start.14) | async-done | bytes 2621472 | tf_op jit(solution)/shard_map/all_to_all | solution.py:83
  694.3 35.9 %all-to-all-done.3 = bf16[1,40,256,128]{3,1,0,2:T(8,128)(2,1)} async-done(((bf16[1,40,256,128]{3,1,0,2:T(8,128)(2,1)}), bf16[1,40,256,128]{3,1,0,2:T(8,128)(2,1)}, u32[]{:S(2)}, u32[]{:S(2)}) %all-to-all-start.3) | async-done | bytes 2621472 | tf_op jit(solution)/shard_map/all_to_all | solution.py:87
  765.3 28.2 %all-to-all-done.5 = bf16[1,40,256,128]{3,1,0,2:T(8,128)(2,1)S(1)} async-done(((bf16[1,40,256,128]{3,1,0,2:T(8,128)(2,1)}), bf16[1,40,256,128]{3,1,0,2:T(8,128)(2,1)S(1)}, u32[]{:S(2)}, u32[]{:S(2)}) %all-to-all-start.5) | async-done | bytes 2621472 | tf_op jit(solution)/shard_map/all_to_all | solution.py:87
  831.0 6.3 fusion.220
  894.0 7.4 fusion.166
  926.1 7.8 fusion.165
  954.5 7.4 fusion.164
  961.9 9.4 fusion.163
  972.7 22.2 %fusion.234 = bf16[320,32,128]{2,0,1:T(8,128)(2,1)} fusion(f32[1,640,32,128]{3,1,2,0:T(8,128)} %fusion.163, bf16[1,320,32,128]{3,1,2,0:T(8,128)(2,1)S(1)} %copy-done.22, bf16[1,320,32,128]{3,1,2,0:T(8,128)(2,1)S(1)} %copy-done.18, f32[1,640,32,128]{3,1,2,0:T(8,128)} %fusion.164, bf16[1,320,32,128]{3,1,2,0:T(8,128)(2,1)S(1)} %copy-done.14, ...), kind=kLoop, calls=%fused_computation.355 | loop fusion | flops 39321600 | bytes 62914560 | tf_op jit(solution)/shard_map/convert_element_type | solution.py:135
  1027.3 6.4 fusion.214
  1044.4 25.6 %all-to-all-done.13 = bf16[1,40,256,128]{3,1,0,2:T(8,128)(2,1)} async-done(((bf16[1,40,256,128]{3,1,0,2:T(8,128)(2,1)}), bf16[1,40,256,128]{3,1,0,2:T(8,128)(2,1)}, u32[]{:S(2)}, u32[]{:S(2)}) %all-to-all-start.13) | async-done | bytes 2621472 | tf_op jit(solution)/shard_map/all_to_all | solution.py:87
  1108.4 7.4 fusion.162
  1115.8 7.4 fusion.161
  1123.2 7.4 fusion.160
  1146.1 9.2 fusion.159
  1156.6 16.3 %fusion.233 = bf16[320,32,128]{2,0,1:T(8,128)(2,1)} fusion(f32[1,640,32,128]{3,1,2,0:T(8,128)} %fusion.159, bf16[1,320,32,128]{3,1,2,0:T(8,128)(2,1)S(1)} %copy-done.23, bf16[1,320,32,128]{3,1,2,0:T(8,128)(2,1)S(1)} %copy-done.19, f32[1,640,32,128]{3,1,2,0:T(8,128)} %fusion.160, bf16[1,320,32,128]{3,1,2,0:T(8,128)(2,1)S(1)} %copy-done.15, ...), kind=kLoop, calls=%fused_computation.354 | loop fusion | flops 31457280 | bytes 65536000 | tf_op jit(solution)/shard_map/convert_element_type | solution.py:135
  1172.9 33.9 %reduce-scatter.5.cloned.1.call-done = bf16[80,32,128]{2,0,1:T(8,128)(2,1)} async-done(((bf16[320,32,128]{2,0,1:T(8,128)(2,1)}), bf16[80,32,128]{2,0,1:T(8,128)(2,1)}) %reduce-scatter.5.cloned.1.call-update) | async-done | bytes 655376 | tf_op jit(solution)/shard_map/reduce_scatter | solution.py:135
  (374 shorter events, 544.1 us)
Async XLA Ops:
  11.4 540.0 %copy-start.76 = (bf16[320,320]{1,0:T(8,128)(2,1)}, bf16[320,320]{1,0:T(8,128)(2,1)S(1)}, u32[]{:S(2)}) copy-start(bf16[320,320]{1,0:T(8,128)(2,1)S(1)} %get-tuple-element.155) | copy-start | bytes 614404
  43.1 10.7 copy-start.26
  61.2 67.3 %all-to-all-start = ((bf16[1,320,32,128]{3,2,0,1:T(8,128)(2,1)}), bf16[1,320,32,128]{3,2,0,1:T(8,128)(2,1)}, u32[]{:S(2)}, u32[]{:S(2)}) async-start(bf16[1,320,32,128]{3,2,0,1:T(8,128)(2,1)} %copy.257), calls=%async_computation | async-start | bytes 5242880 | tf_op jit(solution)/shard_map/all_to_all | solution.py:83
  81.8 58.7 %copy-start.88 = (pred[40,128]{1,0:T(8,128)(4,1)}, pred[40,128]{1,0:T(8,128)(4,1)S(1)}, u32[]{:S(2)}) copy-start(pred[40,128]{1,0:T(8,128)(4,1)S(1)} %get-tuple-element.141) | copy-start | bytes 15364
  157.7 63.6 %all-to-all-start.1 = ((bf16[1,40,256,128]{3,1,0,2:T(8,128)(2,1)}), bf16[1,40,256,128]{3,1,0,2:T(8,128)(2,1)}, u32[]{:S(2)}, u32[]{:S(2)}) async-start(bf16[1,40,256,128]{3,1,0,2:T(8,128)(2,1)} %copy.263), calls=%async_computation.1 | async-start | bytes 5242880 | tf_op jit(solution)/shard_map/all_to_all | solution.py:87
  221.3 63.6 %all-to-all-start.2 = ((bf16[1,320,32,128]{3,2,0,1:T(8,128)(2,1)}), bf16[1,320,32,128]{3,2,0,1:T(8,128)(2,1)}, u32[]{:S(2)}, u32[]{:S(2)}) async-start(bf16[1,320,32,128]{3,2,0,1:T(8,128)(2,1)} %copy.272), calls=%async_computation.2 | async-start | bytes 5242880 | tf_op jit(solution)/shard_map/all_to_all | solution.py:83
  284.9 63.8 %all-to-all-start.4 = ((bf16[1,320,32,128]{3,2,0,1:T(8,128)(2,1)}), bf16[1,320,32,128]{3,2,0,1:T(8,128)(2,1)}, u32[]{:S(2)}, u32[]{:S(2)}) async-start(bf16[1,320,32,128]{3,2,0,1:T(8,128)(2,1)} %copy.287), calls=%async_computation.4 | async-start | bytes 5242880 | tf_op jit(solution)/shard_map/all_to_all | solution.py:83
  348.7 63.6 %all-to-all-start.6 = ((bf16[1,320,32,128]{3,2,0,1:T(8,128)(2,1)}), bf16[1,320,32,128]{3,2,0,1:T(8,128)(2,1)}, u32[]{:S(2)}, u32[]{:S(2)}) async-start(bf16[1,320,32,128]{3,2,0,1:T(8,128)(2,1)} %copy.302), calls=%async_computation.6 | async-start | bytes 5242880 | tf_op jit(solution)/shard_map/all_to_all | solution.py:83
  412.3 63.6 %all-to-all-start.8 = ((bf16[1,320,32,128]{3,2,0,1:T(8,128)(2,1)}), bf16[1,320,32,128]{3,2,0,1:T(8,128)(2,1)}, u32[]{:S(2)}, u32[]{:S(2)}) async-start(bf16[1,320,32,128]{3,2,0,1:T(8,128)(2,1)} %copy.316), calls=%async_computation.9 | async-start | bytes 5242880 | tf_op jit(solution)/shard_map/all_to_all | solution.py:83
  475.9 63.8 %all-to-all-start.10 = ((bf16[1,320,32,128]{3,2,0,1:T(8,128)(2,1)}), bf16[1,320,32,128]{3,2,0,1:T(8,128)(2,1)}, u32[]{:S(2)}, u32[]{:S(2)}) async-start(bf16[1,320,32,128]{3,2,0,1:T(8,128)(2,1)} %copy.329), calls=%async_computation.11 | async-start | bytes 5242880 | tf_op jit(solution)/shard_map/all_to_all | solution.py:83
  539.7 63.6 %all-to-all-start.12 = ((bf16[1,320,32,128]{3,2,0,1:T(8,128)(2,1)}), bf16[1,320,32,128]{3,2,0,1:T(8,128)(2,1)}, u32[]{:S(2)}, u32[]{:S(2)}) async-start(bf16[1,320,32,128]{3,2,0,1:T(8,128)(2,1)} %copy.342), calls=%async_computation.13 | async-start | bytes 5242880 | tf_op jit(solution)/shard_map/all_to_all | solution.py:83
  603.2 63.3 %all-to-all-start.14 = ((bf16[1,320,32,128]{3,2,0,1:T(8,128)(2,1)}), bf16[1,320,32,128]{3,2,0,1:T(8,128)(2,1)S(1)}, u32[]{:S(2)}, u32[]{:S(2)}) async-start(bf16[1,320,32,128]{3,2,0,1:T(8,128)(2,1)} %copy.355), calls=%async_computation.15 | async-start | bytes 5242880 | tf_op jit(solution)/shard_map/all_to_all | solution.py:83
  666.5 63.6 %all-to-all-start.3 = ((bf16[1,40,256,128]{3,1,0,2:T(8,128)(2,1)}), bf16[1,40,256,128]{3,1,0,2:T(8,128)(2,1)}, u32[]{:S(2)}, u32[]{:S(2)}) async-start(bf16[1,40,256,128]{3,1,0,2:T(8,128)(2,1)} %copy.278), calls=%async_computation.3 | async-start | bytes 5242880 | tf_op jit(solution)/shard_map/all_to_all | solution.py:87
  730.1 63.3 %all-to-all-start.5 = ((bf16[1,40,256,128]{3,1,0,2:T(8,128)(2,1)}), bf16[1,40,256,128]{3,1,0,2:T(8,128)(2,1)S(1)}, u32[]{:S(2)}, u32[]{:S(2)}) async-start(bf16[1,40,256,128]{3,1,0,2:T(8,128)(2,1)} %copy.293), calls=%async_computation.5 | async-start | bytes 5242880 | tf_op jit(solution)/shard_map/all_to_all | solution.py:87
  793.4 66.7 %all-to-all-start.7 = ((bf16[1,40,256,128]{3,1,0,2:T(8,128)(2,1)}), bf16[1,40,256,128]{3,1,0,2:T(8,128)(2,1)}, u32[]{:S(2)}, u32[]{:S(2)}) async-start(bf16[1,40,256,128]{3,1,0,2:T(8,128)(2,1)} %copy.308), calls=%async_computation.7 | async-start | bytes 5242880 | tf_op jit(solution)/shard_map/all_to_all | solution.py:87
  860.1 73.8 %all-to-all-start.9 = ((bf16[1,40,256,128]{3,1,0,2:T(8,128)(2,1)}), bf16[1,40,256,128]{3,1,0,2:T(8,128)(2,1)}, u32[]{:S(2)}, u32[]{:S(2)}) async-start(bf16[1,40,256,128]{3,1,0,2:T(8,128)(2,1)} %copy.322), calls=%async_computation.10 | async-start | bytes 5242880 | tf_op jit(solution)/shard_map/all_to_all | solution.py:87
  933.9 72.6 %all-to-all-start.11 = ((bf16[1,40,256,128]{3,1,0,2:T(8,128)(2,1)}), bf16[1,40,256,128]{3,1,0,2:T(8,128)(2,1)}, u32[]{:S(2)}, u32[]{:S(2)}) async-start(bf16[1,40,256,128]{3,1,0,2:T(8,128)(2,1)} %copy.335), calls=%async_computation.12 | async-start | bytes 5242880 | tf_op jit(solution)/shard_map/all_to_all | solution.py:87
  939.9 99.7 %reduce-scatter.3.cloned.1.call-start = ((), (), s32[]{:S(2)}) async-start(), calls=%async_computation.18 | async-start | bytes 3276800 | tf_op jit(solution)/shard_map/reduce_scatter | solution.py:135
  961.9 9.4 copy-start.3
  961.9 9.4 copy-start.6
  961.9 9.4 copy-start.10
  961.9 9.4 copy-start.14
  961.9 9.4 copy-start.18
  961.9 9.4 copy-start.22
  961.9 10.7 copy-start.25
  1006.5 63.5 %all-to-all-start.13 = ((bf16[1,40,256,128]{3,1,0,2:T(8,128)(2,1)}), bf16[1,40,256,128]{3,1,0,2:T(8,128)(2,1)}, u32[]{:S(2)}, u32[]{:S(2)}) async-start(bf16[1,40,256,128]{3,1,0,2:T(8,128)(2,1)} %copy.348), calls=%async_computation.14 | async-start | bytes 5242880 | tf_op jit(solution)/shard_map/all_to_all | solution.py:87
  1070.0 63.3 %all-to-all-start.15 = ((bf16[1,40,256,128]{3,1,0,2:T(8,128)(2,1)}), bf16[1,40,256,128]{3,1,0,2:T(8,128)(2,1)}, u32[]{:S(2)}, u32[]{:S(2)}) async-start(bf16[1,40,256,128]{3,1,0,2:T(8,128)(2,1)} %copy.361), calls=%async_computation.16 | async-start | bytes 5242880 | tf_op jit(solution)/shard_map/all_to_all | solution.py:87
  1074.4 132.4 %reduce-scatter.5.cloned.1.call-start = ((), (), s32[]{:S(2)}) async-start(), calls=%async_computation.19 | async-start | bytes 3276800 | tf_op jit(solution)/shard_map/reduce_scatter | solution.py:135
  1146.0 9.2 copy-start.19
  1146.0 9.2 copy-start.23
  1146.1 10.5 copy-start.30
  1172.9 33.9 %copy-start.71 = (bf16[80,32,128]{2,0,1:T(8,128)(2,1)S(1)}, bf16[80,32,128]{2,0,1:T(8,128)(2,1)}, u32[]{:S(2)}) copy-start(bf16[80,32,128]{2,0,1:T(8,128)(2,1)} %reduce-scatter.3.cloned.1.call-done) | copy-start | bytes 1966084
  (76 other events, 291.7 us)
Sparse Core Ops, SparseCore 0:
  995.0 36.0 reduce-scatter.2
  1173.0 33.7 reduce-scatter.4

commit v12 on v9

--- a/solution.py
+++ b/solution.py
@@ -41,7 +41,10 @@
 
 
 def forward_y(pixels, sens_real, sens_imag, y_fwd):
-    coil_image = (sens_real * pixels + sens_imag * turned(pixels)).astype(BF16)
+    coil_image = (
+        sens_real.astype(F32) * pixels.astype(F32)
+        + sens_imag.astype(F32) * turned(pixels).astype(F32)
+    ).astype(BF16)
     return jnp.einsum(
         "ky,cyzl->ckzl", y_fwd, with_turned(coil_image, 1), preferred_element_type=F32
     ).astype(BF16)
@@ -116,9 +119,6 @@
                 pixels, chunk_real, chunk_imag, _ = lax.optimization_barrier(
                     (pixels, chunk_real, chunk_imag, spectrum)
                 )
-            pixels = pixels.astype(F32)
-            chunk_real = chunk_real.astype(F32)
-            chunk_imag = chunk_imag.astype(F32)
             spectrum = forward_y(pixels, chunk_real, chunk_imag, y_fwd)
             if first_gathered is not None and state == 0 and first == group:
                 spectrum = after(spectrum, first_gathered)

time: 1180 us -> 1180 us (level)
  waiting for transfers between devices: 412 us -> 442 us
  other arithmetic: 246 us -> 229 us
  local copies, waits for them, and re-layouts: 299 us -> 283 us
    concatenate x4 -> x0, local copies, waits for them, and re-layouts: 22.4 us -> none  [turned(): return jnp.concatenate([-values[..., half:], values[..., :half]], axis=-1)]
    all_to_all x4, waiting for transfers between devices: 97.2 us -> 117 us  [to_z_slabs(): lax.all_to_all(values, 'slab', split_axis=2, concat_axis=1, tiled=True)]
    concatenate x4 -> x0, other arithmetic: 15.5 us -> none  [turned(): return jnp.concatenate([-values[..., half:], values[..., :half]], axis=-1)]
    unnamed x100 -> x98, local copies, waits for them, and re-layouts: 38.1 us -> 35.5 us
    convert_element_type x7 -> x8, other arithmetic: 25.4 us -> 27.4 us  [the longest x4 22.3 us: forward_y(): coil_image = (sens_real.astype(F32) * pixels.astype(F32) + sens_imag.asty...]
  transfers between devices with their start and end apart: 10 -> 10, of which waited for: 8 -> 8; matrix products, arithmetic and copies ran while one was open for 46% -> 44% of each run, Pallas kernels for 0% -> 0%
where the time goes in v12:
time: 1180 us; the launch traced here: 1170 us
  waiting for transfers between devices  442 us (37%)
  local copies, waits for them, and re-layouts  283 us (24%)
  other arithmetic  229 us (19%)
  matrix products  161 us (14%)
  starting transfers between devices  42.7 us (4%)
  between operations  14.6 us (1%)
    all_to_all x4, waiting for transfers between devices, to_ky_blocks(): lax.all_to_all(values, 'slab', split_axis=1, concat_axis=2, tiled=True)  291 us
    all_to_all x4, waiting for transfers between devices, to_z_slabs(): lax.all_to_all(values, 'slab', split_axis=2, concat_axis=1, tiled=True)  117 us
    neg x20, other arithmetic, turned(): return jnp.concatenate([-values[..., half:], values[..., :half]], axis=-1)  94.9 us
    dot_general x4, matrix products, backward_y(): jnp.einsum('yk,ckzl->cyzl', y_back, with_turned(returned, 1), preferred_e...  68.1 us
    all_to_all x12, local copies, waits for them, and re-layouts, to_z_slabs(): lax.all_to_all(values, 'slab', split_axis=2, concat_axis=1, tiled=True)  64.7 us
    reduce_sum x4, other arithmetic, backward_y(): return jnp.sum(sens_real * coil_back - sens_imag * turned_back, axis=0)  58.5 us
    all_to_all x8, local copies, waits for them, and re-layouts, to_ky_blocks(): lax.all_to_all(values, 'slab', split_axis=1, concat_axis=2, tiled=True)  58 us
    convert_element_type x3, local copies, waits for them, and re-layouts, middle_z(): return jnp.einsum('kjz,ckjl->ckzl', rows_back, with_turned(residual, 2),...  41.3 us
  transfers between devices with their start and end apart: 10, of which 8 were waited for; matrix products, arithmetic and copies ran while one was open for 44% of the time, Pallas kernels for 0%

profile of v12, /device:TPU:0, one launch (start us, length us, event | category | flops | bytes accessed | tf_op | source)
XLA Modules:
  0.0 1172.1 jit_solution(6169567559000797529)
XLA Ops:
  41.4 9.7 copy.151
  51.1 9.9 fusion.1
  61.0 10.0 slice_negate_fusion.3
  118.9 10.0 slice_negate_fusion.2
  128.8 10.4 convert_bitcast_fusion.5
  139.3 69.6 %all-to-all-done = bf16[2,320,32,128]{3,2,0,1:T(8,128)(2,1)} async-done(((bf16[2,320,32,128]{3,2,0,1:T(8,128)(2,1)}), bf16[2,320,32,128]{3,2,0,1:T(8,128)(2,1)}, u32[]{:S(2)}, u32[]{:S(2)}) %all-to-all-start) | async-done | bytes 5242912 | tf_op jit(solution)/shard_map/all_to_all | solution.py:86
  276.1 13.8 %copy.161 = bf16[2,40,256,128]{3,0,1,2:T(2,128)(2,1)} copy(bf16[2,40,256,128]{2,3,0,1:T(8,128)(2,1)} %convert_bitcast_fusion.6) | data formatting | bytes 10485760 | tf_op jit(solution)/shard_map/convert_element_type | solution.py:72
  289.9 51.3 %all-to-all-done.2 = bf16[2,320,32,128]{3,2,0,1:T(8,128)(2,1)} async-done(((bf16[2,320,32,128]{3,2,0,1:T(8,128)(2,1)}), bf16[2,320,32,128]{3,2,0,1:T(8,128)(2,1)}, u32[]{:S(2)}, u32[]{:S(2)}) %all-to-all-start.2) | async-done | bytes 5242912 | tf_op jit(solution)/shard_map/all_to_all | solution.py:86
  346.1 10.3 pad_maximum_fusion
  366.8 9.9 slice_negate_fusion.1
  376.7 10.4 convert_bitcast_fusion.3
  397.8 9.9 slice_negate_fusion
  422.1 38.9 %all-to-all-done.1 = bf16[2,40,256,128]{3,0,1,2:T(2,128)(2,1)} async-done(((bf16[2,40,256,128]{3,0,1,2:T(2,128)(2,1)}), bf16[2,40,256,128]{3,0,1,2:T(2,128)(2,1)}, u32[]{:S(2)}, u32[]{:S(2)}) %all-to-all-start.1) | async-done | bytes 5242912 | tf_op jit(solution)/shard_map/all_to_all | solution.py:90
  474.1 106.7 %all-to-all-done.6 = bf16[2,320,32,128]{3,2,0,1:T(8,128)(2,1)} async-done(((bf16[2,320,32,128]{3,2,0,1:T(8,128)(2,1)}), bf16[2,320,32,128]{3,2,0,1:T(8,128)(2,1)}, u32[]{:S(2)}, u32[]{:S(2)}) %all-to-all-start.6) | async-done | bytes 5242912 | tf_op jit(solution)/shard_map/all_to_all | solution.py:86
  623.5 13.8 %copy.179 = bf16[2,40,256,128]{3,0,1,2:T(2,128)(2,1)} copy(bf16[2,40,256,128]{2,3,0,1:T(8,128)(2,1)} %convert_bitcast_fusion.4) | data formatting | bytes 10485760 | tf_op jit(solution)/shard_map/convert_element_type | solution.py:72
  637.3 63.0 %all-to-all-done.4 = bf16[2,320,32,128]{3,2,0,1:T(8,128)(2,1)} async-done(((bf16[2,320,32,128]{3,2,0,1:T(8,128)(2,1)}), bf16[2,320,32,128]{3,2,0,1:T(8,128)(2,1)}, u32[]{:S(2)}, u32[]{:S(2)}) %all-to-all-start.4) | async-done | bytes 5242912 | tf_op jit(solution)/shard_map/all_to_all | solution.py:86
  722.8 8.7 copy.166
  767.1 13.8 %copy.195 = bf16[2,40,256,128]{3,0,1,2:T(2,128)(2,1)} copy(bf16[2,40,256,128]{2,3,0,1:T(8,128)(2,1)} %convert_bitcast_fusion.2) | data formatting | bytes 10485760 | tf_op jit(solution)/shard_map/convert_element_type | solution.py:72
  786.1 17.0 %fusion.97 = f32[2,640,32,128]{3,1,2,0:T(8,128)} fusion(bf16[2,320,32,64]{1,3,2,0:T(8,128)(2,1)} %get-tuple-element.40, bf16[2,320,32,64]{1,3,2,0:T(8,128)(2,1)S(1)} %get-tuple-element.39, bf16[2,320,32,128]{1,3,2,0:T(8,128)(2,1)} %copy.166, bf16[320,320]{1,0:T(8,128)(2,1)} %copy-done.27, bf16[320,320]{1,0:T(8,128)(2,1)} %copy-done.28, ...), kind=kOutput, calls=%fused_computation.107 | convolution fusion | flops 6745620480 | bytes 32071680 | tf_op jit(solution)/shard_map/yk,ckzl->cyzl/dot_general | solution.py:77
  803.1 16.9 %all-to-all-done.3 = bf16[2,40,256,128]{3,0,1,2:T(2,128)(2,1)} async-done(((bf16[2,40,256,128]{3,0,1,2:T(2,128)(2,1)}), bf16[2,40,256,128]{3,0,1,2:T(2,128)(2,1)}, u32[]{:S(2)}, u32[]{:S(2)}) %all-to-all-start.3) | async-done | bytes 5242912 | tf_op jit(solution)/shard_map/all_to_all | solution.py:90
  824.8 18.2 %fusion.3 = f32[320,32,128]{2,0,1:T(8,128)} fusion(f32[2,640,32,128]{3,1,2,0:T(8,128)} %fusion.97, bf16[2,320,32,64]{3,1,2,0:T(8,128)(2,1)} %copy-done.4, bf16[2,320,32,64]{3,1,2,0:T(8,128)(2,1)} %copy-done.3), kind=kLoop, calls=%fused_computation.19 | loop fusion | flops 30146560 | bytes 31457280 | tf_op jit(solution)/shard_map/reduce_sum | solution.py:82
  850.5 8.7 copy.184
  864.2 16.9 %fusion.94 = f32[2,640,32,128]{3,1,2,0:T(8,128)} fusion(bf16[2,320,32,64]{1,3,2,0:T(8,128)(2,1)} %get-tuple-element.38, bf16[2,320,32,64]{1,3,2,0:T(8,128)(2,1)S(1)} %get-tuple-element.37, bf16[2,320,32,128]{1,3,2,0:T(8,128)(2,1)} %copy.184, bf16[320,320]{1,0:T(8,128)(2,1)} %copy-done.27, bf16[320,320]{1,0:T(8,128)(2,1)} %copy-done.28, ...), kind=kOutput, calls=%fused_computation.106 | convolution fusion | flops 6745620480 | bytes 32071680 | tf_op jit(solution)/shard_map/yk,ckzl->cyzl/dot_general | solution.py:77
  881.2 13.3 %fusion.7 = f32[320,32,128]{2,0,1:T(8,128)S(1)} fusion(bf16[2,320,32,128]{3,1,2,0:T(8,128)(2,1)} %copy-done, bf16[2,320,32,128]{3,1,2,0:T(8,128)(2,1)} %copy-done.1, f32[2,640,32,128]{3,1,2,0:T(8,128)} %fusion.94), kind=kLoop, calls=%fused_computation.23 | loop fusion | flops 14417920 | bytes 36700160 | tf_op jit(solution)/shard_map/reduce_sum | solution.py:82
  938.3 13.7 %copy.211 = bf16[2,40,256,128]{3,0,1,2:T(2,128)(2,1)} copy(bf16[2,40,256,128]{2,3,0,1:T(8,128)(2,1)} %convert_bitcast_fusion) | data formatting | bytes 10485760 | tf_op jit(solution)/shard_map/optimization_barrier | solution.py:96
  965.4 8.9 copy.200
  979.4 17.0 %fusion.91 = f32[2,640,32,128]{3,1,2,0:T(8,128)} fusion(bf16[2,320,32,64]{1,3,2,0:T(8,128)(2,1)} %get-tuple-element.42, bf16[2,320,32,64]{1,3,2,0:T(8,128)(2,1)S(1)} %get-tuple-element.41, bf16[2,320,32,128]{1,3,2,0:T(8,128)(2,1)} %copy.200, bf16[320,320]{1,0:T(8,128)(2,1)} %copy-done.27, bf16[320,320]{1,0:T(8,128)(2,1)} %copy-done.28, ...), kind=kOutput, calls=%fused_computation.105 | convolution fusion | flops 6745620480 | bytes 32071680 | tf_op jit(solution)/shard_map/yk,ckzl->cyzl/dot_general | solution.py:77
  996.3 14.0 %fusion.11 = f32[320,32,128]{2,0,1:T(8,128)} fusion(bf16[2,320,32,128]{3,1,2,0:T(8,128)(2,1)} %copy-done.5, bf16[2,320,32,128]{3,1,2,0:T(8,128)(2,1)} %copy-done.6, f32[2,640,32,128]{3,1,2,0:T(8,128)} %fusion.91), kind=kLoop, calls=%fused_computation.27 | loop fusion | flops 14417920 | bytes 36700160 | tf_op jit(solution)/shard_map/reduce_sum | solution.py:82
  1010.3 61.5 %all-to-all-done.7 = bf16[2,40,256,128]{3,0,1,2:T(2,128)(2,1)} async-done(((bf16[2,40,256,128]{3,0,1,2:T(2,128)(2,1)}), bf16[2,40,256,128]{3,0,1,2:T(2,128)(2,1)}, u32[]{:S(2)}, u32[]{:S(2)}) %all-to-all-start.7) | async-done | bytes 5242912 | tf_op jit(solution)/shard_map/all_to_all | solution.py:90
  1093.1 17.1 %fusion.88 = f32[2,640,32,128]{3,1,2,0:T(8,128)} fusion(bf16[2,320,32,64]{1,3,2,0:T(8,128)(2,1)} %get-tuple-element.36, bf16[2,320,32,64]{1,3,2,0:T(8,128)(2,1)S(1)} %get-tuple-element.35, bf16[2,320,32,128]{1,3,2,0:T(8,128)(2,1)} %copy.216, bf16[320,320]{1,0:T(8,128)(2,1)} %copy-done.27, bf16[320,320]{1,0:T(8,128)(2,1)} %copy-done.28, ...), kind=kOutput, calls=%fused_computation.104 | convolution fusion | flops 6745620480 | bytes 32071680 | tf_op jit(solution)/shard_map/yk,ckzl->cyzl/dot_general | solution.py:77
  1110.2 13.1 %fusion.15 = f32[320,32,128]{2,0,1:T(8,128)S(1)} fusion(bf16[2,320,32,128]{3,1,2,0:T(8,128)(2,1)} %copy-done, bf16[2,320,32,128]{3,1,2,0:T(8,128)(2,1)} %copy-done.1, f32[2,640,32,128]{3,1,2,0:T(8,128)} %fusion.88), kind=kLoop, calls=%fused_computation.31 | loop fusion | flops 14417920 | bytes 36700160 | tf_op jit(solution)/shard_map/reduce_sum | solution.py:82
  1128.2 34.0 %reduce-scatter.5.cloned.1.call-done = bf16[80,32,128]{2,0,1:T(8,128)(2,1)} async-done(((bf16[320,32,128]{2,0,1:T(8,128)(2,1)}), bf16[80,32,128]{2,0,1:T(8,128)(2,1)}) %reduce-scatter.5.cloned.1.call-update) | async-done | bytes 655376 | tf_op jit(solution)/shard_map/reduce_scatter | solution.py:135
  (195 shorter events, 417.2 us)
Async XLA Ops:
  9.4 398.4 %copy-start.27 = (bf16[320,320]{1,0:T(8,128)(2,1)}, bf16[320,320]{1,0:T(8,128)(2,1)S(1)}, u32[]{:S(2)}) copy-start(bf16[320,320]{1,0:T(8,128)(2,1)S(1)} %get-tuple-element.91) | copy-start | bytes 614404
  11.4 396.4 %copy-start.28 = (bf16[320,320]{1,0:T(8,128)(2,1)}, bf16[320,320]{1,0:T(8,128)(2,1)S(1)}, u32[]{:S(2)}) copy-start(bf16[320,320]{1,0:T(8,128)(2,1)S(1)} %fusion.196) | copy-start | bytes 614404
  19.5 6.7 slice-start.4
  19.5 6.7 slice-start.5
  20.8 5.4 slice-start.6
  39.3 11.8 %copy-start.3 = (bf16[2,320,32,64]{3,1,2,0:T(8,128)(2,1)}, bf16[2,320,32,64]{3,1,2,0:T(8,128)(2,1)S(1)}, u32[]{:S(2)}) copy-start(bf16[2,320,32,64]{3,1,2,0:T(8,128)(2,1)S(1)} %copy.233) | copy-start | bytes 7864324
  39.3 11.8 %slice-start.7 = ((s8[5242880]{0:T(1024)(128)(4,1)}), s8[1048576]{0:T(1024)(128)(4,1)S(1)}, s32[]{:S(2)}) async-start(s8[5242880]{0:T(1024)(128)(4,1)} %bitcast.172), calls=%async_computation.19 | async-start | bytes 2097152
  41.3 9.8 copy-start.4
  41.3 9.8 slice-start.8
  85.4 123.5 %all-to-all-start = ((bf16[2,320,32,128]{3,2,0,1:T(8,128)(2,1)}), bf16[2,320,32,128]{3,2,0,1:T(8,128)(2,1)}, u32[]{:S(2)}, u32[]{:S(2)}) async-start(bf16[2,320,32,128]{3,2,0,1:T(8,128)(2,1)} %copy.154), calls=%async_computation | async-start | bytes 10485760 | tf_op jit(solution)/shard_map/all_to_all | solution.py:86
  108.5 6.3 copy-start
  108.5 6.3 copy-start.1
  208.9 6.6 copy-start.16
  221.2 120.0 %all-to-all-start.2 = ((bf16[2,320,32,128]{3,2,0,1:T(8,128)(2,1)}), bf16[2,320,32,128]{3,2,0,1:T(8,128)(2,1)}, u32[]{:S(2)}, u32[]{:S(2)}) async-start(bf16[2,320,32,128]{3,2,0,1:T(8,128)(2,1)} %copy.172), calls=%async_computation.2 | async-start | bytes 10485760 | tf_op jit(solution)/shard_map/all_to_all | solution.py:86
  254.9 5.3 copy-start.9
  341.2 119.7 %all-to-all-start.1 = ((bf16[2,40,256,128]{3,0,1,2:T(2,128)(2,1)}), bf16[2,40,256,128]{3,0,1,2:T(2,128)(2,1)}, u32[]{:S(2)}, u32[]{:S(2)}) async-start(bf16[2,40,256,128]{3,0,1,2:T(2,128)(2,1)} %copy.161), calls=%async_computation.1 | async-start | bytes 10485760 | tf_op jit(solution)/shard_map/all_to_all | solution.py:90
  346.1 10.3 copy-start.2
  356.4 6.3 copy-start.5
  356.4 6.3 copy-start.6
  461.0 119.7 %all-to-all-start.6 = ((bf16[2,320,32,128]{3,2,0,1:T(8,128)(2,1)}), bf16[2,320,32,128]{3,2,0,1:T(8,128)(2,1)}, u32[]{:S(2)}, u32[]{:S(2)}) async-start(bf16[2,320,32,128]{3,2,0,1:T(8,128)(2,1)} %copy.204), calls=%async_computation.7 | async-start | bytes 10485760 | tf_op jit(solution)/shard_map/all_to_all | solution.py:86
  474.1 111.3 %copy-start.13 = (bf16[1,2,40,128,128]{4,3,2,1,0:T(8,128)(2,1)S(1)}, bf16[1,2,40,128,128]{4,3,2,1,0:T(8,128)(2,1)}, u32[]{:S(2)}) copy-start(bf16[1,2,40,128,128]{4,3,2,1,0:T(8,128)(2,1)} %get-tuple-element.27) | copy-start | bytes 7864324
  580.7 119.6 %all-to-all-start.4 = ((bf16[2,320,32,128]{3,2,0,1:T(8,128)(2,1)}), bf16[2,320,32,128]{3,2,0,1:T(8,128)(2,1)}, u32[]{:S(2)}, u32[]{:S(2)}) async-start(bf16[2,320,32,128]{3,2,0,1:T(8,128)(2,1)} %copy.188), calls=%async_computation.5 | async-start | bytes 10485760 | tf_op jit(solution)/shard_map/all_to_all | solution.py:86
  602.4 5.3 copy-start.7
  637.3 67.9 %copy-start.12 = (bf16[1,2,40,128,128]{4,3,2,1,0:T(8,128)(2,1)S(1)}, bf16[1,2,40,128,128]{4,3,2,1,0:T(8,128)(2,1)}, u32[]{:S(2)}) copy-start(bf16[1,2,40,128,128]{4,3,2,1,0:T(8,128)(2,1)} %get-tuple-element.28) | copy-start | bytes 7864324
  700.3 119.8 %all-to-all-start.3 = ((bf16[2,40,256,128]{3,0,1,2:T(2,128)(2,1)}), bf16[2,40,256,128]{3,0,1,2:T(2,128)(2,1)}, u32[]{:S(2)}, u32[]{:S(2)}) async-start(bf16[2,40,256,128]{3,0,1,2:T(2,128)(2,1)} %copy.179), calls=%async_computation.3 | async-start | bytes 10485760 | tf_op jit(solution)/shard_map/all_to_all | solution.py:90
  746.0 5.3 copy-start.10
  820.1 132.0 %all-to-all-start.5 = ((bf16[2,40,256,128]{3,0,1,2:T(2,128)(2,1)}), bf16[2,40,256,128]{3,0,1,2:T(2,128)(2,1)}, u32[]{:S(2)}, u32[]{:S(2)}) async-start(bf16[2,40,256,128]{3,0,1,2:T(2,128)(2,1)} %copy.195), calls=%async_computation.6 | async-start | bytes 10485760 | tf_op jit(solution)/shard_map/all_to_all | solution.py:90
  824.8 113.6 %reduce-scatter.3.cloned.1.call-start = ((), (), s32[]{:S(2)}) async-start(), calls=%async_computation.10 | async-start | bytes 3276800 | tf_op jit(solution)/shard_map/reduce_scatter | solution.py:135
  916.7 5.7 copy-start.8
  952.1 119.7 %all-to-all-start.7 = ((bf16[2,40,256,128]{3,0,1,2:T(2,128)(2,1)}), bf16[2,40,256,128]{3,0,1,2:T(2,128)(2,1)}, u32[]{:S(2)}, u32[]{:S(2)}) async-start(bf16[2,40,256,128]{3,0,1,2:T(2,128)(2,1)} %copy.211), calls=%async_computation.8 | async-start | bytes 10485760 | tf_op jit(solution)/shard_map/all_to_all | solution.py:90
  957.9 204.3 %reduce-scatter.5.cloned.1.call-start = ((), (), s32[]{:S(2)}) async-start(), calls=%async_computation.11 | async-start | bytes 3276800 | tf_op jit(solution)/shard_map/reduce_scatter | solution.py:135
  1123.3 38.9 %copy-start.25 = (bf16[80,32,128]{2,0,1:T(8,128)(2,1)S(1)}, bf16[80,32,128]{2,0,1:T(8,128)(2,1)}, u32[]{:S(2)}) copy-start(bf16[80,32,128]{2,0,1:T(8,128)(2,1)} %reduce-scatter.3.cloned.1.call-done) | copy-start | bytes 1966084
  (23 other events, 72.0 us)
Sparse Core Ops, SparseCore 0:
  899.6 35.9 reduce-scatter.2
  1128.4 33.7 reduce-scatter.4
